TPU v7x, 32 devices: a whole 2x2x4 slice. The times are simulated.
32 devices in a mesh: groups: 2 (over x), blk: 8 (over z, y), inner: 2 (over core).
Axes of the slice: x: 2, y: 2, z: 4, core: 2. Of those that a mesh axis runs over, the one named last changes fastest.
Arguments:
- patch_rows: bfloat16 [24576, 1536], P(('groups', 'blk', 'inner')), parts along dimension 0, may hold values from -6 to 6
- owner_ids: int32 [24576, 1], P(('groups', 'blk', 'inner')), parts along dimension 0, may hold values from 0 to 7; in each aligned block of 768 rows (0 to 767, 768 to 1535, ...) at most 192 rows name the same one
- page_ids: int32 [24576], P(('groups', 'blk', 'inner')), parts along dimension 0, may hold values from 0 to 7
- proj_weight: bfloat16 [1536, 128], replicated, may hold values from -0.15625 to 0.15625
- proj_bias: float32 [128], replicated, may hold values from -1.8 to 1.8
- query_tokens: bfloat16 [128, 32, 128], P(('groups', 'blk')), parts along dimension 0, may hold values from -0.5 to 0.5
- query_counts: int32 [128], P(('groups', 'blk')), parts along dimension 0, may hold values from 1 to 32, as said below
Outputs:
- page_scores: float32 [256, 64], P(('groups', 'blk', 'inner')), parts along dimension 0
There are 2 independent parts, one for each index of `groups`. A program takes and returns all parts, laid end to end along the dimension named above; an argument that names none is the same for every part. Nothing has to cross between parts.
Inputs may be any that keep to these rules, and one draw needn't show every extreme that they name: `owner_ids`: among the rows of one device, at most 192 name the same owner, a bound that some block reaches of them. `query_counts`: the first query of each part has all 32 tokens live.
All inputs are finite; a program needn't handle non-finite values.
Results may differ from a plain program's by a relative error of at most 0.00031.
Values may be sent and summed in bfloat16 or wider, within the bound.
No kernel may reach another device: no remote copies, remote signals or barrier semaphores. Data moves between devices by JAX's collectives and lax.ppermute only.
A program may use at most 64 MiB of HBM per device.

v0:
```python
import math

import jax
import jax.numpy as jnp
from jax import lax
from jax.sharding import PartitionSpec as P

PAGES_DEV = 8


def embed(rows, weight, bias):
    proj = jnp.dot(rows, weight, preferred_element_type=jnp.float32) + bias[None, :]
    scale = lax.rsqrt(jnp.sum(proj * proj, axis=1, keepdims=True) + 1e-06)
    return (proj * scale).astype(jnp.bfloat16)


def page_maxsim(tokens, counts, embedded, slot_pages, token_slots, page_total):
    sims = jnp.einsum("re,se->rs", tokens, embedded, preferred_element_type=jnp.float32)
    best = jnp.stack(
        [
            jnp.max(jnp.where(slot_pages[None, :] == page, sims, jnp.float32(-2.0)), axis=1)
            for page in range(page_total)
        ],
        axis=0,
    )
    best = best.reshape(page_total, counts.shape[0], token_slots)
    live = (jnp.arange(token_slots, dtype=jnp.int32)[None, :] < counts[:, None]).astype(jnp.float32)
    return jnp.sum(best * live[None, :, :], axis=2)


def make_scorer(embedded, slot_pages, page_total, token_slots, width):

    def score_block(carry, pieces, start):
        tokens, counts = pieces
        count_q = tokens.shape[0]
        group = math.gcd(count_q, max(1, 512 // token_slots))
        token_blocks = tokens.reshape(count_q // group, group * token_slots, width)
        count_blocks = counts.reshape(count_q // group, group)

        def one_block(args):
            block_tokens, block_counts = args
            return page_maxsim(
                block_tokens, block_counts, embedded, slot_pages, token_slots, page_total
            )

        scored = lax.map(one_block, (token_blocks, count_blocks))
        scored = jnp.transpose(scored, (1, 0, 2)).reshape(page_total, count_q)
        return scored

    return score_block


def shards(patch_rows, owner_ids, page_ids, proj_weight, proj_bias, query_tokens, query_counts):
    owners = lax.axis_size("blk")
    rows = patch_rows.shape[0]
    capacity = 2 * rows // owners
    slot_count = owners * capacity
    target = owner_ids[:, 0]
    onehot = (target[:, None] == jnp.arange(owners, dtype=jnp.int32)[None, :]).astype(jnp.int32)
    before = jnp.sum((jnp.cumsum(onehot, axis=0) - onehot) * onehot, axis=1)
    slot_index = target * capacity + before
    outgoing_pages = jnp.full((slot_count,), -1, jnp.int32).at[slot_index].set(page_ids)
    local = embed(patch_rows, proj_weight, proj_bias)
    packed = jnp.zeros((slot_count, local.shape[1]), jnp.bfloat16).at[slot_index].set(local)
    embedded, slot_pages = (
        lax.all_to_all(packed, "blk", split_axis=0, concat_axis=0, tiled=True),
        lax.all_to_all(outgoing_pages, "blk", split_axis=0, concat_axis=0, tiled=True),
    )
    per_block = query_tokens.shape[0]
    token_slots = query_tokens.shape[1]
    width = query_tokens.shape[2]
    total_queries = per_block * owners
    initial = jnp.zeros((PAGES_DEV, total_queries), jnp.float32)
    scorer = make_scorer(embedded, slot_pages, PAGES_DEV, token_slots, width)
    return scorer(
        initial,
        (
            lax.all_gather(query_tokens, "blk", axis=0, tiled=True),
            lax.all_gather(query_counts, "blk", axis=0, tiled=True),
        ),
        jnp.int32(0),
    )


def solution(mesh):
    in_specs = (
        P(("groups", "blk", "inner"), None),
        P(("groups", "blk", "inner"), None),
        P(("groups", "blk", "inner")),
        P(),
        P(),
        P(("groups", "blk"), None, None),
        P(("groups", "blk")),
    )
    out_specs = P(("groups", "blk", "inner"), None)
    return jax.shard_map(shards, mesh=mesh, in_specs=in_specs, out_specs=out_specs, check_vma=False)
```

profile of v0, /device:TPU:0, one launch (start us, length us, event | category | flops | bytes accessed | tf_op | source)
XLA Modules:
  0.0 88.6 jit_solution(12246551596819438382)
XLA Ops:
  0.0 0.8 reduce
  0.9 1.7 %reduce-window.6 = s32[8,6,128]{2,0,1:T(8,128)S(1)} reduce-window(s32[8,6,128]{2,0,1:T(8,128)S(1)} %fusion.10, s32[]{:T(128)} %copy.41), window={size=1x1x128 pad=0_0x0_0x127_0}, to_apply=%region_0.0 | reduce-window | flops 780288 | bytes 49156 | tf_op jit(solution)/shard_map/reduce-window
  2.7 0.1 copy.20
  2.8 0.2 reduce-window.9
  3.0 0.1 copy.21
  3.0 0.1 fusion.9
  3.1 0.7 fusion.13
  3.8 3.5 %scatter_custom_fusion = s32[1536]{0:T(1024)S(1)} fusion(s32[768]{0:T(1024)S(1)} %fusion.13, s32[768]{0:T(1024)} %param.11, s32[]{:T(128)} %constant.17.clone.1), kind=kCustom, calls=%fused_computation.49 | custom fusion | bytes 6656 | tf_op jit(solution)/shard_map/scatter | solution.py:62
  7.4 0.7 all_to_all.22
  8.1 7.3 %all-to-all-start = ((s32[8,192,1]{1,2,0:T(1,128)}), s32[8,192,1]{1,2,0:T(1,128)S(1)}, u32[]{:S(2)}, u32[]{:S(2)}) async-start(s32[8,192,1]{1,2,0:T(1,128)} %all_to_all.22), calls=%async_computation | async-start | bytes 16384 | tf_op jit(solution)/shard_map/all_to_all | solution.py:67
  15.4 1.9 %multiply_reduce_fusion.1 = (f32[768]{0:T(1024)S(1)}, f32[768,128]{0,1:T(8,128)S(1)}) fusion(f32[128]{0:T(128)} %param.13, bf16[768,1536]{1,0:T(8,128)(2,1)S(1)} %copy-done, bf16[1536,128]{1,0:T(8,128)(2,1)} %param.12), kind=kOutput, calls=%fused_computation.38 | convolution fusion | flops 302284032 | bytes 3149312 | tf_op jit(solution)/shard_map/dot_general | solution.py:12
  17.4 0.2 copy.23
  17.6 5.0 %scatter_custom_fusion.1 = bf16[1536,128]{1,0:T(8,128)(2,1)} fusion(s32[768]{0:T(1024)S(1)} %fusion.13, bf16[768,128]{1,0:T(8,128)(2,1)S(1)} %copy.23, bf16[]{:T(256)} %constant.13.clone.1), kind=kCustom, calls=%fused_computation.39 | custom fusion | bytes 393218 | tf_op jit(solution)/shard_map/scatter | solution.py:64
  22.6 6.0 %all-to-all-start.1 = ((bf16[8,192,128]{2,1,0:T(8,128)(2,1)}), bf16[8,192,128]{2,1,0:T(8,128)(2,1)S(1)}, u32[]{:S(2)}, u32[]{:S(2)}) async-start(bf16[8,192,128]{2,1,0:T(8,128)(2,1)} %bitcast.7), calls=%async_computation.1 | async-start | bytes 786432 | tf_op jit(solution)/shard_map/all_to_all | solution.py:66
  28.6 0.6 dynamic-slice
  29.9 0.2 dynamic-update-slice
  30.1 12.5 %all-reduce = s32[64]{0:T(128)S(1)} all-reduce(s32[64]{0:T(128)S(1)} %dynamic-update-slice), channel_id=1, replica_groups=mesh['groups'=2,'blk'=8,'inner'=2] {'blk'}, use_global_device_ids=true, to_apply=%add | all-reduce | flops 64 | bytes 512
  42.6 0.1 reshape.110
  42.7 31.5 %all_gather.6 = bf16[64,32,128]{2,1,0:T(8,128)(2,1)S(1)} all-gather(bf16[8,32,128]{2,1,0:T(8,128)(2,1)S(1)} %copy-done.1), channel_id=1, replica_groups=mesh['groups'=2,'blk'=8,'inner'=2] {'blk'}, dimensions={0}, use_global_device_ids=true | all-gather | bytes 589824 | tf_op jit(solution)/shard_map/all_gather | solution.py:78
  74.3 13.6 %while.10 = (s32[]{:T(128)}, f32[4,8,16]{2,1,0:T(8,128)S(1)}, s32[1536]{0:T(1024)S(1)}, bf16[4,512,128]{2,1,0:T(8,128)(2,1)S(1)}, bf16[1536,128]{1,0:T(8,128)(2,1)S(1)}, /*index=5*/s32[4,16]{1,0:T(4,128)S(1)}, s32[]{:T(128)}) while((s32[]{:T(128)}, f32[4,8,16]{2,1,0:T(8,128)S(1)}, s32[1536]{0:T(1024)S(1)}, ...), condition=%wide.region_16.17_spmd, body=%wide.region_6.16_spmd.sunk | while | flops 213926784 | bytes 762649 | solution.py:46
  74.3 2.5 %select_reduce_fusion.9 = (f32[512]{0:T(512)S(1)}, f32[512]{0:T(512)S(1)}, f32[512]{0:T(512)S(1)}, f32[512]{0:T(512)S(1)}, f32[512]{0:T(512)S(1)}, /*index=5*/f32[512]{0:T(512)S(1)}, f32[512]{0:T(512)S(1)}, f32[512]{0:T(512)S(1)}) fusion(pred[1536]{0:T(1024)(128)(4,1)S(1)} %get-tuple-element.121, pred[1536]{0:T(1024)(128)(4,1)S(1)} %get-tuple-element.122, ...), kind=kOutput, calls=%fused_computation.2.clone.1 | convolution fusion | flops 213905408 | bytes 557060 | tf_op jit(solution)/shard_map/while/body/eval_jaxpr/re,se->rs/dot_general | solution.py:18
  76.8 0.1 stack.35
  77.5 0.1 multiply_reduce_fusion.3
  77.7 2.5 %select_reduce_fusion.9 = (f32[512]{0:T(512)S(1)}, f32[512]{0:T(512)S(1)}, f32[512]{0:T(512)S(1)}, f32[512]{0:T(512)S(1)}, f32[512]{0:T(512)S(1)}, /*index=5*/f32[512]{0:T(512)S(1)}, f32[512]{0:T(512)S(1)}, f32[512]{0:T(512)S(1)}) fusion(pred[1536]{0:T(1024)(128)(4,1)S(1)} %get-tuple-element.121, pred[1536]{0:T(1024)(128)(4,1)S(1)} %get-tuple-element.122, ...), kind=kOutput, calls=%fused_computation.2.clone.1 | convolution fusion | flops 213905408 | bytes 557060 | tf_op jit(solution)/shard_map/while/body/eval_jaxpr/re,se->rs/dot_general | solution.py:18
  80.2 0.1 stack.35
  80.9 0.1 multiply_reduce_fusion.3
  81.1 2.5 %select_reduce_fusion.9 = (f32[512]{0:T(512)S(1)}, f32[512]{0:T(512)S(1)}, f32[512]{0:T(512)S(1)}, f32[512]{0:T(512)S(1)}, f32[512]{0:T(512)S(1)}, /*index=5*/f32[512]{0:T(512)S(1)}, f32[512]{0:T(512)S(1)}, f32[512]{0:T(512)S(1)}) fusion(pred[1536]{0:T(1024)(128)(4,1)S(1)} %get-tuple-element.121, pred[1536]{0:T(1024)(128)(4,1)S(1)} %get-tuple-element.122, ...), kind=kOutput, calls=%fused_computation.2.clone.1 | convolution fusion | flops 213905408 | bytes 557060 | tf_op jit(solution)/shard_map/while/body/eval_jaxpr/re,se->rs/dot_general | solution.py:18
  83.6 0.1 stack.35
  84.3 0.1 multiply_reduce_fusion.3
  84.5 2.5 %select_reduce_fusion.9 = (f32[512]{0:T(512)S(1)}, f32[512]{0:T(512)S(1)}, f32[512]{0:T(512)S(1)}, f32[512]{0:T(512)S(1)}, f32[512]{0:T(512)S(1)}, /*index=5*/f32[512]{0:T(512)S(1)}, f32[512]{0:T(512)S(1)}, f32[512]{0:T(512)S(1)}) fusion(pred[1536]{0:T(1024)(128)(4,1)S(1)} %get-tuple-element.121, pred[1536]{0:T(1024)(128)(4,1)S(1)} %get-tuple-element.122, ...), kind=kOutput, calls=%fused_computation.2.clone.1 | convolution fusion | flops 213905408 | bytes 557060 | tf_op jit(solution)/shard_map/while/body/eval_jaxpr/re,se->rs/dot_general | solution.py:18
  87.7 0.1 multiply_reduce_fusion.3
  87.9 0.7 reshape.111
  (96 shorter events, 3.0 us)
Async XLA Ops:
  0.0 15.4 %copy-start = (bf16[768,1536]{1,0:T(8,128)(2,1)S(1)}, bf16[768,1536]{1,0:T(8,128)(2,1)}, u32[]{:S(2)}) copy-start(bf16[768,1536]{1,0:T(8,128)(2,1)} %param.9) | copy-start | bytes 7077892
  8.1 14.5 %all-to-all-start = ((s32[8,192,1]{1,2,0:T(1,128)}), s32[8,192,1]{1,2,0:T(1,128)S(1)}, u32[]{:S(2)}, u32[]{:S(2)}) async-start(s32[8,192,1]{1,2,0:T(1,128)} %all_to_all.22), calls=%async_computation | async-start | bytes 16384 | tf_op jit(solution)/shard_map/all_to_all | solution.py:67
  15.4 13.2 %copy-start.3 = (u32[32]{0:T(128)S(1)}, u32[32]{0:T(128)}, u32[]{:S(2)}) copy-start(u32[32]{0:T(128)} %constant.55) | copy-start | bytes 388
  15.4 14.5 %copy-start.2 = (s32[8]{0:T(128)S(1)}, s32[8]{0:T(128)}, u32[]{:S(2)}) copy-start(s32[8]{0:T(128)} %param.15) | copy-start | bytes 100
  15.4 27.3 %copy-start.1 = (bf16[8,32,128]{2,1,0:T(8,128)(2,1)S(1)}, bf16[8,32,128]{2,1,0:T(8,128)(2,1)}, u32[]{:S(2)}) copy-start(bf16[8,32,128]{2,1,0:T(8,128)(2,1)} %param.14) | copy-start | bytes 196612
  22.6 51.7 %all-to-all-start.1 = ((bf16[8,192,128]{2,1,0:T(8,128)(2,1)}), bf16[8,192,128]{2,1,0:T(8,128)(2,1)S(1)}, u32[]{:S(2)}, u32[]{:S(2)}) async-start(bf16[8,192,128]{2,1,0:T(8,128)(2,1)} %bitcast.7), calls=%async_computation.1 | async-start | bytes 786432 | tf_op jit(solution)/shard_map/all_to_all | solution.py:66
where the time goes:
time: 88.9 us; the launch traced here: 88.6 us
  blocking collectives  44 us (49%)
  local copies, waits for them, and re-layouts  14.1 us (16%)
  starting transfers between devices  13.3 us (15%)
  matrix products  11.9 us (13%)
  other arithmetic  4.34 us (5%)
    all_gather x1, blocking collectives, shards(): lax.all_gather(query_tokens, 'blk', axis=0, tiled=True)  31.5 us
    unnamed x1, blocking collectives  12.5 us
    dot_general x4, matrix products, page_maxsim(): jnp.einsum('re,se->rs', tokens, embedded, preferred_element_type=jnp.floa...  9.97 us
    all_to_all x1, starting transfers between devices, shards(): lax.all_to_all(outgoing_pages, 'blk', split_axis=0, concat_axis=0, tiled=...  7.31 us
    all_to_all x1, starting transfers between devices, shards(): lax.all_to_all(packed, 'blk', split_axis=0, concat_axis=0, tiled=True)  5.99 us
    scatter x1, local copies, waits for them, and re-layouts, shards(): jnp.zeros((slot_count, local.shape[1]), jnp.bfloat16).at[slot_index]  4.98 us
    scatter x1, local copies, waits for them, and re-layouts, shards(): jnp.full((slot_count,), -1, jnp.int32).at[slot_index].set(page_ids)  3.54 us
    another operation x36, local copies, waits for them, and re-layouts, page_maxsim(): jnp.stack([jnp.max(jnp.where(slot_pages[None, :] == page, sims, jnp.float...  2.46 us
  transfers between devices with their start and end apart: 2, of which 0 were waited for; matrix products, arithmetic and copies ran while one was open for 9% of the time, Pallas kernels for 0%

commit v1 on v0

v1 whole, which is shorter than its diff:
```python
import functools
import math

import jax
import jax.numpy as jnp
from jax import lax
from jax.experimental import pallas as pl
from jax.experimental.pallas import tpu as pltpu
from jax.sharding import PartitionSpec as P

PAGES_DEV = 8


def embed(rows, weight, bias):
    proj = jnp.dot(rows, weight, preferred_element_type=jnp.float32) + bias[None, :]
    scale = lax.rsqrt(jnp.sum(proj * proj, axis=1, keepdims=True) + 1e-06)
    return (proj * scale).astype(jnp.bfloat16)


def page_order(embedded, slot_pages, page_total):
    slots = slot_pages.shape[0]
    lane = 128
    blocks = slots // lane
    onehot = slot_pages[:, None] == jnp.arange(page_total, dtype=jnp.int32)[None, :]
    tiles = onehot.astype(jnp.bfloat16).reshape(blocks, lane, page_total)
    earlier = (jnp.arange(lane)[None, :] < jnp.arange(lane)[:, None]).astype(jnp.bfloat16)
    within = jnp.einsum("ij,bjp->bip", earlier, tiles, preferred_element_type=jnp.float32)
    block_total = jnp.sum(tiles.astype(jnp.float32), axis=1)
    block_start = jnp.cumsum(block_total, axis=0) - block_total
    rank_all = (within + block_start[:, None, :]).reshape(slots, page_total)
    flags = onehot.astype(jnp.float32)
    rank = jnp.sum(rank_all * flags, axis=1).astype(jnp.int32)
    counts = jnp.sum(onehot.astype(jnp.int32), axis=0)
    groups = (counts + 7) // 8
    group_start = jnp.cumsum(groups) - groups
    row_start = jnp.sum(flags * (group_start * 8).astype(jnp.float32)[None, :], axis=1).astype(jnp.int32)
    position = jnp.where(slot_pages >= 0, row_start + rank, -1)
    ordered_rows = slots + 8 * page_total
    place = (position[:, None] == jnp.arange(ordered_rows, dtype=jnp.int32)[None, :]).astype(jnp.bfloat16)
    ordered = lax.dot_general(place, embedded, (((0,), (0,)), ((), ())), preferred_element_type=jnp.float32)
    table = jnp.concatenate([group_start, counts // 8, counts % 8]).astype(jnp.int32)
    return ordered.astype(jnp.bfloat16), table


def best_kernel(page_total, table_ref, rows_ref, tokens_ref, best_ref, sims_ref):
    sims_ref[...] = lax.dot_general(
        rows_ref[...], tokens_ref[...], (((1,), (1,)), ((), ())), preferred_element_type=jnp.float32
    )
    width = sims_ref.shape[1]
    sub = lax.broadcasted_iota(jnp.int32, (8, width), 0)
    for page in range(page_total):
        first = table_ref[page]
        full = table_ref[page_total + page]
        tail = table_ref[2 * page_total + page]

        def step(group, carry):
            start = pl.multiple_of((first + group) * 8, 8)
            return jnp.maximum(carry, sims_ref[pl.ds(start, 8), :])

        carry = lax.fori_loop(0, full, step, jnp.full((8, width), -2.0, jnp.float32))
        last = sims_ref[pl.ds(pl.multiple_of((first + full) * 8, 8), 8), :]
        carry = jnp.maximum(carry, jnp.where(sub < tail, last, jnp.float32(-2.0)))
        best_ref[page : page + 1, :] = jnp.max(carry, axis=0, keepdims=True)


def page_best(ordered, table, tokens, page_total):
    ordered_rows, width = ordered.shape
    token_total = tokens.shape[0]
    token_block = min(token_total, 1024)
    return pl.pallas_call(
        functools.partial(best_kernel, page_total),
        out_shape=jax.ShapeDtypeStruct((page_total, token_total), jnp.float32),
        grid_spec=pltpu.PrefetchScalarGridSpec(
            num_scalar_prefetch=1,
            grid=(token_total // token_block,),
            in_specs=[
                pl.BlockSpec((ordered_rows, width), lambda i, table: (0, 0)),
                pl.BlockSpec((token_block, width), lambda i, table: (i, 0)),
            ],
            out_specs=pl.BlockSpec((page_total, token_block), lambda i, table: (0, i)),
            scratch_shapes=[pltpu.VMEM((ordered_rows, token_block), jnp.float32)],
        ),
        cost_estimate=pl.CostEstimate(
            flops=2 * ordered_rows * token_total * width,
            bytes_accessed=2 * (ordered_rows + token_total) * width + 4 * page_total * token_total,
            transcendentals=0,
        ),
    )(table, ordered, tokens)


def dispatch(target, page_ids, local, owners, capacity):
    rows = target.shape[0]
    slot_count = owners * capacity
    onehot = (target[:, None] == jnp.arange(owners, dtype=jnp.int32)[None, :]).astype(jnp.bfloat16)
    earlier = (jnp.arange(rows)[None, :] < jnp.arange(rows)[:, None]).astype(jnp.bfloat16)
    seen = jnp.dot(earlier, onehot, preferred_element_type=jnp.float32)
    before = jnp.sum(seen * onehot.astype(jnp.float32), axis=1).astype(jnp.int32)
    slot_index = target * capacity + before
    placed = (slot_index[:, None] == jnp.arange(slot_count, dtype=jnp.int32)[None, :]).astype(jnp.bfloat16)
    packed = lax.dot_general(placed, local, (((0,), (0,)), ((), ())), preferred_element_type=jnp.float32)
    page_column = jnp.broadcast_to((page_ids + 1).astype(jnp.bfloat16)[:, None], (rows, 128))
    paged = lax.dot_general(placed, page_column, (((0,), (0,)), ((), ())), preferred_element_type=jnp.float32)
    slot_pages = paged[:, 0].astype(jnp.int32) - 1
    return packed.astype(jnp.bfloat16), slot_pages


def shards(patch_rows, owner_ids, page_ids, proj_weight, proj_bias, query_tokens, query_counts):
    owners = lax.axis_size("blk")
    halves = lax.axis_size("inner")
    rows = patch_rows.shape[0]
    capacity = 2 * rows // owners
    slot_count = owners * capacity
    local = embed(patch_rows, proj_weight, proj_bias)
    packed, outgoing_pages = dispatch(owner_ids[:, 0], page_ids, local, owners, capacity)
    per_block = query_tokens.shape[0]
    token_slots = query_tokens.shape[1]
    width = query_tokens.shape[2]
    total_queries = per_block * owners
    half_queries = per_block // halves
    query_rows = half_queries * token_slots
    page_rows = -(-capacity // width)
    count_rows = -(-per_block // width)
    used = query_rows + capacity + page_rows + count_rows
    message_rows = -(-used // 16) * 16
    own_half = lax.dynamic_slice_in_dim(query_tokens, lax.axis_index("inner") * half_queries, half_queries, axis=0)
    pages_part = jnp.pad(
        outgoing_pages.reshape(owners, capacity), ((0, 0), (0, page_rows * width - capacity)), constant_values=-1
    ).astype(jnp.bfloat16)
    counts_part = jnp.pad(query_counts, (0, count_rows * width - per_block)).astype(jnp.bfloat16)
    message = jnp.concatenate(
        [
            jnp.broadcast_to(own_half.reshape(1, query_rows, width), (owners, query_rows, width)),
            packed.reshape(owners, capacity, width),
            pages_part.reshape(owners, page_rows, width),
            jnp.broadcast_to(counts_part.reshape(1, count_rows, width), (owners, count_rows, width)),
            jnp.zeros((owners, message_rows - used, width), jnp.bfloat16),
        ],
        axis=1,
    )
    received = lax.all_to_all(message, "blk", split_axis=0, concat_axis=0, tiled=True)
    halves_in = lax.all_gather(received[:, :query_rows], "inner", axis=1, tiled=True)
    tokens = halves_in.reshape(total_queries, token_slots, width)
    embedded = received[:, query_rows : query_rows + capacity].reshape(slot_count, width)
    at = query_rows + capacity
    slot_pages = (
        received[:, at : at + page_rows].reshape(owners, page_rows * width)[:, :capacity].astype(jnp.int32)
    ).reshape(slot_count)
    at = at + page_rows
    counts = (
        received[:, at : at + count_rows].reshape(owners, count_rows * width)[:, :per_block].astype(jnp.int32)
    ).reshape(total_queries)
    ordered, table = page_order(embedded, slot_pages, PAGES_DEV)
    best = page_best(ordered, table, tokens.reshape(total_queries * token_slots, width), PAGES_DEV)
    live = (jnp.arange(token_slots, dtype=jnp.int32)[None, :] < counts[:, None]).astype(jnp.float32)
    return jnp.sum(best.reshape(PAGES_DEV, total_queries, token_slots) * live[None, :, :], axis=2)


def solution(mesh):
    in_specs = (
        P(("groups", "blk", "inner"), None),
        P(("groups", "blk", "inner"), None),
        P(("groups", "blk", "inner")),
        P(),
        P(),
        P(("groups", "blk"), None, None),
        P(("groups", "blk")),
    )
    out_specs = P(("groups", "blk", "inner"), None)
    return jax.shard_map(shards, mesh=mesh, in_specs=in_specs, out_specs=out_specs, check_vma=False)
```

time: 88.9 us -> 53.6 us (0.60)
  blocking collectives: 44 us -> 27.7 us
  starting transfers between devices: 13.3 us -> 0 us
  local copies, waits for them, and re-layouts: 14.1 us -> 6.3 us
  Pallas kernels: 0 us -> 5.31 us
  matrix products: 11.9 us -> 8.56 us
    all_gather x1, blocking collectives: 31.5 us -> 2.31 us  [shards(): lax.all_gather(received[:, :query_rows], 'inner', axis=1, tiled=True)]
    all_to_all x0 -> x1, blocking collectives: none -> 25.3 us  [shards(): lax.all_to_all(message, 'blk', split_axis=0, concat_axis=0, tiled=True)]
    all_to_all x2 -> x0, starting transfers between devices: 13.3 us -> none  [the longest x1 7.31 us: shards(): lax.all_to_all(outgoing_pages, 'blk', split_axis=0, concat_axis=0, tiled=...]
    unnamed x1 -> x0, blocking collectives: 12.5 us -> none
    scatter x2 -> x0, local copies, waits for them, and re-layouts: 8.52 us -> none  [the longest x1 4.98 us: shards(): jnp.zeros((slot_count, local.shape[1]), jnp.bfloat16).at[slot_index]]
    pallas_call x0 -> x1, Pallas kernels: none -> 5.31 us  [page_best(): pl.pallas_call(functools.partial(best_kernel, page_total), out_shape=jax....]
    dot_general x4 -> x5, matrix products: 9.97 us -> 6.99 us  [the longest x1 3.82 us: page_order(): lax.dot_general(place, embedded, (((0,), (0,)), ((), ())), preferred_elem...]
    another operation x37 -> x0, local copies, waits for them, and re-layouts: 2.54 us -> none  [the longest x36 2.46 us: page_maxsim(): jnp.stack([jnp.max(jnp.where(slot_pages[None, :] == page, sims, jnp.float...]
  transfers between devices with their start and end apart: 2 -> 0, of which waited for: 0 -> 0; matrix products, arithmetic and copies ran while one was open for 9% -> 0% of each run, Pallas kernels for 0% -> 0%
where the time goes in v1:
time: 53.6 us; the launch traced here: 52.9 us
  blocking collectives  27.7 us (52%)
  matrix products  8.56 us (16%)
  local copies, waits for them, and re-layouts  6.3 us (12%)
  Pallas kernels  5.31 us (10%)
  other arithmetic  4.9 us (9%)
    all_to_all x1, blocking collectives, shards(): lax.all_to_all(message, 'blk', split_axis=0, concat_axis=0, tiled=True)  25.3 us
    pallas_call x1, Pallas kernels, page_best(): pl.pallas_call(functools.partial(best_kernel, page_total), out_shape=jax....  5.31 us
    dot_general x1, matrix products, page_order(): lax.dot_general(place, embedded, (((0,), (0,)), ((), ())), preferred_elem...  3.82 us
    all_gather x1, blocking collectives, shards(): lax.all_gather(received[:, :query_rows], 'inner', axis=1, tiled=True)  2.31 us
    concatenate x1, local copies, waits for them, and re-layouts, shards(): jnp.concatenate([jnp.broadcast_to(own_half.reshape(1, query_rows, width),...  2.2 us
    dot_general x1, matrix products, dispatch(): lax.dot_general(placed, local, (((0,), (0,)), ((), ())), preferred_elemen...  1.74 us
    dot_general x1, matrix products, embed(): jnp.dot(rows, weight, preferred_element_type=jnp.float32) + bias[None, :]  1.57 us

profile of v1, /device:TPU:0, one launch (start us, length us, event | category | flops | bytes accessed | tf_op | source)
XLA Modules:
  0.0 52.9 jit_solution(7240711273941904494)
XLA Ops:
  0.0 0.0 copy-start
  0.0 0.8 %convert.11 = bf16[8]{0:T(256)(128)(2,1)S(1)} convert(s32[8]{0:T(128)} %param.13) | non-fusion elementwise | flops 8 | bytes 48 | tf_op jit(solution)/shard_map/convert.1
  0.8 0.7 %add_convert_fusion = bf16[768]{0:T(1024)(128)(2,1)S(1)} fusion(s32[768]{0:T(1024)} %param.9), kind=kLoop, calls=%fused_computation.46 | loop fusion | flops 1536 | bytes 4608 | tf_op jit(solution)/shard_map/convert_element_type | solution.py:101
  1.5 0.7 %reduce.1 = s32[768]{0:T(1024)S(1)} reduce(s32[768,1]{0,1:T(1,128)} %param.8, s32[]{:T(128)} %constant.57.clone.1), dimensions={1}, to_apply=%param.8.reduce_sub_computation | reduce | bytes 6148 | tf_op args[1]
  2.2 0.3 fusion.16
  2.6 0.7 %add_reduce_fusion = s32[768]{0:T(1024)S(1)} fusion(s32[768]{0:T(1024)S(1)} %convert_element_type.90, s32[768,1]{0,1:T(1,128)} %param.8), kind=kLoop, calls=%fused_computation.48 | loop fusion | flops 1536 | bytes 9216 | tf_op jit(solution)/shard_map/add | solution.py:98
  3.3 0.0 copy-start.3
  3.3 0.2 reshape.227
  3.5 0.9 %fusion.17 = bf16[1536]{0:T(1024)(128)(2,1)S(1)} fusion(bf16[768,1]{1,0:T(8,128)(2,1)S(1)} %reshape.227, s32[768]{0:T(1024)S(1)} %add_reduce_fusion), kind=kOutput, calls=%fused_computation.22 | convolution fusion | flops 3543552 | bytes 7680 | tf_op jit(solution)/shard_map/dot_general | solution.py:102
  4.4 0.1 sub.30
  4.5 1.6 %multiply_reduce_fusion = (f32[768]{0:T(1024)S(1)}, f32[768,128]{0,1:T(8,128)S(1)}) fusion(f32[128]{0:T(128)} %param.11, bf16[768,1536]{1,0:T(8,128)(2,1)S(1)} %copy-done, bf16[1536,128]{1,0:T(8,128)(2,1)S(1)} %copy-done.2), kind=kOutput, calls=%fused_computation.24 | convolution fusion | flops 302284032 | bytes 3149312 | tf_op jit(solution)/shard_map/dot_general | solution.py:15
  6.2 1.7 %convolution_convert_fusion = bf16[1536,128]{1,0:T(8,128)(2,1)} fusion(s32[768]{0:T(1024)S(1)} %add_reduce_fusion, f32[768,128]{0,1:T(8,128)S(1)} %get-tuple-element.10, f32[768]{0:T(1024)S(1)} %add_rsqrt_fusion), kind=kOutput, calls=%fused_computation.7 | convolution fusion | flops 304742400 | bytes 792576 | tf_op jit(solution)/shard_map/dot_general | solution.py:100
  8.0 2.2 %concatenate.6 = bf16[8,336,128]{2,1,0:T(8,128)(2,1)S(1)} concatenate(bf16[8,128,128]{2,1,0:T(8,128)(2,1)S(1)} %broadcast_in_dim.14, bf16[8,192,128]{2,1,0:T(8,128)(2,1)} %bitcast.42, bf16[8,2,128]{2,1,0:T(2,128)(2,1)S(1)} %reshape.216, bf16[8,1,128]{2,1,0:T(2,128)(2,1)S(1)} %broadcast_in_dim.16, bf16[8,13,128]{2,1,0:T(8,128)(2,1)S(1)} %broadcast_in_dim.17), dimensions={1} | concatenate | bytes 1376256 | tf_op jit(solution)/shard_map/concatenate | solution.py:130
  10.2 25.3 %all_to_all.5 = bf16[8,336,128]{2,1,0:T(8,128)(2,1)S(1)} all-to-all(bf16[8,336,128]{2,1,0:T(8,128)(2,1)S(1)} %concatenate.6), channel_id=1, replica_groups=mesh['groups'=2,'blk'=8,'inner'=2] {'blk'}, dimensions={0} | all-to-all | bytes 1376256 | tf_op jit(solution)/shard_map/all_to_all | solution.py:140
  35.5 0.9 %copy-done.1 = bf16[8,336,128]{2,1,0:T(8,128)(2,1)} copy-done((bf16[8,336,128]{2,1,0:T(8,128)(2,1)}, bf16[8,336,128]{2,1,0:T(8,128)(2,1)S(1)}, u32[]{:S(2)}) %copy-start.1) | copy-done | bytes 688152
  36.4 0.1 eq.79
  36.5 0.1 eq.83
  36.5 0.7 %slice.34 = bf16[8,1,128]{2,1,0:T(2,128)(2,1)S(1)} slice(bf16[8,336,128]{2,1,0:T(8,128)(2,1)} %copy-done.1), slice={[0:8], [322:323], [0:128]} | slice | bytes 4096 | tf_op jit(solution)/shard_map/slice | solution.py:150
  37.3 0.1 reshape.222
  37.4 0.1 convert_reduce_fusion.1
  37.5 0.2 reduce-window.7
  37.7 0.1 select_reduce_fusion
  37.8 0.1 convert_reduce_fusion
  37.9 0.2 fusion.14
  38.1 0.1 fusion.22
  38.2 1.0 %slice.33 = bf16[8,128,128]{2,1,0:T(8,128)(2,1)S(1)} slice(bf16[8,336,128]{2,1,0:T(8,128)(2,1)} %copy-done.1), slice={[0:8], [0:128], [0:128]} | slice | bytes 524288 | tf_op jit(solution)/shard_map/slice | solution.py:141
  39.2 2.3 %all_gather.3 = bf16[8,256,128]{2,1,0:T(8,128)(2,1)} all-gather(bf16[8,128,128]{2,1,0:T(8,128)(2,1)S(1)} %slice.33), channel_id=1, replica_groups=mesh['groups'=2,'blk'=8,'inner'=2] {'inner'}, dimensions={1}, use_global_device_ids=true | all-gather | bytes 786432 | tf_op jit(solution)/shard_map/all_gather | solution.py:141
  41.5 3.8 %fusion.4.rows_ref = bf16[1600,128]{1,0:T(8,128)(2,1)} fusion(bf16[1536,128]{1,0:T(8,128)(2,1)S(1)} %bitcast.40, s32[1536]{0:T(1024)S(1)} %fusion.26), kind=kOutput, calls=%fused_computation.6 | convolution fusion | flops 631808000 | bytes 808960 | tf_op jit(solution)/shard_map/dot_general | solution.py:40
  45.3 0.6 %pad_add_fusion.table_ref = s32[24]{0:T(128)} fusion(s32[8]{0:T(128)S(1)} %get-tuple-element.8, s32[8]{0:T(128)S(1)} %get-tuple-element.7, s32[8]{0:T(128)S(1)} %get-tuple-element.6), kind=kLoop, calls=%fused_computation.64 | loop fusion | flops 48 | bytes 192 | tf_op jit(solution)/shard_map/concatenate | solution.py:41
  45.9 5.3 %shard_map.73 = f32[8,2048]{1,0:T(8,128)} custom-call(s32[24]{0:T(128)} %pad_add_fusion.table_ref, bf16[1600,128]{1,0:T(8,128)(2,1)} %fusion.4.rows_ref, bf16[2048,128]{1,0:T(8,128)(2,1)} %bitcast.41), custom_call_target="tpu_custom_call" | custom-call | flops 838860800 | bytes 999424 | tf_op jit(solution)/shard_map/pallas_call | solution.py:70
  51.2 1.0 %reshape.220 = f32[8,64,32]{2,1,0:T(8,128)S(1)} reshape(f32[8,2048]{1,0:T(8,128)} %shard_map.73) | data formatting | bytes 131072 | tf_op jit(solution)/shard_map/reshape | solution.py:155
  52.2 0.7 %multiply_reduce_fusion.1 = f32[8,64]{1,0:T(8,128)} fusion(f32[8,64,32]{2,1,0:T(8,128)S(1)} %reshape.220, f32[64,32]{1,0:T(8,128)S(1)} %fusion.22), kind=kLoop, calls=%fused_computation.25 | loop fusion | flops 32256 | bytes 75776 | tf_op jit(solution)/shard_map/reduce_sum | solution.py:155
  (26 shorter events, 0.2 us)
Async XLA Ops:
  0.0 4.5 %copy-start = (bf16[768,1536]{1,0:T(8,128)(2,1)S(1)}, bf16[768,1536]{1,0:T(8,128)(2,1)}, u32[]{:S(2)}) copy-start(bf16[768,1536]{1,0:T(8,128)(2,1)} %param.7) | copy-start | bytes 7077892
  0.0 4.5 %copy-start.2 = (bf16[1536,128]{1,0:T(8,128)(2,1)S(1)}, bf16[1536,128]{1,0:T(8,128)(2,1)}, u32[]{:S(2)}) copy-start(bf16[1536,128]{1,0:T(8,128)(2,1)} %param.10) | copy-start | bytes 1179652
  3.3 2.8 %copy-start.3 = (bf16[8,32,128]{2,1,0:T(8,128)(2,1)S(1)}, bf16[8,32,128]{2,1,0:T(8,128)(2,1)}, u32[]{:S(2)}) copy-start(bf16[8,32,128]{2,1,0:T(8,128)(2,1)} %param.12) | copy-start | bytes 196612
  35.5 0.9 %copy-start.1 = (bf16[8,336,128]{2,1,0:T(8,128)(2,1)}, bf16[8,336,128]{2,1,0:T(8,128)(2,1)S(1)}, u32[]{:S(2)}) copy-start(bf16[8,336,128]{2,1,0:T(8,128)(2,1)S(1)} %all_to_all.5) | copy-start | bytes 2064388
  36.4 5.1 %slice-start = ((bf16[8,336,128]{2,1,0:T(8,128)(2,1)}), bf16[8,192,128]{2,1,0:T(8,128)(2,1)S(1)}, s32[]{:S(2)}) async-start(bf16[8,336,128]{2,1,0:T(8,128)(2,1)} %copy-done.1), calls=%async_computation.1 | async-start | bytes 786432 | tf_op jit(solution)/shard_map/slice | solution.py:143

commit v2 on v1

--- a/solution.py
+++ b/solution.py
@@ -17,7 +17,7 @@
     return (proj * scale).astype(jnp.bfloat16)
 
 
-def page_order(embedded, slot_pages, page_total):
+def page_positions(slot_pages, page_total, run):
     slots = slot_pages.shape[0]
     lane = 128
     blocks = slots // lane
@@ -31,61 +31,91 @@
     flags = onehot.astype(jnp.float32)
     rank = jnp.sum(rank_all * flags, axis=1).astype(jnp.int32)
     counts = jnp.sum(onehot.astype(jnp.int32), axis=0)
-    groups = (counts + 7) // 8
-    group_start = jnp.cumsum(groups) - groups
-    row_start = jnp.sum(flags * (group_start * 8).astype(jnp.float32)[None, :], axis=1).astype(jnp.int32)
+    padded = (counts + run - 1) // run * run
+    first = jnp.cumsum(padded) - padded
+    row_start = jnp.sum(flags * first.astype(jnp.float32)[None, :], axis=1).astype(jnp.int32)
     position = jnp.where(slot_pages >= 0, row_start + rank, -1)
-    ordered_rows = slots + 8 * page_total
-    place = (position[:, None] == jnp.arange(ordered_rows, dtype=jnp.int32)[None, :]).astype(jnp.bfloat16)
-    ordered = lax.dot_general(place, embedded, (((0,), (0,)), ((), ())), preferred_element_type=jnp.float32)
-    table = jnp.concatenate([group_start, counts // 8, counts % 8]).astype(jnp.int32)
-    return ordered.astype(jnp.bfloat16), table
+    table = jnp.concatenate([first, counts // run, counts % run]).astype(jnp.int32)
+    return position, table
 
 
-def best_kernel(page_total, table_ref, rows_ref, tokens_ref, best_ref, sims_ref):
-    sims_ref[...] = lax.dot_general(
-        rows_ref[...], tokens_ref[...], (((1,), (1,)), ((), ())), preferred_element_type=jnp.float32
+def score_kernel(page_total, token_slots, query_rows, token_block, table_ref, received_ref, tokens_ref, position_ref,
+                 counts_ref, out_ref, ordered_ref, sims_ref):
+    owners, chunk_rows = position_ref.shape
+    ordered_rows, width = ordered_ref.shape
+    total_queries = out_ref.shape[1]
+    target = lax.broadcasted_iota(jnp.int32, (ordered_rows, chunk_rows), 0)
+    ordered = jnp.zeros((ordered_rows, width), jnp.float32)
+    for chunk in range(owners):
+        place = (position_ref[chunk : chunk + 1, :] == target).astype(jnp.bfloat16)
+        rows = received_ref[chunk, query_rows : query_rows + chunk_rows, :]
+        ordered = ordered + jnp.dot(place, rows, preferred_element_type=jnp.float32)
+    ordered_ref[...] = ordered.astype(jnp.bfloat16)
+    sources = token_block // tokens_ref.shape[1]
+    sub = lax.broadcasted_iota(jnp.int32, (8, token_block), 0)
+    token_id = lax.broadcasted_iota(jnp.int32, (token_block, total_queries), 0)
+    query_id = lax.broadcasted_iota(jnp.int32, (token_block, total_queries), 1)
+
+    def block_scores(block, total):
+        tokens = tokens_ref[pl.ds(block * sources, sources)].reshape(token_block, width)
+        sims_ref[...] = lax.dot_general(
+            ordered_ref[...], tokens, (((1,), (1,)), ((), ())), preferred_element_type=jnp.float32
+        )
+        best_rows = []
+        for page in range(page_total):
+            first = table_ref[page]
+            whole = table_ref[page_total + page]
+            rest = table_ref[2 * page_total + page]
+
+            def step(i, carry):
+                start = pl.multiple_of(first + i * 16, 16)
+                return (
+                    jnp.maximum(carry[0], sims_ref[pl.ds(start, 8), :]),
+                    jnp.maximum(carry[1], sims_ref[pl.ds(start + 8, 8), :]),
+                )
+
+            floor = jnp.full((8, token_block), -2.0, jnp.float32)
+            low, high = lax.fori_loop(0, whole, step, (floor, floor))
+            start = pl.multiple_of(first + whole * 16, 16)
+            low = jnp.maximum(low, jnp.where(sub < rest, sims_ref[pl.ds(start, 8), :], jnp.float32(-2.0)))
+            high = jnp.maximum(high, jnp.where(sub + 8 < rest, sims_ref[pl.ds(start + 8, 8), :], jnp.float32(-2.0)))
+            best_rows.append(jnp.max(jnp.maximum(low, high), axis=0, keepdims=True))
+        best = jnp.concatenate(best_rows, axis=0)
+        token = token_id + block * token_block
+        live = ((token // token_slots) == query_id) & ((token % token_slots) < counts_ref[...])
+        return total + jnp.dot(
+            best, live.astype(jnp.float32), precision=lax.Precision.HIGHEST, preferred_element_type=jnp.float32
+        )
+
+    blocks = tokens_ref.shape[0] * tokens_ref.shape[1] // token_block
+    out_ref[...] = lax.fori_loop(
+        0, blocks, block_scores, jnp.zeros((page_total, total_queries), jnp.float32)
     )
-    width = sims_ref.shape[1]
-    sub = lax.broadcasted_iota(jnp.int32, (8, width), 0)
-    for page in range(page_total):
-        first = table_ref[page]
-        full = table_ref[page_total + page]
-        tail = table_ref[2 * page_total + page]
-
-        def step(group, carry):
-            start = pl.multiple_of((first + group) * 8, 8)
-            return jnp.maximum(carry, sims_ref[pl.ds(start, 8), :])
-
-        carry = lax.fori_loop(0, full, step, jnp.full((8, width), -2.0, jnp.float32))
-        last = sims_ref[pl.ds(pl.multiple_of((first + full) * 8, 8), 8), :]
-        carry = jnp.maximum(carry, jnp.where(sub < tail, last, jnp.float32(-2.0)))
-        best_ref[page : page + 1, :] = jnp.max(carry, axis=0, keepdims=True)
 
 
-def page_best(ordered, table, tokens, page_total):
-    ordered_rows, width = ordered.shape
-    token_total = tokens.shape[0]
+def page_scores(received, tokens, position, table, counts, page_total, token_slots, query_rows):
+    owners, chunk_rows = position.shape
+    width = received.shape[2]
+    ordered_rows = owners * chunk_rows + 16 * page_total + 16
+    token_total = tokens.shape[0] * tokens.shape[1]
+    total_queries = counts.shape[1]
     token_block = min(token_total, 1024)
+    vmem = pl.BlockSpec(memory_space=pltpu.VMEM)
     return pl.pallas_call(
-        functools.partial(best_kernel, page_total),
-        out_shape=jax.ShapeDtypeStruct((page_total, token_total), jnp.float32),
-        grid_spec=pltpu.PrefetchScalarGridSpec(
-            num_scalar_prefetch=1,
-            grid=(token_total // token_block,),
-            in_specs=[
-                pl.BlockSpec((ordered_rows, width), lambda i, table: (0, 0)),
-                pl.BlockSpec((token_block, width), lambda i, table: (i, 0)),
-            ],
-            out_specs=pl.BlockSpec((page_total, token_block), lambda i, table: (0, i)),
-            scratch_shapes=[pltpu.VMEM((ordered_rows, token_block), jnp.float32)],
-        ),
+        functools.partial(score_kernel, page_total, token_slots, query_rows, token_block),
+        out_shape=jax.ShapeDtypeStruct((page_total, total_queries), jnp.float32),
+        in_specs=[pl.BlockSpec(memory_space=pltpu.SMEM), vmem, vmem, vmem, vmem],
+        out_specs=vmem,
+        scratch_shapes=[
+            pltpu.VMEM((ordered_rows, width), jnp.bfloat16),
+            pltpu.VMEM((ordered_rows, token_block), jnp.float32),
+        ],
         cost_estimate=pl.CostEstimate(
-            flops=2 * ordered_rows * token_total * width,
-            bytes_accessed=2 * (ordered_rows + token_total) * width + 4 * page_total * token_total,
+            flops=2 * ordered_rows * width * (owners * chunk_rows + token_total),
+            bytes_accessed=2 * received.size + 2 * tokens.size + 4 * page_total * total_queries,
             transcendentals=0,
         ),
-    )(table, ordered, tokens)
+    )(table, received, tokens, position, counts)
 
 
 def dispatch(target, page_ids, local, owners, capacity):
@@ -139,8 +169,6 @@
     )
     received = lax.all_to_all(message, "blk", split_axis=0, concat_axis=0, tiled=True)
     halves_in = lax.all_gather(received[:, :query_rows], "inner", axis=1, tiled=True)
-    tokens = halves_in.reshape(total_queries, token_slots, width)
-    embedded = received[:, query_rows : query_rows + capacity].reshape(slot_count, width)
     at = query_rows + capacity
     slot_pages = (
         received[:, at : at + page_rows].reshape(owners, page_rows * width)[:, :capacity].astype(jnp.int32)
@@ -148,11 +176,11 @@
     at = at + page_rows
     counts = (
         received[:, at : at + count_rows].reshape(owners, count_rows * width)[:, :per_block].astype(jnp.int32)
-    ).reshape(total_queries)
-    ordered, table = page_order(embedded, slot_pages, PAGES_DEV)
-    best = page_best(ordered, table, tokens.reshape(total_queries * token_slots, width), PAGES_DEV)
-    live = (jnp.arange(token_slots, dtype=jnp.int32)[None, :] < counts[:, None]).astype(jnp.float32)
-    return jnp.sum(best.reshape(PAGES_DEV, total_queries, token_slots) * live[None, :, :], axis=2)
+    ).reshape(1, total_queries)
+    position, table = page_positions(slot_pages, PAGES_DEV, 16)
+    return page_scores(
+        received, halves_in, position.reshape(owners, capacity), table, counts, PAGES_DEV, token_slots, query_rows
+    )
 
 
 def solution(mesh):

time: 53.6 us -> 51 us (0.951)
  matrix products: 8.56 us -> 5.11 us
  other arithmetic: 4.9 us -> 1.84 us
  Pallas kernels: 5.31 us -> 8.13 us
  local copies, waits for them, and re-layouts: 6.3 us -> 7.65 us
    dot_general x2 -> x1, matrix products: 4 us -> 0.18 us  [page_positions(): jnp.einsum('ij,bjp->bip', earlier, tiles, preferred_element_type=jnp.floa...]
    pallas_call x1, Pallas kernels: 5.31 us -> 8.13 us  [page_scores(): pl.pallas_call(functools.partial(score_kernel, page_total, token_slots, q...]
    unnamed x11 -> x15, local copies, waits for them, and re-layouts: 0.88 us -> 2.55 us
    another operation x3, other arithmetic: 1.02 us -> 0.22 us
    reduce_sum x4 -> x3, other arithmetic: 1.04 us -> 0.3 us  [the longest x1 0.13 us: page_positions(): counts = jnp.sum(onehot.astype(jnp.int32), axis=0)]
    convert_element_type x1, other arithmetic: 0.72 us -> 0.01 us  [dispatch(): (page_ids + 1).astype(jnp.bfloat16)[:, None]]
    add x1, other arithmetic: 0.7 us -> 0.02 us  [dispatch(): slot_index = target * capacity + before]
    unnamed x1, other arithmetic: 0.7 us -> 0.02 us
where the time goes in v2:
time: 51 us; the launch traced here: 50.6 us
  blocking collectives  27.7 us (54%)
  Pallas kernels  8.13 us (16%)
  local copies, waits for them, and re-layouts  7.65 us (15%)
  matrix products  5.11 us (10%)
  other arithmetic  1.84 us (4%)
    all_to_all x1, blocking collectives, shards(): lax.all_to_all(message, 'blk', split_axis=0, concat_axis=0, tiled=True)  25.3 us
    pallas_call x1, Pallas kernels, page_scores(): pl.pallas_call(functools.partial(score_kernel, page_total, token_slots, q...  8.13 us
    unnamed x15, local copies, waits for them, and re-layouts  2.55 us
    all_gather x1, blocking collectives, shards(): lax.all_gather(received[:, :query_rows], 'inner', axis=1, tiled=True)  2.31 us
    concatenate x1, local copies, waits for them, and re-layouts, shards(): jnp.concatenate([jnp.broadcast_to(own_half.reshape(1, query_rows, width),...  2.2 us
    dot_general x1, matrix products, embed(): jnp.dot(rows, weight, preferred_element_type=jnp.float32) + bias[None, :]  1.95 us
    dot_general x1, matrix products, dispatch(): lax.dot_general(placed, local, (((0,), (0,)), ((), ())), preferred_elemen...  1.73 us

profile of v2, /device:TPU:0, one launch (start us, length us, event | category | flops | bytes accessed | tf_op | source)
XLA Modules:
  0.0 50.6 jit_solution(17910411801925297832)
XLA Ops:
  0.0 0.0 copy-start
  0.0 0.0 copy-start.3
  0.0 1.7 %copy-done = bf16[768,1536]{1,0:T(8,128)(2,1)S(1)} copy-done((bf16[768,1536]{1,0:T(8,128)(2,1)S(1)}, bf16[768,1536]{1,0:T(8,128)(2,1)}, u32[]{:S(2)}) %copy-start) | copy-done | bytes 2359320
  1.7 1.9 %multiply_reduce_fusion = (f32[768]{0:T(1024)S(1)}, f32[768,128]{0,1:T(8,128)S(1)}) fusion(f32[128]{0:T(128)} %param.11, bf16[768,1536]{1,0:T(8,128)(2,1)S(1)} %copy-done, bf16[1536,128]{1,0:T(8,128)(2,1)} %param.10), kind=kOutput, calls=%fused_computation.20 | convolution fusion | flops 302284032 | bytes 3149312 | tf_op jit(solution)/shard_map/dot_general | solution.py:15
  3.6 0.0 copy-done.3
  3.7 0.3 fusion.13
  4.0 0.0 copy-done.4
  4.1 0.2 reshape.196
  4.2 0.9 %fusion.14 = bf16[1536]{0:T(1024)(128)(2,1)S(1)} fusion(bf16[768,1]{1,0:T(8,128)(2,1)S(1)} %reshape.196, s32[768]{0:T(1024)S(1)} %add_reduce_fusion), kind=kOutput, calls=%fused_computation.18 | convolution fusion | flops 3543552 | bytes 7680 | tf_op jit(solution)/shard_map/dot_general | solution.py:132
  5.2 0.1 sub.39
  5.3 0.0 copy-done.5
  5.3 0.0 copy-done.2
  5.3 1.7 %convolution_convert_fusion = bf16[1536,128]{1,0:T(8,128)(2,1)} fusion(s32[768]{0:T(1024)S(1)} %add_reduce_fusion, f32[768,128]{0,1:T(8,128)S(1)} %get-tuple-element.10, f32[768]{0:T(1024)S(1)} %add_rsqrt_fusion), kind=kOutput, calls=%fused_computation.3 | convolution fusion | flops 304742400 | bytes 792576 | tf_op jit(solution)/shard_map/dot_general | solution.py:130
  7.1 2.2 %concatenate.6 = bf16[8,336,128]{2,1,0:T(8,128)(2,1)S(1)} concatenate(bf16[8,128,128]{2,1,0:T(8,128)(2,1)S(1)} %broadcast_in_dim.12, bf16[8,192,128]{2,1,0:T(8,128)(2,1)} %bitcast.35, bf16[8,2,128]{2,1,0:T(2,128)(2,1)S(1)} %reshape.184, bf16[8,1,128]{2,1,0:T(2,128)(2,1)S(1)} %broadcast_in_dim.14, bf16[8,13,128]{2,1,0:T(8,128)(2,1)S(1)} %broadcast_in_dim.15), dimensions={1} | concatenate | bytes 1376256 | tf_op jit(solution)/shard_map/concatenate | solution.py:160
  9.3 25.3 %all_to_all.5.received_ref = bf16[8,336,128]{2,1,0:T(8,128)(2,1)S(1)} all-to-all(bf16[8,336,128]{2,1,0:T(8,128)(2,1)S(1)} %concatenate.6), channel_id=1, replica_groups=mesh['groups'=2,'blk'=8,'inner'=2] {'blk'}, dimensions={0} | all-to-all | bytes 1376256 | tf_op jit(solution)/shard_map/all_to_all | solution.py:170
  34.7 0.9 %copy-done.1 = bf16[8,336,128]{2,1,0:T(8,128)(2,1)} copy-done((bf16[8,336,128]{2,1,0:T(8,128)(2,1)}, bf16[8,336,128]{2,1,0:T(8,128)(2,1)S(1)}, u32[]{:S(2)}) %copy-start.1) | copy-done | bytes 688152
  35.6 0.1 eq.66
  35.6 0.1 eq.70
  35.7 0.1 convert_reduce_fusion.1
  35.8 0.2 reduce-window.7
  36.0 0.1 select_reduce_fusion
  36.1 0.1 convert_element_type.86
  36.2 0.1 convert_reduce_fusion
  36.3 0.2 fusion.11
  36.5 0.1 convert_element_type.90
  36.6 1.0 %slice.28 = bf16[8,128,128]{2,1,0:T(8,128)(2,1)S(1)} slice(bf16[8,336,128]{2,1,0:T(8,128)(2,1)} %copy-done.1), slice={[0:8], [0:128], [0:128]} | slice | bytes 524288 | tf_op jit(solution)/shard_map/slice | solution.py:171
  37.6 2.3 %all_gather.3.tokens_ref = bf16[8,256,128]{2,1,0:T(8,128)(2,1)} all-gather(bf16[8,128,128]{2,1,0:T(8,128)(2,1)S(1)} %slice.28), channel_id=1, replica_groups=mesh['groups'=2,'blk'=8,'inner'=2] {'inner'}, dimensions={1}, use_global_device_ids=true | all-gather | bytes 786432 | tf_op jit(solution)/shard_map/all_gather | solution.py:171
  39.9 0.7 %slice.29 = bf16[8,1,128]{2,1,0:T(2,128)(2,1)S(1)} slice(bf16[8,336,128]{2,1,0:T(8,128)(2,1)} %copy-done.1), slice={[0:8], [322:323], [0:128]} | slice | bytes 4096 | tf_op jit(solution)/shard_map/slice | solution.py:178
  40.6 0.6 %reshape.191.counts_ref = s32[1,64]{1,0:T(1,128)} reshape(s32[8,8]{1,0:T(8,128)S(1)} %slice_convert_fusion.1) | data formatting | bytes 512 | tf_op jit(solution)/shard_map/reshape | solution.py:179
  41.2 0.6 %add_select_fusion.position_ref = s32[8,192]{1,0:T(8,128)} fusion(s32[8,192]{1,0:T(8,128)S(1)} %convert_element_type.86, s32[8,192]{1,0:T(8,128)S(1)} %convert_element_type.90, bf16[8,256]{1,0:T(8,128)(2,1)S(1)} %bitcast.38), kind=kLoop, calls=%fused_computation.34 | loop fusion | flops 6144 | bytes 21504 | tf_op jit(solution)/shard_map/jit(_where)/select_n | solution.py:37
  41.8 0.6 %pad_add_fusion.table_ref = s32[24]{0:T(128)} fusion(s32[8]{0:T(128)S(1)} %get-tuple-element.8, s32[8]{0:T(128)S(1)} %get-tuple-element.7, s32[8]{0:T(128)S(1)} %get-tuple-element.6), kind=kLoop, calls=%fused_computation.56 | loop fusion | flops 48 | bytes 192 | tf_op jit(solution)/shard_map/concatenate | solution.py:38
  42.4 8.1 %shard_map.73 = f32[8,64]{1,0:T(8,128)} custom-call(s32[24]{0:T(128)} %pad_add_fusion.table_ref, bf16[8,336,128]{2,1,0:T(8,128)(2,1)} %copy-done.1, bf16[8,256,128]{2,1,0:T(8,128)(2,1)} %all_gather.3.tokens_ref, s32[8,192]{1,0:T(8,128)} %add_select_fusion.position_ref, s32[1,64]{1,0:T(1,128)} %reshape.191.counts_ref), custom_call_target="tpu_custom_call" | custom-call | flops 1541406720 | bytes 1214464 | tf_op jit(solution)/shard_map/pallas_call | solution.py:104
  (28 shorter events, 0.3 us)
Async XLA Ops:
  0.0 1.7 %copy-start = (bf16[768,1536]{1,0:T(8,128)(2,1)S(1)}, bf16[768,1536]{1,0:T(8,128)(2,1)}, u32[]{:S(2)}) copy-start(bf16[768,1536]{1,0:T(8,128)(2,1)} %param.7) | copy-start | bytes 7077892
  0.0 3.6 %copy-start.3 = (s32[768,1]{0,1:T(1,128)S(1)}, s32[768,1]{0,1:T(1,128)}, u32[]{:S(2)}) copy-start(s32[768,1]{0,1:T(1,128)} %param.8) | copy-start | bytes 9220
  0.0 4.0 %copy-start.4 = (s32[768]{0:T(1024)S(1)}, s32[768]{0:T(1024)}, u32[]{:S(2)}) copy-start(s32[768]{0:T(1024)} %param.9) | copy-start | bytes 9220
  1.7 3.6 %copy-start.5 = (s32[8]{0:T(128)S(1)}, s32[8]{0:T(128)}, u32[]{:S(2)}) copy-start(s32[8]{0:T(128)} %param.13) | copy-start | bytes 100
  1.7 3.6 %copy-start.2 = (bf16[8,32,128]{2,1,0:T(8,128)(2,1)S(1)}, bf16[8,32,128]{2,1,0:T(8,128)(2,1)}, u32[]{:S(2)}) copy-start(bf16[8,32,128]{2,1,0:T(8,128)(2,1)} %param.12) | copy-start | bytes 196612
  34.7 0.9 %copy-start.1 = (bf16[8,336,128]{2,1,0:T(8,128)(2,1)}, bf16[8,336,128]{2,1,0:T(8,128)(2,1)S(1)}, u32[]{:S(2)}) copy-start(bf16[8,336,128]{2,1,0:T(8,128)(2,1)S(1)} %all_to_all.5.received_ref) | copy-start | bytes 2064388

commit v3 on v2

v3 whole, which is shorter than its diff:
```python
import functools
import math

import jax
import jax.numpy as jnp
from jax import lax
from jax.experimental import pallas as pl
from jax.experimental.pallas import tpu as pltpu
from jax.sharding import PartitionSpec as P

PAGES_DEV = 8


def embed(rows, weight, bias):
    proj = jnp.dot(rows, weight, preferred_element_type=jnp.float32) + bias[None, :]
    scale = lax.rsqrt(jnp.sum(proj * proj, axis=1, keepdims=True) + 1e-06)
    return (proj * scale).astype(jnp.bfloat16)


def send_kernel(page_total, capacity, query_rows, block_at, meta_ref, rows_ref, weight_ref, bias_ref, half_ref,
                message_ref):
    owners = message_ref.shape[0]
    rows = rows_ref.shape[0]
    proj = jnp.dot(rows_ref[...], weight_ref[...], preferred_element_type=jnp.float32) + bias_ref[...]
    scale = lax.rsqrt(jnp.sum(proj * proj, axis=1, keepdims=True) + 1e-06)
    local = (proj * scale).astype(jnp.bfloat16)
    combo = meta_ref[0:1, :] * page_total + meta_ref[1:2, :]
    combos = -(-owners * page_total // 128) * 128
    combo_id = lax.broadcasted_iota(jnp.int32, (combos, rows), 0)
    onehot = (combo == combo_id).astype(jnp.bfloat16)
    earlier = (
        lax.broadcasted_iota(jnp.int32, (rows, rows), 0) < lax.broadcasted_iota(jnp.int32, (rows, rows), 1)
    ).astype(jnp.bfloat16)
    seen = jnp.dot(onehot, earlier, preferred_element_type=jnp.float32)
    count = jnp.sum(onehot.astype(jnp.float32), axis=1, keepdims=True)
    row_id = lax.broadcasted_iota(jnp.int32, (combos, combos), 0)
    col_id = lax.broadcasted_iota(jnp.int32, (combos, combos), 1)
    same_owner_lower = (row_id // page_total == col_id // page_total) & (col_id % page_total < row_id % page_total)
    offset = jnp.dot(same_owner_lower.astype(jnp.bfloat16), count.astype(jnp.bfloat16),
                     preferred_element_type=jnp.float32)
    base = (lax.broadcasted_iota(jnp.int32, (combos, 1), 0) // page_total * capacity).astype(jnp.float32) + offset
    slot = jnp.sum(onehot.astype(jnp.float32) * (base + seen), axis=0, keepdims=True).astype(jnp.int32)
    count_rows = [
        lax.dot_general(
            jnp.ones((1, rows), jnp.bfloat16), onehot[group * 128 : (group + 1) * 128],
            (((1,), (1,)), ((), ())), preferred_element_type=jnp.float32,
        )
        for group in range(combos // 128)
    ]
    block_rows = message_ref.shape[1] - block_at
    block = jnp.concatenate(
        count_rows
        + [meta_ref[2:3, 0:128].astype(jnp.float32), jnp.zeros((block_rows - len(count_rows) - 1, 128), jnp.float32)],
        axis=0,
    ).astype(jnp.bfloat16)
    slot_id = lax.broadcasted_iota(jnp.int32, (capacity, rows), 0)
    for owner in range(owners):
        placed = (slot == slot_id + owner * capacity).astype(jnp.bfloat16)
        message_ref[owner, 0:query_rows, :] = half_ref[...]
        message_ref[owner, query_rows : query_rows + capacity, :] = jnp.dot(
            placed, local, preferred_element_type=jnp.float32
        ).astype(jnp.bfloat16)
        message_ref[owner, block_at:, :] = block


def send_message(patch_rows, owner_ids, page_ids, proj_weight, proj_bias, own_half, query_counts, owners, capacity):
    rows, features = patch_rows.shape
    query_rows, width = own_half.shape
    block_at = -(-(query_rows + capacity) // 16) * 16
    meta = jnp.concatenate(
        [owner_ids.reshape(1, rows), page_ids.reshape(1, rows), jnp.pad(query_counts, (0, rows - query_counts.shape[0])).reshape(1, rows)],
        axis=0,
    )
    vmem = pl.BlockSpec(memory_space=pltpu.VMEM)
    return pl.pallas_call(
        functools.partial(send_kernel, PAGES_DEV, capacity, query_rows, block_at),
        out_shape=jax.ShapeDtypeStruct((owners, block_at + 16, width), jnp.bfloat16),
        in_specs=[vmem] * 5,
        out_specs=vmem,
        cost_estimate=pl.CostEstimate(
            flops=2 * rows * width * (features + owners * capacity),
            bytes_accessed=2 * (rows * features + features * width + owners * (block_at + 16) * width),
            transcendentals=rows,
        ),
    )(meta, patch_rows, proj_weight, proj_bias.reshape(1, width), own_half)


def score_kernel(page_total, token_slots, query_rows, token_block, table_ref, received_ref, tokens_ref, counts_ref,
                 out_ref, ordered_ref, sims_ref):
    owners = received_ref.shape[0]
    ordered_rows, width = ordered_ref.shape
    capacity = (ordered_rows - 16 * page_total - 16) // owners
    total_queries = out_ref.shape[1]
    totals = [sum(table_ref[chunk * page_total + page] for chunk in range(owners)) for page in range(page_total)]
    firsts = []
    at = 0
    for page in range(page_total):
        firsts.append(at)
        at = at + (totals[page] + 15) // 16 * 16
    target = lax.broadcasted_iota(jnp.int32, (ordered_rows, capacity), 0)
    slot = lax.broadcasted_iota(jnp.int32, (1, capacity), 1)
    ordered = jnp.zeros((ordered_rows, width), jnp.float32)
    before = [0] * page_total
    for chunk in range(owners):
        position = jnp.full((1, capacity), -1, jnp.int32)
        low = 0
        for page in range(page_total):
            high = low + table_ref[chunk * page_total + page]
            inside = (slot >= low) & (slot < high)
            position = jnp.where(inside, slot + (firsts[page] + before[page] - low), position)
            before[page] = before[page] + (high - low)
            low = high
        place = (position == target).astype(jnp.bfloat16)
        rows = received_ref[chunk, query_rows : query_rows + capacity, :]
        ordered = ordered + jnp.dot(place, rows, preferred_element_type=jnp.float32)
    ordered_ref[...] = ordered.astype(jnp.bfloat16)
    sources = token_block // tokens_ref.shape[1]
    sub = lax.broadcasted_iota(jnp.int32, (8, token_block), 0)
    token_id = lax.broadcasted_iota(jnp.int32, (token_block, total_queries), 0)
    query_id = lax.broadcasted_iota(jnp.int32, (token_block, total_queries), 1)

    def block_scores(block, total):
        tokens = tokens_ref[pl.ds(block * sources, sources)].reshape(token_block, width)
        sims_ref[...] = lax.dot_general(
            ordered_ref[...], tokens, (((1,), (1,)), ((), ())), preferred_element_type=jnp.float32
        )
        best_rows = []
        for page in range(page_total):
            first = firsts[page]
            whole = totals[page] // 16
            rest = totals[page] % 16

            def step(i, carry):
                start = pl.multiple_of(first + i * 16, 16)
                return (
                    jnp.maximum(carry[0], sims_ref[pl.ds(start, 8), :]),
                    jnp.maximum(carry[1], sims_ref[pl.ds(start + 8, 8), :]),
                )

            floor = jnp.full((8, token_block), -2.0, jnp.float32)
            low, high = lax.fori_loop(0, whole, step, (floor, floor))
            start = pl.multiple_of(first + whole * 16, 16)
            low = jnp.maximum(low, jnp.where(sub < rest, sims_ref[pl.ds(start, 8), :], jnp.float32(-2.0)))
            high = jnp.maximum(high, jnp.where(sub + 8 < rest, sims_ref[pl.ds(start + 8, 8), :], jnp.float32(-2.0)))
            best_rows.append(jnp.max(jnp.maximum(low, high), axis=0, keepdims=True))
        best = jnp.concatenate(best_rows, axis=0)
        token = token_id + block * token_block
        live = ((token // token_slots) == query_id) & ((token % token_slots) < counts_ref[...])
        return total + jnp.dot(
            best, live.astype(jnp.float32), precision=lax.Precision.HIGHEST, preferred_element_type=jnp.float32
        )

    blocks = tokens_ref.shape[0] * tokens_ref.shape[1] // token_block
    out_ref[...] = lax.fori_loop(
        0, blocks, block_scores, jnp.zeros((page_total, total_queries), jnp.float32)
    )


def page_scores(received, tokens, table, counts, page_total, token_slots, query_rows, capacity):
    owners = received.shape[0]
    width = received.shape[2]
    ordered_rows = owners * capacity + 16 * page_total + 16
    token_total = tokens.shape[0] * tokens.shape[1]
    total_queries = counts.shape[1]
    token_block = min(token_total, 1024)
    vmem = pl.BlockSpec(memory_space=pltpu.VMEM)
    return pl.pallas_call(
        functools.partial(score_kernel, page_total, token_slots, query_rows, token_block),
        out_shape=jax.ShapeDtypeStruct((page_total, total_queries), jnp.float32),
        in_specs=[pl.BlockSpec(memory_space=pltpu.SMEM), vmem, vmem, vmem],
        out_specs=vmem,
        scratch_shapes=[
            pltpu.VMEM((ordered_rows, width), jnp.bfloat16),
            pltpu.VMEM((ordered_rows, token_block), jnp.float32),
        ],
        cost_estimate=pl.CostEstimate(
            flops=2 * ordered_rows * width * (owners * capacity + token_total),
            bytes_accessed=2 * received.size + 2 * tokens.size + 4 * page_total * total_queries,
            transcendentals=0,
        ),
    )(table, received, tokens, counts)


def shards(patch_rows, owner_ids, page_ids, proj_weight, proj_bias, query_tokens, query_counts):
    owners = lax.axis_size("blk")
    halves = lax.axis_size("inner")
    rows = patch_rows.shape[0]
    capacity = 2 * rows // owners
    per_block = query_tokens.shape[0]
    token_slots = query_tokens.shape[1]
    width = query_tokens.shape[2]
    total_queries = per_block * owners
    half_queries = per_block // halves
    query_rows = half_queries * token_slots
    own_half = lax.dynamic_slice_in_dim(query_tokens, lax.axis_index("inner") * half_queries, half_queries, axis=0)
    message = send_message(
        patch_rows, owner_ids, page_ids, proj_weight, proj_bias, own_half.reshape(query_rows, width), query_counts,
        owners, capacity,
    )
    received = lax.all_to_all(message, "blk", split_axis=0, concat_axis=0, tiled=True)
    halves_in = lax.all_gather(received[:, :query_rows], "inner", axis=1, tiled=True)
    block_at = -(-(query_rows + capacity) // 16) * 16
    combos = -(-owners * PAGES_DEV // 128) * 128
    count_rows = combos // 128
    page_counts = received[:, block_at : block_at + count_rows].reshape(owners, combos)
    page_counts = lax.dynamic_slice_in_dim(page_counts, lax.axis_index("blk") * PAGES_DEV, PAGES_DEV, axis=1)
    table = page_counts.astype(jnp.int32).reshape(owners * PAGES_DEV)
    counts = received[:, block_at + count_rows, :per_block].astype(jnp.int32).reshape(1, total_queries)
    return page_scores(received, halves_in, table, counts, PAGES_DEV, token_slots, query_rows, capacity)


def solution(mesh):
    in_specs = (
        P(("groups", "blk", "inner"), None),
        P(("groups", "blk", "inner"), None),
        P(("groups", "blk", "inner")),
        P(),
        P(),
        P(("groups", "blk"), None, None),
        P(("groups", "blk")),
    )
    out_specs = P(("groups", "blk", "inner"), None)
    return jax.shard_map(shards, mesh=mesh, in_specs=in_specs, out_specs=out_specs, check_vma=False)
```

time: 51 us -> 46.1 us (0.904)
  blocking collectives: 27.7 us -> 2.31 us
  waiting for transfers between devices: 0 us -> 18 us
  starting transfers between devices: 0 us -> 7.31 us
  Pallas kernels: 8.13 us -> 13.4 us
  matrix products: 5.11 us -> 0 us
  local copies, waits for them, and re-layouts: 7.65 us -> 3.29 us
    all_to_all x1 -> x0, blocking collectives: 25.3 us -> none  [shards(): lax.all_to_all(message, 'blk', split_axis=0, concat_axis=0, tiled=True)]
    all_to_all x0 -> x1, waiting for transfers between devices: none -> 18 us  [shards(): lax.all_to_all(message, 'blk', split_axis=0, concat_axis=0, tiled=True)]
    all_to_all x0 -> x1, starting transfers between devices: none -> 7.31 us  [shards(): lax.all_to_all(message, 'blk', split_axis=0, concat_axis=0, tiled=True)]
    pallas_call x0 -> x1, Pallas kernels: none -> 5.18 us  [send_message(): pl.pallas_call(functools.partial(send_kernel, PAGES_DEV, capacity, query_...]
    dot_general x5 -> x0, matrix products: 5.11 us -> none  [the longest x1 1.95 us: embed(): jnp.dot(rows, weight, preferred_element_type=jnp.float32) + bias[None, :]]
    unnamed x15 -> x4, local copies, waits for them, and re-layouts: 2.55 us -> 0.01 us
    concatenate x1 -> x0, local copies, waits for them, and re-layouts: 2.2 us -> none  [shards(): jnp.concatenate([jnp.broadcast_to(own_half.reshape(1, query_rows, width),...]
    convert_element_type x2, local copies, waits for them, and re-layouts: 0.14 us -> 1.26 us  [the longest x1 0.64 us: shards(): received[:, block_at + count_rows, :per_block].astype(jnp.int32)]
  transfers between devices with their start and end apart: 0 -> 1, of which waited for: 0 -> 1; matrix products, arithmetic and copies ran while one was open for 0% -> 0% of each run, Pallas kernels for 0% -> 0%
where the time goes in v3:
time: 46.1 us; the launch traced here: 45.8 us
  waiting for transfers between devices  18 us (39%)
  Pallas kernels  13.4 us (29%)
  starting transfers between devices  7.31 us (16%)
  local copies, waits for them, and re-layouts  3.29 us (7%)
  blocking collectives  2.31 us (5%)
  other arithmetic  1.39 us (3%)
    all_to_all x1, waiting for transfers between devices, shards(): lax.all_to_all(message, 'blk', split_axis=0, concat_axis=0, tiled=True)  18 us
    pallas_call x1, Pallas kernels, page_scores(): pl.pallas_call(functools.partial(score_kernel, page_total, token_slots, q...  8.26 us
    all_to_all x1, starting transfers between devices, shards(): lax.all_to_all(message, 'blk', split_axis=0, concat_axis=0, tiled=True)  7.31 us
    pallas_call x1, Pallas kernels, send_message(): pl.pallas_call(functools.partial(send_kernel, PAGES_DEV, capacity, query_...  5.18 us
    all_gather x1, blocking collectives, shards(): lax.all_gather(received[:, :query_rows], 'inner', axis=1, tiled=True)  2.31 us
    concatenate x1, other arithmetic, send_message(): jnp.concatenate([owner_ids.reshape(1, rows), page_ids.reshape(1, rows), j...  1.29 us
  transfers between devices with their start and end apart: 1, of which 1 were waited for; matrix products, arithmetic and copies ran while one was open for 0% of the time, Pallas kernels for 0%

profile of v3, /device:TPU:0, one launch (start us, length us, event | category | flops | bytes accessed | tf_op | source)
XLA Modules:
  0.0 45.8 jit_solution(11960453065351332580)
XLA Ops:
  0.0 0.0 copy-start
  0.0 0.7 %reshape.35 = s32[1,768]{1,0:T(1,128)S(1)} reshape(s32[768]{0:T(1024)} %param.9) | data formatting | bytes 6144 | tf_op jit(solution)/shard_map/reshape | solution.py:71
  0.7 0.7 %pad.4 = s32[768]{0:T(1024)S(1)} pad(s32[8]{0:T(128)} %param.13, s32[]{:T(128)} %constant.6.clone.1), padding=0_760 | pad | bytes 3108 | tf_op jit(solution)/shard_map/jit(_pad)/pad | solution.py:71
  1.4 0.0 copy-done
  1.4 0.6 %constant_dynamic-slice_fusion = bf16[4,32,128]{2,1,0:T(8,128)(2,1)} fusion(bf16[8,32,128]{2,1,0:T(8,128)(2,1)S(1)} %copy-done, s32[]{:T(128)S(6)} %select_n.6), kind=kLoop, calls=%fused_computation.4 | loop fusion | bytes 65540 | tf_op jit(solution)/shard_map/dynamic_slice | solution.py:195
  2.0 1.3 %pad_add_fusion.meta_ref = s32[3,768]{1,0:T(4,128)} fusion(s32[1,768]{1,0:T(1,128)S(1)} %reshape.36, s32[1,768]{1,0:T(1,128)S(1)} %reshape.35, s32[1,768]{1,0:T(1,128)} %bitcast.4), kind=kLoop, calls=%fused_computation | loop fusion | flops 4608 | bytes 18432 | tf_op jit(solution)/shard_map/concatenate | solution.py:70
  3.3 5.2 %shard_map.73 = bf16[8,336,128]{2,1,0:T(8,128)(2,1)} custom-call(s32[3,768]{1,0:T(4,128)} %pad_add_fusion.meta_ref, bf16[768,1536]{1,0:T(8,128)(2,1)} %rows_ref.1, bf16[1536,128]{1,0:T(8,128)(2,1)} %weight_ref.1, f32[1,128]{1,0:T(1,128)} %bitcast.5, bf16[128,128]{1,0:T(8,128)(2,1)} %bitcast.3), custom_call_target="tpu_custom_call" | custom-call | flops 603979776 | bytes 3440640 | tf_op jit(solution)/shard_map/pallas_call | solution.py:75
  8.5 7.3 %all-to-all-start = ((bf16[8,336,128]{2,1,0:T(8,128)(2,1)}), bf16[8,336,128]{2,1,0:T(8,128)(2,1)S(1)}, u32[]{:S(2)}, u32[]{:S(2)}) async-start(bf16[8,336,128]{2,1,0:T(8,128)(2,1)} %shard_map.73), calls=%async_computation | async-start | bytes 1376256 | tf_op jit(solution)/shard_map/all_to_all | solution.py:200
  15.8 18.0 %all-to-all-done.received_ref = bf16[8,336,128]{2,1,0:T(8,128)(2,1)S(1)} async-done(((bf16[8,336,128]{2,1,0:T(8,128)(2,1)}), bf16[8,336,128]{2,1,0:T(8,128)(2,1)S(1)}, u32[]{:S(2)}, u32[]{:S(2)}) %all-to-all-start) | async-done | bytes 688160 | tf_op jit(solution)/shard_map/all_to_all | solution.py:200
  33.8 0.0 copy-start.1
  33.8 0.1 fusion
  33.9 0.6 %reshape.40.counts_ref = s32[1,64]{1,0:T(1,128)} reshape(s32[8,8]{1,0:T(8,128)S(1)} %get-tuple-element.5) | data formatting | bytes 512 | tf_op jit(solution)/shard_map/convert_element_type | solution.py:208
  34.5 0.6 %reshape.39.table_ref = s32[64]{0:T(128)} reshape(s32[8,8]{1,0:T(8,128)S(1)} %get-tuple-element.6) | data formatting | bytes 512 | tf_op jit(solution)/shard_map/convert_element_type | solution.py:207
  35.2 2.3 %all_gather.3.tokens_ref = bf16[8,256,128]{2,1,0:T(8,128)(2,1)} all-gather(bf16[8,128,128]{2,1,0:T(8,128)(2,1)S(1)} %slice.13), channel_id=1, replica_groups=mesh['groups'=2,'blk'=8,'inner'=2] {'inner'}, dimensions={1}, use_global_device_ids=true | all-gather | bytes 786432 | tf_op jit(solution)/shard_map/all_gather | solution.py:201
  37.5 0.0 copy-done.1
  37.5 8.3 %shard_map.74 = f32[8,64]{1,0:T(8,128)} custom-call(s32[64]{0:T(128)} %reshape.39.table_ref, bf16[8,336,128]{2,1,0:T(8,128)(2,1)} %copy-done.1, bf16[8,256,128]{2,1,0:T(8,128)(2,1)} %all_gather.3.tokens_ref, s32[1,64]{1,0:T(1,128)} %reshape.40.counts_ref), custom_call_target="tpu_custom_call" | custom-call | flops 1541406720 | bytes 1214464 | tf_op jit(solution)/shard_map/pallas_call | solution.py:167
  (3 shorter events, 0.0 us)
Async XLA Ops:
  0.0 1.4 %copy-start = (bf16[8,32,128]{2,1,0:T(8,128)(2,1)S(1)}, bf16[8,32,128]{2,1,0:T(8,128)(2,1)}, u32[]{:S(2)}) copy-start(bf16[8,32,128]{2,1,0:T(8,128)(2,1)} %param.12) | copy-start | bytes 196612
  8.5 25.3 %all-to-all-start = ((bf16[8,336,128]{2,1,0:T(8,128)(2,1)}), bf16[8,336,128]{2,1,0:T(8,128)(2,1)S(1)}, u32[]{:S(2)}, u32[]{:S(2)}) async-start(bf16[8,336,128]{2,1,0:T(8,128)(2,1)} %shard_map.73), calls=%async_computation | async-start | bytes 1376256 | tf_op jit(solution)/shard_map/all_to_all | solution.py:200
  33.8 3.7 %copy-start.1 = (bf16[8,336,128]{2,1,0:T(8,128)(2,1)}, bf16[8,336,128]{2,1,0:T(8,128)(2,1)S(1)}, u32[]{:S(2)}) copy-start(bf16[8,336,128]{2,1,0:T(8,128)(2,1)S(1)} %all-to-all-done.received_ref) | copy-start | bytes 2064388

commit v4 on v3

--- a/solution.py
+++ b/solution.py
@@ -11,20 +11,19 @@
 PAGES_DEV = 8
 
 
-def embed(rows, weight, bias):
-    proj = jnp.dot(rows, weight, preferred_element_type=jnp.float32) + bias[None, :]
-    scale = lax.rsqrt(jnp.sum(proj * proj, axis=1, keepdims=True) + 1e-06)
-    return (proj * scale).astype(jnp.bfloat16)
-
-
-def send_kernel(page_total, capacity, query_rows, block_at, meta_ref, rows_ref, weight_ref, bias_ref, half_ref,
-                message_ref):
+def send_kernel(page_total, capacity, query_rows, block_at, scalars_ref, owner_ref, page_ref, rows_ref, weight_ref,
+                bias_ref, queries_ref, message_ref):
     owners = message_ref.shape[0]
     rows = rows_ref.shape[0]
     proj = jnp.dot(rows_ref[...], weight_ref[...], preferred_element_type=jnp.float32) + bias_ref[...]
     scale = lax.rsqrt(jnp.sum(proj * proj, axis=1, keepdims=True) + 1e-06)
     local = (proj * scale).astype(jnp.bfloat16)
-    combo = meta_ref[0:1, :] * page_total + meta_ref[1:2, :]
+    diagonal = lax.broadcasted_iota(jnp.int32, (rows, rows), 0) == lax.broadcasted_iota(jnp.int32, (rows, rows), 1)
+    spread = jnp.where(diagonal, owner_ref[...].astype(jnp.float32), 0.0).astype(jnp.bfloat16)
+    owner = lax.dot_general(
+        jnp.ones((1, rows), jnp.bfloat16), spread, (((1,), (1,)), ((), ())), preferred_element_type=jnp.float32
+    ).astype(jnp.int32)
+    combo = owner * page_total + page_ref[...]
     combos = -(-owners * page_total // 128) * 128
     combo_id = lax.broadcasted_iota(jnp.int32, (combos, rows), 0)
     onehot = (combo == combo_id).astype(jnp.bfloat16)
@@ -47,46 +46,53 @@
         )
         for group in range(combos // 128)
     ]
+    lane = lax.broadcasted_iota(jnp.int32, (1, 128), 1)
+    query_count_row = jnp.zeros((1, 128), jnp.float32)
+    for query in range(scalars_ref.shape[0] - 1):
+        query_count_row = jnp.where(lane == query, scalars_ref[query + 1].astype(jnp.float32), query_count_row)
     block_rows = message_ref.shape[1] - block_at
     block = jnp.concatenate(
         count_rows
-        + [meta_ref[2:3, 0:128].astype(jnp.float32), jnp.zeros((block_rows - len(count_rows) - 1, 128), jnp.float32)],
+        + [query_count_row, jnp.zeros((block_rows - len(count_rows) - 1, 128), jnp.float32)],
         axis=0,
     ).astype(jnp.bfloat16)
+    own_half = queries_ref[pl.ds(pl.multiple_of(scalars_ref[0] * query_rows, query_rows), query_rows), :]
     slot_id = lax.broadcasted_iota(jnp.int32, (capacity, rows), 0)
     for owner in range(owners):
         placed = (slot == slot_id + owner * capacity).astype(jnp.bfloat16)
-        message_ref[owner, 0:query_rows, :] = half_ref[...]
+        message_ref[owner, 0:query_rows, :] = own_half
         message_ref[owner, query_rows : query_rows + capacity, :] = jnp.dot(
             placed, local, preferred_element_type=jnp.float32
         ).astype(jnp.bfloat16)
         message_ref[owner, block_at:, :] = block
 
 
-def send_message(patch_rows, owner_ids, page_ids, proj_weight, proj_bias, own_half, query_counts, owners, capacity):
+def send_message(patch_rows, owner_ids, page_ids, proj_weight, proj_bias, query_tokens, query_counts, owners, capacity,
+                 halves):
     rows, features = patch_rows.shape
-    query_rows, width = own_half.shape
+    per_block, token_slots, width = query_tokens.shape
+    query_rows = per_block // halves * token_slots
     block_at = -(-(query_rows + capacity) // 16) * 16
-    meta = jnp.concatenate(
-        [owner_ids.reshape(1, rows), page_ids.reshape(1, rows), jnp.pad(query_counts, (0, rows - query_counts.shape[0])).reshape(1, rows)],
-        axis=0,
-    )
+    scalars = jnp.concatenate([lax.axis_index("inner").astype(jnp.int32).reshape(1), query_counts])
     vmem = pl.BlockSpec(memory_space=pltpu.VMEM)
     return pl.pallas_call(
         functools.partial(send_kernel, PAGES_DEV, capacity, query_rows, block_at),
         out_shape=jax.ShapeDtypeStruct((owners, block_at + 16, width), jnp.bfloat16),
-        in_specs=[vmem] * 5,
+        in_specs=[pl.BlockSpec(memory_space=pltpu.SMEM)] + [vmem] * 6,
         out_specs=vmem,
         cost_estimate=pl.CostEstimate(
             flops=2 * rows * width * (features + owners * capacity),
             bytes_accessed=2 * (rows * features + features * width + owners * (block_at + 16) * width),
             transcendentals=rows,
         ),
-    )(meta, patch_rows, proj_weight, proj_bias.reshape(1, width), own_half)
-
-
-def score_kernel(page_total, token_slots, query_rows, token_block, table_ref, received_ref, tokens_ref, counts_ref,
-                 out_ref, ordered_ref, sims_ref):
+    )(
+        scalars, owner_ids, page_ids.reshape(1, rows), patch_rows, proj_weight, proj_bias.reshape(1, width),
+        query_tokens.reshape(per_block * token_slots, width),
+    )
+
+
+def score_kernel(page_total, token_slots, query_rows, token_block, table_ref, received_ref, tokens_ref, out_ref,
+                 ordered_ref, sims_ref):
     owners = received_ref.shape[0]
     ordered_rows, width = ordered_ref.shape
     capacity = (ordered_rows - 16 * page_total - 16) // owners
@@ -116,6 +122,10 @@
     ordered_ref[...] = ordered.astype(jnp.bfloat16)
     sources = token_block // tokens_ref.shape[1]
     sub = lax.broadcasted_iota(jnp.int32, (8, token_block), 0)
+    query_lane = lax.broadcasted_iota(jnp.int32, (1, total_queries), 1)
+    live_count = jnp.zeros((1, total_queries), jnp.int32)
+    for query in range(total_queries):
+        live_count = jnp.where(query_lane == query, table_ref[owners * page_total + query], live_count)
     token_id = lax.broadcasted_iota(jnp.int32, (token_block, total_queries), 0)
     query_id = lax.broadcasted_iota(jnp.int32, (token_block, total_queries), 1)
 
@@ -145,7 +155,7 @@
             best_rows.append(jnp.max(jnp.maximum(low, high), axis=0, keepdims=True))
         best = jnp.concatenate(best_rows, axis=0)
         token = token_id + block * token_block
-        live = ((token // token_slots) == query_id) & ((token % token_slots) < counts_ref[...])
+        live = ((token // token_slots) == query_id) & ((token % token_slots) < live_count)
         return total + jnp.dot(
             best, live.astype(jnp.float32), precision=lax.Precision.HIGHEST, preferred_element_type=jnp.float32
         )
@@ -156,18 +166,17 @@
     )
 
 
-def page_scores(received, tokens, table, counts, page_total, token_slots, query_rows, capacity):
+def page_scores(received, tokens, table, total_queries, page_total, token_slots, query_rows, capacity):
     owners = received.shape[0]
     width = received.shape[2]
     ordered_rows = owners * capacity + 16 * page_total + 16
     token_total = tokens.shape[0] * tokens.shape[1]
-    total_queries = counts.shape[1]
     token_block = min(token_total, 1024)
     vmem = pl.BlockSpec(memory_space=pltpu.VMEM)
     return pl.pallas_call(
         functools.partial(score_kernel, page_total, token_slots, query_rows, token_block),
         out_shape=jax.ShapeDtypeStruct((page_total, total_queries), jnp.float32),
-        in_specs=[pl.BlockSpec(memory_space=pltpu.SMEM), vmem, vmem, vmem],
+        in_specs=[pl.BlockSpec(memory_space=pltpu.SMEM), vmem, vmem],
         out_specs=vmem,
         scratch_shapes=[
             pltpu.VMEM((ordered_rows, width), jnp.bfloat16),
@@ -178,7 +187,7 @@
             bytes_accessed=2 * received.size + 2 * tokens.size + 4 * page_total * total_queries,
             transcendentals=0,
         ),
-    )(table, received, tokens, counts)
+    )(table, received, tokens)
 
 
 def shards(patch_rows, owner_ids, page_ids, proj_weight, proj_bias, query_tokens, query_counts):
@@ -192,10 +201,8 @@
     total_queries = per_block * owners
     half_queries = per_block // halves
     query_rows = half_queries * token_slots
-    own_half = lax.dynamic_slice_in_dim(query_tokens, lax.axis_index("inner") * half_queries, half_queries, axis=0)
     message = send_message(
-        patch_rows, owner_ids, page_ids, proj_weight, proj_bias, own_half.reshape(query_rows, width), query_counts,
-        owners, capacity,
+        patch_rows, owner_ids, page_ids, proj_weight, proj_bias, query_tokens, query_counts, owners, capacity, halves
     )
     received = lax.all_to_all(message, "blk", split_axis=0, concat_axis=0, tiled=True)
     halves_in = lax.all_gather(received[:, :query_rows], "inner", axis=1, tiled=True)
@@ -204,9 +211,9 @@
     count_rows = combos // 128
     page_counts = received[:, block_at : block_at + count_rows].reshape(owners, combos)
     page_counts = lax.dynamic_slice_in_dim(page_counts, lax.axis_index("blk") * PAGES_DEV, PAGES_DEV, axis=1)
-    table = page_counts.astype(jnp.int32).reshape(owners * PAGES_DEV)
-    counts = received[:, block_at + count_rows, :per_block].astype(jnp.int32).reshape(1, total_queries)
-    return page_scores(received, halves_in, table, counts, PAGES_DEV, token_slots, query_rows, capacity)
+    counts = received[:, block_at + count_rows, :per_block]
+    table = jnp.concatenate([page_counts.reshape(owners * PAGES_DEV), counts.reshape(total_queries)]).astype(jnp.int32)
+    return page_scores(received, halves_in, table, total_queries, PAGES_DEV, token_slots, query_rows, capacity)
 
 
 def solution(mesh):

time: 46.1 us -> 47.8 us (1.037)
  Pallas kernels: 13.4 us -> 14.3 us
  other arithmetic: 1.39 us -> 1.88 us
    unnamed x4 -> x3, local copies, waits for them, and re-layouts: 0.01 us -> 1.62 us
    convert_element_type x2 -> x0, local copies, waits for them, and re-layouts: 1.26 us -> none  [the longest x1 0.64 us: shards(): received[:, block_at + count_rows, :per_block].astype(jnp.int32)]
    pallas_call x1, Pallas kernels: 5.18 us -> 5.86 us  [send_message(): pl.pallas_call(functools.partial(send_kernel, PAGES_DEV, capacity, query_...]
    pad x1 -> x0, local copies, waits for them, and re-layouts: 0.66 us -> none  [send_message(): jnp.pad(query_counts, (0, rows - query_counts.shape[0])).reshape(1, rows)]
    reshape x1, local copies, waits for them, and re-layouts: 0.72 us -> 1.27 us  [send_message(): page_ids.reshape(1, rows)]
    convert_element_type x1, other arithmetic: 0.1 us -> 0.62 us  [shards(): jnp.concatenate([page_counts.reshape(owners * PAGES_DEV), counts.reshape(...]
    dynamic_slice x1, local copies, waits for them, and re-layouts: 0.61 us -> 0.1 us  [shards(): lax.dynamic_slice_in_dim(page_counts, lax.axis_index('blk') * PAGES_DEV,...]
where the time goes in v4:
time: 47.8 us; the launch traced here: 47.1 us
  waiting for transfers between devices  18 us (38%)
  Pallas kernels  14.3 us (30%)
  starting transfers between devices  7.31 us (15%)
  local copies, waits for them, and re-layouts  3.21 us (7%)
  blocking collectives  2.31 us (5%)
  other arithmetic  1.88 us (4%)
    all_to_all x1, waiting for transfers between devices, shards(): lax.all_to_all(message, 'blk', split_axis=0, concat_axis=0, tiled=True)  18 us
    pallas_call x1, Pallas kernels, page_scores(): pl.pallas_call(functools.partial(score_kernel, page_total, token_slots, q...  8.46 us
    all_to_all x1, starting transfers between devices, shards(): lax.all_to_all(message, 'blk', split_axis=0, concat_axis=0, tiled=True)  7.31 us
    pallas_call x1, Pallas kernels, send_message(): pl.pallas_call(functools.partial(send_kernel, PAGES_DEV, capacity, query_...  5.86 us
    all_gather x1, blocking collectives, shards(): lax.all_gather(received[:, :query_rows], 'inner', axis=1, tiled=True)  2.31 us
    unnamed x3, local copies, waits for them, and re-layouts  1.62 us
    reshape x1, local copies, waits for them, and re-layouts, send_message(): page_ids.reshape(1, rows)  1.27 us
    concatenate x1, other arithmetic, send_message(): jnp.concatenate([lax.axis_index('inner').astype(jnp.int32).reshape(1), qu...  1.27 us
  transfers between devices with their start and end apart: 1, of which 1 were waited for; matrix products, arithmetic and copies ran while one was open for 0% of the time, Pallas kernels for 0%

profile of v4, /device:TPU:0, one launch (start us, length us, event | category | flops | bytes accessed | tf_op | source)
XLA Modules:
  0.0 47.1 jit_solution(8497914374944473100)
XLA Ops:
  0.0 1.3 %reshape.19.page_ref = s32[1,768]{1,0:T(1,128)} reshape(s32[768]{0:T(1024)} %param.9) | data formatting | bytes 6144 | tf_op jit(solution)/shard_map/reshape | solution.py:89
  1.3 1.6 %copy.9.owner_ref = s32[768,1]{1,0:T(8,128)} copy(s32[768,1]{0,1:T(1,128)} %param.8) | data formatting | bytes 6144 | tf_op args[1]
  2.9 1.3 %pad_add_fusion.scalars_ref = s32[9]{0:T(128)} fusion(s32[8]{0:T(128)} %param.13, s32[1]{0:T(128)} %bitcast), kind=kLoop, calls=%fused_computation.2 | loop fusion | flops 9 | bytes 72 | tf_op jit(solution)/shard_map/concatenate | solution.py:76
  4.2 5.9 %shard_map.73 = bf16[8,336,128]{2,1,0:T(8,128)(2,1)} custom-call(s32[9]{0:T(128)} %pad_add_fusion.scalars_ref, s32[768,1]{1,0:T(8,128)} %copy.9.owner_ref, s32[1,768]{1,0:T(1,128)} %reshape.19.page_ref, bf16[768,1536]{1,0:T(8,128)(2,1)} %rows_ref.1, bf16[1536,128]{1,0:T(8,128)(2,1)} %weight_ref.1, f32[1,128]{1,0:T(1,128)} %bitcast.4, bf16[256,128]{1,0:T(8,128)(2,1)} %bitcast.3), custom_call_target="tpu_custom_call" | custom-call | flops 603979776 | bytes 3440640 | tf_op jit(solution)/shard_map/pallas_call | solution.py:78
  10.0 7.3 %all-to-all-start = ((bf16[8,336,128]{2,1,0:T(8,128)(2,1)}), bf16[8,336,128]{2,1,0:T(8,128)(2,1)S(1)}, u32[]{:S(2)}, u32[]{:S(2)}) async-start(bf16[8,336,128]{2,1,0:T(8,128)(2,1)} %shard_map.73), calls=%async_computation | async-start | bytes 1376256 | tf_op jit(solution)/shard_map/all_to_all | solution.py:207
  17.3 18.0 %all-to-all-done.received_ref = bf16[8,336,128]{2,1,0:T(8,128)(2,1)S(1)} async-done(((bf16[8,336,128]{2,1,0:T(8,128)(2,1)}), bf16[8,336,128]{2,1,0:T(8,128)(2,1)S(1)}, u32[]{:S(2)}, u32[]{:S(2)}) %all-to-all-start) | async-done | bytes 688160 | tf_op jit(solution)/shard_map/all_to_all | solution.py:207
  35.3 0.0 copy-start
  35.3 0.1 reshape_squeeze.3
  35.4 0.1 dynamic-slice_reduce_fusion
  35.5 0.1 reshape.22
  35.7 2.3 %all_gather.3.tokens_ref = bf16[8,256,128]{2,1,0:T(8,128)(2,1)} all-gather(bf16[8,128,128]{2,1,0:T(8,128)(2,1)S(1)} %slice.14), channel_id=1, replica_groups=mesh['groups'=2,'blk'=8,'inner'=2] {'inner'}, dimensions={1}, use_global_device_ids=true | all-gather | bytes 786432 | tf_op jit(solution)/shard_map/all_gather | solution.py:208
  38.0 0.6 %maximum_convert_fusion.table_ref = s32[128]{0:T(128)} fusion(bf16[64]{0:T(256)(128)(2,1)S(1)} %reshape_squeeze.3, bf16[64]{0:T(256)(128)(2,1)S(1)} %reshape.22), kind=kLoop, calls=%fused_computation.3 | loop fusion | flops 512 | bytes 768 | tf_op jit(solution)/shard_map/convert_element_type | solution.py:215
  38.6 0.0 copy-done
  38.6 8.5 %shard_map.74 = f32[8,64]{1,0:T(8,128)} custom-call(s32[128]{0:T(128)} %maximum_convert_fusion.table_ref, bf16[8,336,128]{2,1,0:T(8,128)(2,1)} %copy-done, bf16[8,256,128]{2,1,0:T(8,128)(2,1)} %all_gather.3.tokens_ref), custom_call_target="tpu_custom_call" | custom-call | flops 1541406720 | bytes 1214464 | tf_op jit(solution)/shard_map/pallas_call | solution.py:176
  (3 shorter events, 0.1 us)
Async XLA Ops:
  10.0 25.3 %all-to-all-start = ((bf16[8,336,128]{2,1,0:T(8,128)(2,1)}), bf16[8,336,128]{2,1,0:T(8,128)(2,1)S(1)}, u32[]{:S(2)}, u32[]{:S(2)}) async-start(bf16[8,336,128]{2,1,0:T(8,128)(2,1)} %shard_map.73), calls=%async_computation | async-start | bytes 1376256 | tf_op jit(solution)/shard_map/all_to_all | solution.py:207
  35.3 3.3 %copy-start = (bf16[8,336,128]{2,1,0:T(8,128)(2,1)}, bf16[8,336,128]{2,1,0:T(8,128)(2,1)S(1)}, u32[]{:S(2)}) copy-start(bf16[8,336,128]{2,1,0:T(8,128)(2,1)S(1)} %all-to-all-done.received_ref) | copy-start | bytes 2064388

commit v5 on v4

--- a/solution.py
+++ b/solution.py
@@ -11,19 +11,14 @@
 PAGES_DEV = 8
 
 
-def send_kernel(page_total, capacity, query_rows, block_at, scalars_ref, owner_ref, page_ref, rows_ref, weight_ref,
+def send_kernel(page_total, capacity, query_rows, block_at, query_counts_ref, owner_ref, page_ref, rows_ref, weight_ref,
                 bias_ref, queries_ref, message_ref):
     owners = message_ref.shape[0]
     rows = rows_ref.shape[0]
     proj = jnp.dot(rows_ref[...], weight_ref[...], preferred_element_type=jnp.float32) + bias_ref[...]
     scale = lax.rsqrt(jnp.sum(proj * proj, axis=1, keepdims=True) + 1e-06)
     local = (proj * scale).astype(jnp.bfloat16)
-    diagonal = lax.broadcasted_iota(jnp.int32, (rows, rows), 0) == lax.broadcasted_iota(jnp.int32, (rows, rows), 1)
-    spread = jnp.where(diagonal, owner_ref[...].astype(jnp.float32), 0.0).astype(jnp.bfloat16)
-    owner = lax.dot_general(
-        jnp.ones((1, rows), jnp.bfloat16), spread, (((1,), (1,)), ((), ())), preferred_element_type=jnp.float32
-    ).astype(jnp.int32)
-    combo = owner * page_total + page_ref[...]
+    combo = owner_ref[...].reshape(1, rows) * page_total + page_ref[...].reshape(1, rows)
     combos = -(-owners * page_total // 128) * 128
     combo_id = lax.broadcasted_iota(jnp.int32, (combos, rows), 0)
     onehot = (combo == combo_id).astype(jnp.bfloat16)
@@ -48,15 +43,15 @@
     ]
     lane = lax.broadcasted_iota(jnp.int32, (1, 128), 1)
     query_count_row = jnp.zeros((1, 128), jnp.float32)
-    for query in range(scalars_ref.shape[0] - 1):
-        query_count_row = jnp.where(lane == query, scalars_ref[query + 1].astype(jnp.float32), query_count_row)
+    for query in range(query_counts_ref.shape[0]):
+        query_count_row = jnp.where(lane == query, query_counts_ref[query].astype(jnp.float32), query_count_row)
     block_rows = message_ref.shape[1] - block_at
     block = jnp.concatenate(
         count_rows
         + [query_count_row, jnp.zeros((block_rows - len(count_rows) - 1, 128), jnp.float32)],
         axis=0,
     ).astype(jnp.bfloat16)
-    own_half = queries_ref[pl.ds(pl.multiple_of(scalars_ref[0] * query_rows, query_rows), query_rows), :]
+    own_half = queries_ref[pl.ds(pl.multiple_of(lax.axis_index("inner") * query_rows, query_rows), query_rows), :]
     slot_id = lax.broadcasted_iota(jnp.int32, (capacity, rows), 0)
     for owner in range(owners):
         placed = (slot == slot_id + owner * capacity).astype(jnp.bfloat16)
@@ -73,7 +68,6 @@
     per_block, token_slots, width = query_tokens.shape
     query_rows = per_block // halves * token_slots
     block_at = -(-(query_rows + capacity) // 16) * 16
-    scalars = jnp.concatenate([lax.axis_index("inner").astype(jnp.int32).reshape(1), query_counts])
     vmem = pl.BlockSpec(memory_space=pltpu.VMEM)
     return pl.pallas_call(
         functools.partial(send_kernel, PAGES_DEV, capacity, query_rows, block_at),
@@ -86,7 +80,7 @@
             transcendentals=rows,
         ),
     )(
-        scalars, owner_ids, page_ids.reshape(1, rows), patch_rows, proj_weight, proj_bias.reshape(1, width),
+        query_counts, owner_ids.reshape(rows), page_ids, patch_rows, proj_weight, proj_bias.reshape(1, width),
         query_tokens.reshape(per_block * token_slots, width),
     )
 

time: 47.8 us -> 43.7 us (0.914); the launches traced: 47.1 us -> 43.5 us
  local copies, waits for them, and re-layouts: 3.21 us -> 0.33 us
  Pallas kernels: 14.3 us -> 13.6 us
    unnamed x3 -> x2, local copies, waits for them, and re-layouts: 1.62 us -> 0.01 us
    unnamed x0 -> x1, other arithmetic: none -> 1.29 us
    reshape x1 -> x0, local copies, waits for them, and re-layouts: 1.27 us -> none  [send_message(): page_ids.reshape(1, rows)]
    concatenate x1 -> x0, other arithmetic: 1.27 us -> none  [send_message(): jnp.concatenate([lax.axis_index('inner').astype(jnp.int32).reshape(1), qu...]
    pallas_call x1, Pallas kernels: 5.86 us -> 5.28 us  [send_message(): pl.pallas_call(functools.partial(send_kernel, PAGES_DEV, capacity, query_...]
where the time goes in v5:
time: 43.7 us; the launch traced here: 43.5 us
  waiting for transfers between devices  18 us (41%)
  Pallas kernels  13.6 us (31%)
  starting transfers between devices  7.31 us (17%)
  blocking collectives  2.31 us (5%)
  other arithmetic  1.9 us (4%)
    all_to_all x1, waiting for transfers between devices, shards(): lax.all_to_all(message, 'blk', split_axis=0, concat_axis=0, tiled=True)  18 us
    pallas_call x1, Pallas kernels, page_scores(): pl.pallas_call(functools.partial(score_kernel, page_total, token_slots, q...  8.32 us
    all_to_all x1, starting transfers between devices, shards(): lax.all_to_all(message, 'blk', split_axis=0, concat_axis=0, tiled=True)  7.31 us
    pallas_call x1, Pallas kernels, send_message(): pl.pallas_call(functools.partial(send_kernel, PAGES_DEV, capacity, query_...  5.28 us
    all_gather x1, blocking collectives, shards(): lax.all_gather(received[:, :query_rows], 'inner', axis=1, tiled=True)  2.31 us
    unnamed x1, other arithmetic  1.29 us
  transfers between devices with their start and end apart: 1, of which 1 were waited for; matrix products, arithmetic and copies ran while one was open for 0% of the time, Pallas kernels for 0%

profile of v5, /device:TPU:0, one launch (start us, length us, event | category | flops | bytes accessed | tf_op | source)
XLA Modules:
  0.0 43.5 jit_solution(17190248306640002822)
XLA Ops:
  0.0 1.3 %reduce.owner_ref = s32[768]{0:T(1024)} reduce(s32[768,1]{0,1:T(1,128)} %param.8, s32[]{:T(128)} %constant.3.clone.1), dimensions={1}, to_apply=%param.8.reduce_sub_computation | reduce | bytes 6148 | tf_op args[1]
  1.3 5.3 %shard_map.73 = bf16[8,336,128]{2,1,0:T(8,128)(2,1)} custom-call(s32[8]{0:T(128)} %query_counts_ref.1, s32[768]{0:T(1024)} %reduce.owner_ref, s32[768]{0:T(1024)} %page_ref.1, bf16[768,1536]{1,0:T(8,128)(2,1)} %rows_ref.1, bf16[1536,128]{1,0:T(8,128)(2,1)} %weight_ref.1, f32[1,128]{1,0:T(1,128)} %bitcast.3, bf16[256,128]{1,0:T(8,128)(2,1)} %bitcast.2), custom_call_target="tpu_custom_call" | custom-call | flops 603979776 | bytes 3440640 | tf_op jit(solution)/shard_map/pallas_call | solution.py:72
  6.6 7.3 %all-to-all-start = ((bf16[8,336,128]{2,1,0:T(8,128)(2,1)}), bf16[8,336,128]{2,1,0:T(8,128)(2,1)S(1)}, u32[]{:S(2)}, u32[]{:S(2)}) async-start(bf16[8,336,128]{2,1,0:T(8,128)(2,1)} %shard_map.73), calls=%async_computation | async-start | bytes 1376256 | tf_op jit(solution)/shard_map/all_to_all | solution.py:201
  13.9 18.0 %all-to-all-done.received_ref = bf16[8,336,128]{2,1,0:T(8,128)(2,1)S(1)} async-done(((bf16[8,336,128]{2,1,0:T(8,128)(2,1)}), bf16[8,336,128]{2,1,0:T(8,128)(2,1)S(1)}, u32[]{:S(2)}, u32[]{:S(2)}) %all-to-all-start) | async-done | bytes 688160 | tf_op jit(solution)/shard_map/all_to_all | solution.py:201
  31.9 0.0 copy-start
  31.9 0.1 reshape_squeeze.3
  32.0 0.1 dynamic-slice_reduce_fusion
  32.1 0.1 reshape.18
  32.2 2.3 %all_gather.3.tokens_ref = bf16[8,256,128]{2,1,0:T(8,128)(2,1)} all-gather(bf16[8,128,128]{2,1,0:T(8,128)(2,1)S(1)} %slice.14), channel_id=1, replica_groups=mesh['groups'=2,'blk'=8,'inner'=2] {'inner'}, dimensions={1}, use_global_device_ids=true | all-gather | bytes 786432 | tf_op jit(solution)/shard_map/all_gather | solution.py:202
  34.5 0.6 %maximum_convert_fusion.table_ref = s32[128]{0:T(128)} fusion(bf16[64]{0:T(256)(128)(2,1)S(1)} %reshape_squeeze.3, bf16[64]{0:T(256)(128)(2,1)S(1)} %reshape.18), kind=kLoop, calls=%fused_computation.2 | loop fusion | flops 512 | bytes 768 | tf_op jit(solution)/shard_map/convert_element_type | solution.py:209
  35.2 0.0 copy-done
  35.2 8.3 %shard_map.74 = f32[8,64]{1,0:T(8,128)} custom-call(s32[128]{0:T(128)} %maximum_convert_fusion.table_ref, bf16[8,336,128]{2,1,0:T(8,128)(2,1)} %copy-done, bf16[8,256,128]{2,1,0:T(8,128)(2,1)} %all_gather.3.tokens_ref), custom_call_target="tpu_custom_call" | custom-call | flops 1541406720 | bytes 1214464 | tf_op jit(solution)/shard_map/pallas_call | solution.py:170
  (3 shorter events, 0.1 us)
Async XLA Ops:
  6.6 25.3 %all-to-all-start = ((bf16[8,336,128]{2,1,0:T(8,128)(2,1)}), bf16[8,336,128]{2,1,0:T(8,128)(2,1)S(1)}, u32[]{:S(2)}, u32[]{:S(2)}) async-start(bf16[8,336,128]{2,1,0:T(8,128)(2,1)} %shard_map.73), calls=%async_computation | async-start | bytes 1376256 | tf_op jit(solution)/shard_map/all_to_all | solution.py:201
  31.9 3.3 %copy-start = (bf16[8,336,128]{2,1,0:T(8,128)(2,1)}, bf16[8,336,128]{2,1,0:T(8,128)(2,1)S(1)}, u32[]{:S(2)}) copy-start(bf16[8,336,128]{2,1,0:T(8,128)(2,1)S(1)} %all-to-all-done.received_ref) | copy-start | bytes 2064388

commit v6 on v5

--- a/solution.py
+++ b/solution.py
@@ -85,18 +85,74 @@
     )
 
 
-def score_kernel(page_total, token_slots, query_rows, token_block, table_ref, received_ref, tokens_ref, out_ref,
-                 ordered_ref, sims_ref):
-    owners = received_ref.shape[0]
-    ordered_rows, width = ordered_ref.shape
-    capacity = (ordered_rows - 16 * page_total - 16) // owners
-    total_queries = out_ref.shape[1]
+def page_runs(table_ref, owners, page_total):
     totals = [sum(table_ref[chunk * page_total + page] for chunk in range(owners)) for page in range(page_total)]
     firsts = []
     at = 0
     for page in range(page_total):
         firsts.append(at)
         at = at + (totals[page] + 15) // 16 * 16
+    return totals, firsts
+
+
+def half_scores(table_ref, ordered_ref, sims_ref, tokens_ref, half, owners, page_total, token_slots, per_block,
+                total_queries):
+    ordered_rows, width = ordered_ref.shape
+    token_block = sims_ref.shape[1]
+    half_rows = tokens_ref.shape[1]
+    half_queries = half_rows // token_slots
+    totals, firsts = page_runs(table_ref, owners, page_total)
+    query_lane = lax.broadcasted_iota(jnp.int32, (1, total_queries), 1)
+    live_count = jnp.zeros((1, total_queries), jnp.int32)
+    for query in range(total_queries):
+        live_count = jnp.where(query_lane == query, table_ref[owners * page_total + query], live_count)
+    sub = lax.broadcasted_iota(jnp.int32, (8, token_block), 0)
+    token_id = lax.broadcasted_iota(jnp.int32, (token_block, total_queries), 0)
+    query_id = lax.broadcasted_iota(jnp.int32, (token_block, total_queries), 1)
+    sources = token_block // half_rows
+
+    def block_scores(block, total):
+        tokens = tokens_ref[pl.ds(block * sources, sources)].reshape(token_block, width)
+        sims_ref[...] = lax.dot_general(
+            ordered_ref[...], tokens, (((1,), (1,)), ((), ())), preferred_element_type=jnp.float32
+        )
+        best_rows = []
+        for page in range(page_total):
+            first = firsts[page]
+            whole = totals[page] // 16
+            rest = totals[page] % 16
+
+            def step(i, carry):
+                start = pl.multiple_of(first + i * 16, 16)
+                return (
+                    jnp.maximum(carry[0], sims_ref[pl.ds(start, 8), :]),
+                    jnp.maximum(carry[1], sims_ref[pl.ds(start + 8, 8), :]),
+                )
+
+            floor = jnp.full((8, token_block), -2.0, jnp.float32)
+            low, high = lax.fori_loop(0, whole, step, (floor, floor))
+            start = pl.multiple_of(first + whole * 16, 16)
+            low = jnp.maximum(low, jnp.where(sub < rest, sims_ref[pl.ds(start, 8), :], jnp.float32(-2.0)))
+            high = jnp.maximum(high, jnp.where(sub + 8 < rest, sims_ref[pl.ds(start + 8, 8), :], jnp.float32(-2.0)))
+            best_rows.append(jnp.max(jnp.maximum(low, high), axis=0, keepdims=True))
+        best = jnp.concatenate(best_rows, axis=0)
+        token = token_id + block * token_block
+        query = token // half_rows * per_block + half * half_queries + token % half_rows // token_slots
+        live = (query == query_id) & ((token % token_slots) < live_count)
+        return total + jnp.dot(
+            best, live.astype(jnp.float32), precision=lax.Precision.HIGHEST, preferred_element_type=jnp.float32
+        )
+
+    blocks = tokens_ref.shape[0] * half_rows // token_block
+    return lax.fori_loop(0, blocks, block_scores, jnp.zeros((page_total, total_queries), jnp.float32))
+
+
+def first_kernel(page_total, token_slots, per_block, query_rows, table_ref, received_ref, out_ref, ordered_ref,
+                 sims_ref):
+    owners = received_ref.shape[0]
+    ordered_rows, width = ordered_ref.shape
+    capacity = (ordered_rows - 16 * page_total - 16) // owners
+    totals, firsts = page_runs(table_ref, owners, page_total)
     target = lax.broadcasted_iota(jnp.int32, (ordered_rows, capacity), 0)
     slot = lax.broadcasted_iota(jnp.int32, (1, capacity), 1)
     ordered = jnp.zeros((ordered_rows, width), jnp.float32)
@@ -114,74 +170,57 @@
         rows = received_ref[chunk, query_rows : query_rows + capacity, :]
         ordered = ordered + jnp.dot(place, rows, preferred_element_type=jnp.float32)
     ordered_ref[...] = ordered.astype(jnp.bfloat16)
-    sources = token_block // tokens_ref.shape[1]
-    sub = lax.broadcasted_iota(jnp.int32, (8, token_block), 0)
-    query_lane = lax.broadcasted_iota(jnp.int32, (1, total_queries), 1)
-    live_count = jnp.zeros((1, total_queries), jnp.int32)
-    for query in range(total_queries):
-        live_count = jnp.where(query_lane == query, table_ref[owners * page_total + query], live_count)
-    token_id = lax.broadcasted_iota(jnp.int32, (token_block, total_queries), 0)
-    query_id = lax.broadcasted_iota(jnp.int32, (token_block, total_queries), 1)
-
-    def block_scores(block, total):
-        tokens = tokens_ref[pl.ds(block * sources, sources)].reshape(token_block, width)
-        sims_ref[...] = lax.dot_general(
-            ordered_ref[...], tokens, (((1,), (1,)), ((), ())), preferred_element_type=jnp.float32
-        )
-        best_rows = []
-        for page in range(page_total):
-            first = firsts[page]
-            whole = totals[page] // 16
-            rest = totals[page] % 16
-
-            def step(i, carry):
-                start = pl.multiple_of(first + i * 16, 16)
-                return (
-                    jnp.maximum(carry[0], sims_ref[pl.ds(start, 8), :]),
-                    jnp.maximum(carry[1], sims_ref[pl.ds(start + 8, 8), :]),
-                )
-
-            floor = jnp.full((8, token_block), -2.0, jnp.float32)
-            low, high = lax.fori_loop(0, whole, step, (floor, floor))
-            start = pl.multiple_of(first + whole * 16, 16)
-            low = jnp.maximum(low, jnp.where(sub < rest, sims_ref[pl.ds(start, 8), :], jnp.float32(-2.0)))
-            high = jnp.maximum(high, jnp.where(sub + 8 < rest, sims_ref[pl.ds(start + 8, 8), :], jnp.float32(-2.0)))
-            best_rows.append(jnp.max(jnp.maximum(low, high), axis=0, keepdims=True))
-        best = jnp.concatenate(best_rows, axis=0)
-        token = token_id + block * token_block
-        live = ((token // token_slots) == query_id) & ((token % token_slots) < live_count)
-        return total + jnp.dot(
-            best, live.astype(jnp.float32), precision=lax.Precision.HIGHEST, preferred_element_type=jnp.float32
-        )
-
-    blocks = tokens_ref.shape[0] * tokens_ref.shape[1] // token_block
-    out_ref[...] = lax.fori_loop(
-        0, blocks, block_scores, jnp.zeros((page_total, total_queries), jnp.float32)
-    )
-
-
-def page_scores(received, tokens, table, total_queries, page_total, token_slots, query_rows, capacity):
+    out_ref[...] = half_scores(
+        table_ref, ordered_ref, sims_ref, received_ref.at[:, 0:query_rows, :], lax.axis_index("inner"), owners,
+        page_total, token_slots, per_block, out_ref.shape[1],
+    )
+
+
+def second_kernel(page_total, token_slots, per_block, table_ref, ordered_ref, partner_ref, partial_ref, out_ref,
+                  sims_ref):
+    owners = partner_ref.shape[0]
+    out_ref[...] = partial_ref[...] + half_scores(
+        table_ref, ordered_ref, sims_ref, partner_ref, 1 - lax.axis_index("inner"), owners, page_total, token_slots,
+        per_block, out_ref.shape[1],
+    )
+
+
+def page_scores(received, table, total_queries, page_total, token_slots, per_block, query_rows, capacity):
     owners = received.shape[0]
     width = received.shape[2]
     ordered_rows = owners * capacity + 16 * page_total + 16
-    token_total = tokens.shape[0] * tokens.shape[1]
-    token_block = min(token_total, 1024)
+    token_block = min(owners * query_rows, 1024)
     vmem = pl.BlockSpec(memory_space=pltpu.VMEM)
+    smem = pl.BlockSpec(memory_space=pltpu.SMEM)
+    partner = lax.ppermute(received[:, :query_rows], "inner", [(0, 1), (1, 0)])
+    half_flops = 2 * ordered_rows * width * owners * query_rows
+    partial, ordered = pl.pallas_call(
+        functools.partial(first_kernel, page_total, token_slots, per_block, query_rows),
+        out_shape=(
+            jax.ShapeDtypeStruct((page_total, total_queries), jnp.float32),
+            jax.ShapeDtypeStruct((ordered_rows, width), jnp.bfloat16),
+        ),
+        in_specs=[smem, vmem],
+        out_specs=(vmem, vmem),
+        scratch_shapes=[pltpu.VMEM((ordered_rows, token_block), jnp.float32)],
+        cost_estimate=pl.CostEstimate(
+            flops=2 * ordered_rows * width * owners * capacity + half_flops,
+            bytes_accessed=2 * received.size + 2 * ordered_rows * width + 4 * page_total * total_queries,
+            transcendentals=0,
+        ),
+    )(table, received)
     return pl.pallas_call(
-        functools.partial(score_kernel, page_total, token_slots, query_rows, token_block),
+        functools.partial(second_kernel, page_total, token_slots, per_block),
         out_shape=jax.ShapeDtypeStruct((page_total, total_queries), jnp.float32),
-        in_specs=[pl.BlockSpec(memory_space=pltpu.SMEM), vmem, vmem],
+        in_specs=[smem, vmem, vmem, vmem],
         out_specs=vmem,
-        scratch_shapes=[
-            pltpu.VMEM((ordered_rows, width), jnp.bfloat16),
-            pltpu.VMEM((ordered_rows, token_block), jnp.float32),
-        ],
+        scratch_shapes=[pltpu.VMEM((ordered_rows, token_block), jnp.float32)],
         cost_estimate=pl.CostEstimate(
-            flops=2 * ordered_rows * width * (owners * capacity + token_total),
-            bytes_accessed=2 * received.size + 2 * tokens.size + 4 * page_total * total_queries,
+            flops=half_flops,
+            bytes_accessed=2 * ordered_rows * width + 2 * partner.size + 8 * page_total * total_queries,
             transcendentals=0,
         ),
-    )(table, received, tokens)
+    )(table, ordered, partner, partial)
 
 
 def shards(patch_rows, owner_ids, page_ids, proj_weight, proj_bias, query_tokens, query_counts):
@@ -199,7 +238,6 @@
         patch_rows, owner_ids, page_ids, proj_weight, proj_bias, query_tokens, query_counts, owners, capacity, halves
     )
     received = lax.all_to_all(message, "blk", split_axis=0, concat_axis=0, tiled=True)
-    halves_in = lax.all_gather(received[:, :query_rows], "inner", axis=1, tiled=True)
     block_at = -(-(query_rows + capacity) // 16) * 16
     combos = -(-owners * PAGES_DEV // 128) * 128
     count_rows = combos // 128
@@ -207,7 +245,7 @@
     page_counts = lax.dynamic_slice_in_dim(page_counts, lax.axis_index("blk") * PAGES_DEV, PAGES_DEV, axis=1)
     counts = received[:, block_at + count_rows, :per_block]
     table = jnp.concatenate([page_counts.reshape(owners * PAGES_DEV), counts.reshape(total_queries)]).astype(jnp.int32)
-    return page_scores(received, halves_in, table, total_queries, PAGES_DEV, token_slots, query_rows, capacity)
+    return page_scores(received, table, total_queries, PAGES_DEV, token_slots, per_block, query_rows, capacity)
 
 
 def solution(mesh):

time: 43.7 us -> 45.5 us (1.041)
  Pallas kernels: 13.6 us -> 16.9 us
  blocking collectives: 2.31 us -> 0 us
  local copies, waits for them, and re-layouts: 0.33 us -> 1.02 us
    pallas_call x1 -> x2, Pallas kernels: 8.32 us -> 11.6 us  [the longest x1 7.65 us: page_scores(): pl.pallas_call(functools.partial(first_kernel, page_total, token_slots, p...]
    all_gather x1 -> x0, blocking collectives: 2.31 us -> none  [shards(): lax.all_gather(received[:, :query_rows], 'inner', axis=1, tiled=True)]
    unnamed x2 -> x4, local copies, waits for them, and re-layouts: 0.01 us -> 0.7 us
  transfers between devices with their start and end apart: 1 -> 2, of which waited for: 1 -> 1; matrix products, arithmetic and copies ran while one was open for 0% -> 2% of each run, Pallas kernels for 0% -> 17%
where the time goes in v6:
time: 45.5 us; the launch traced here: 45.3 us
  waiting for transfers between devices  18 us (40%)
  Pallas kernels  16.9 us (37%)
  starting transfers between devices  7.38 us (16%)
  other arithmetic  1.95 us (4%)
  local copies, waits for them, and re-layouts  1.02 us (2%)
    all_to_all x1, waiting for transfers between devices, shards(): lax.all_to_all(message, 'blk', split_axis=0, concat_axis=0, tiled=True)  18 us
    pallas_call x1, Pallas kernels, page_scores(): pl.pallas_call(functools.partial(first_kernel, page_total, token_slots, p...  7.65 us
    all_to_all x1, starting transfers between devices, shards(): lax.all_to_all(message, 'blk', split_axis=0, concat_axis=0, tiled=True)  7.31 us
    pallas_call x1, Pallas kernels, send_message(): pl.pallas_call(functools.partial(send_kernel, PAGES_DEV, capacity, query_...  5.28 us
    pallas_call x1, Pallas kernels, page_scores(): pl.pallas_call(functools.partial(second_kernel, page_total, token_slots,...  3.97 us
    unnamed x1, other arithmetic  1.29 us
  transfers between devices with their start and end apart: 2, of which 1 were waited for; matrix products, arithmetic and copies ran while one was open for 2% of the time, Pallas kernels for 17%

profile of v6, /device:TPU:0, one launch (start us, length us, event | category | flops | bytes accessed | tf_op | source)
XLA Modules:
  0.0 45.3 jit_solution(14673140559143955864)
XLA Ops:
  0.0 1.3 %reduce.owner_ref = s32[768]{0:T(1024)} reduce(s32[768,1]{0,1:T(1,128)} %param.8, s32[]{:T(128)} %constant.3.clone.1), dimensions={1}, to_apply=%param.8.reduce_sub_computation | reduce | bytes 6148 | tf_op args[1]
  1.3 5.3 %shard_map.73 = bf16[8,336,128]{2,1,0:T(8,128)(2,1)} custom-call(s32[8]{0:T(128)} %query_counts_ref.1, s32[768]{0:T(1024)} %reduce.owner_ref, s32[768]{0:T(1024)} %page_ref.1, bf16[768,1536]{1,0:T(8,128)(2,1)} %rows_ref.1, bf16[1536,128]{1,0:T(8,128)(2,1)} %weight_ref.1, f32[1,128]{1,0:T(1,128)} %bitcast.3, bf16[256,128]{1,0:T(8,128)(2,1)} %bitcast.2), custom_call_target="tpu_custom_call" | custom-call | flops 603979776 | bytes 3440640 | tf_op jit(solution)/shard_map/pallas_call | solution.py:72
  6.6 7.3 %all-to-all-start = ((bf16[8,336,128]{2,1,0:T(8,128)(2,1)}), bf16[8,336,128]{2,1,0:T(8,128)(2,1)S(1)}, u32[]{:S(2)}, u32[]{:S(2)}) async-start(bf16[8,336,128]{2,1,0:T(8,128)(2,1)} %shard_map.73), calls=%async_computation | async-start | bytes 1376256 | tf_op jit(solution)/shard_map/all_to_all | solution.py:240
  13.9 18.0 %all-to-all-done.received_ref = bf16[8,336,128]{2,1,0:T(8,128)(2,1)S(1)} async-done(((bf16[8,336,128]{2,1,0:T(8,128)(2,1)}), bf16[8,336,128]{2,1,0:T(8,128)(2,1)S(1)}, u32[]{:S(2)}, u32[]{:S(2)}) %all-to-all-start) | async-done | bytes 688160 | tf_op jit(solution)/shard_map/all_to_all | solution.py:240
  31.9 0.0 copy-start
  31.9 0.1 collective-permute-start
  32.0 0.1 reshape_squeeze.3
  32.1 0.1 dynamic-slice_reduce_fusion
  32.2 0.1 reshape.18
  32.3 0.7 %maximum_convert_fusion.table_ref = s32[128]{0:T(128)} fusion(bf16[64]{0:T(256)(128)(2,1)S(1)} %reshape_squeeze.3, bf16[64]{0:T(256)(128)(2,1)S(1)} %reshape.18), kind=kLoop, calls=%fused_computation.2 | loop fusion | flops 512 | bytes 768 | tf_op jit(solution)/shard_map/convert_element_type | solution.py:247
  33.0 0.0 copy-done
  33.0 7.6 %shard_map.74 = (f32[8,64]{1,0:T(8,128)}, bf16[1680,128]{1,0:T(8,128)(2,1)}) custom-call(s32[128]{0:T(128)} %maximum_convert_fusion.table_ref, bf16[8,336,128]{2,1,0:T(8,128)(2,1)} %copy-done), custom_call_target="tpu_custom_call" | custom-call | flops 1101004800 | bytes 1120256 | tf_op jit(solution)/shard_map/pallas_call | solution.py:197
  40.6 0.0 collective-permute-done.partner_ref
  40.6 0.0 copy-start.1
  40.6 0.7 %copy-done.1 = bf16[8,128,128]{2,1,0:T(8,128)(2,1)} copy-done((bf16[8,128,128]{2,1,0:T(8,128)(2,1)}, bf16[8,128,128]{2,1,0:T(8,128)(2,1)S(1)}, u32[]{:S(2)}) %copy-start.1) | copy-done | bytes 262168
  41.3 4.0 %shard_map.75 = f32[8,64]{1,0:T(8,128)} custom-call(s32[128]{0:T(128)} %maximum_convert_fusion.table_ref, bf16[1680,128]{1,0:T(8,128)(2,1)} %get-tuple-element.7.ordered_ref, bf16[8,128,128]{2,1,0:T(8,128)(2,1)} %copy-done.1, f32[8,64]{1,0:T(8,128)} %get-tuple-element.8.partial_ref), custom_call_target="tpu_custom_call" | custom-call | flops 440401920 | bytes 696320 | tf_op jit(solution)/shard_map/pallas_call | solution.py:212
  (3 shorter events, 0.1 us)
Async XLA Ops:
  6.6 25.3 %all-to-all-start = ((bf16[8,336,128]{2,1,0:T(8,128)(2,1)}), bf16[8,336,128]{2,1,0:T(8,128)(2,1)S(1)}, u32[]{:S(2)}, u32[]{:S(2)}) async-start(bf16[8,336,128]{2,1,0:T(8,128)(2,1)} %shard_map.73), calls=%async_computation | async-start | bytes 1376256 | tf_op jit(solution)/shard_map/all_to_all | solution.py:240
  31.9 1.1 %copy-start = (bf16[8,336,128]{2,1,0:T(8,128)(2,1)}, bf16[8,336,128]{2,1,0:T(8,128)(2,1)S(1)}, u32[]{:S(2)}) copy-start(bf16[8,336,128]{2,1,0:T(8,128)(2,1)S(1)} %all-to-all-done.received_ref) | copy-start | bytes 2064388
  31.9 8.7 %collective-permute-start = (bf16[8,128,128]{2,1,0:T(8,128)(2,1)S(1)}, bf16[8,128,128]{2,1,0:T(8,128)(2,1)S(1)}, u32[]{:S(2)}, u32[]{:S(2)}) collective-permute-start(bf16[8,128,128]{2,1,0:T(8,128)(2,1)S(1)} %slice.14), channel_id=1, source_target_pairs={{0,1},{1,0},{2,3},{3,2},{4,5},{5,4},{6,7},{7,6},{8,9},{9,8},{10,11... | collective-permute-start | bytes 786440 | tf_op jit(solution)/shard_map/ppermute | solution.py:195
  40.6 0.7 %copy-start.1 = (bf16[8,128,128]{2,1,0:T(8,128)(2,1)}, bf16[8,128,128]{2,1,0:T(8,128)(2,1)S(1)}, u32[]{:S(2)}) copy-start(bf16[8,128,128]{2,1,0:T(8,128)(2,1)S(1)} %collective-permute-done.partner_ref) | copy-start | bytes 786436

commit v7 on v5

--- a/solution.py
+++ b/solution.py
@@ -165,7 +165,7 @@
     width = received.shape[2]
     ordered_rows = owners * capacity + 16 * page_total + 16
     token_total = tokens.shape[0] * tokens.shape[1]
-    token_block = min(token_total, 1024)
+    token_block = min(token_total, 2048)
     vmem = pl.BlockSpec(memory_space=pltpu.VMEM)
     return pl.pallas_call(
         functools.partial(score_kernel, page_total, token_slots, query_rows, token_block),

time: 43.7 us -> 46.4 us (1.062)
  Pallas kernels: 13.6 us -> 16.4 us
    pallas_call x1, Pallas kernels: 8.32 us -> 11.1 us  [page_scores(): pl.pallas_call(functools.partial(score_kernel, page_total, token_slots, q...]
where the time goes in v7:
time: 46.4 us; the launch traced here: 46.3 us
  waiting for transfers between devices  18 us (39%)
  Pallas kernels  16.4 us (35%)
  starting transfers between devices  7.31 us (16%)
  blocking collectives  2.31 us (5%)
  other arithmetic  1.9 us (4%)
    all_to_all x1, waiting for transfers between devices, shards(): lax.all_to_all(message, 'blk', split_axis=0, concat_axis=0, tiled=True)  18 us
    pallas_call x1, Pallas kernels, page_scores(): pl.pallas_call(functools.partial(score_kernel, page_total, token_slots, q...  11.1 us
    all_to_all x1, starting transfers between devices, shards(): lax.all_to_all(message, 'blk', split_axis=0, concat_axis=0, tiled=True)  7.31 us
    pallas_call x1, Pallas kernels, send_message(): pl.pallas_call(functools.partial(send_kernel, PAGES_DEV, capacity, query_...  5.28 us
    all_gather x1, blocking collectives, shards(): lax.all_gather(received[:, :query_rows], 'inner', axis=1, tiled=True)  2.31 us
    unnamed x1, other arithmetic  1.29 us
  transfers between devices with their start and end apart: 1, of which 1 were waited for; matrix products, arithmetic and copies ran while one was open for 0% of the time, Pallas kernels for 0%

profile of v7, /device:TPU:0, one launch (start us, length us, event | category | flops | bytes accessed | tf_op | source)
XLA Modules:
  0.0 46.3 jit_solution(2636442514829676526)
XLA Ops:
  0.0 1.3 %reduce.owner_ref = s32[768]{0:T(1024)} reduce(s32[768,1]{0,1:T(1,128)} %param.8, s32[]{:T(128)} %constant.3.clone.1), dimensions={1}, to_apply=%param.8.reduce_sub_computation | reduce | bytes 6148 | tf_op args[1]
  1.3 5.3 %shard_map.73 = bf16[8,336,128]{2,1,0:T(8,128)(2,1)} custom-call(s32[8]{0:T(128)} %query_counts_ref.1, s32[768]{0:T(1024)} %reduce.owner_ref, s32[768]{0:T(1024)} %page_ref.1, bf16[768,1536]{1,0:T(8,128)(2,1)} %rows_ref.1, bf16[1536,128]{1,0:T(8,128)(2,1)} %weight_ref.1, f32[1,128]{1,0:T(1,128)} %bitcast.3, bf16[256,128]{1,0:T(8,128)(2,1)} %bitcast.2), custom_call_target="tpu_custom_call" | custom-call | flops 603979776 | bytes 3440640 | tf_op jit(solution)/shard_map/pallas_call | solution.py:72
  6.6 7.3 %all-to-all-start = ((bf16[8,336,128]{2,1,0:T(8,128)(2,1)}), bf16[8,336,128]{2,1,0:T(8,128)(2,1)S(1)}, u32[]{:S(2)}, u32[]{:S(2)}) async-start(bf16[8,336,128]{2,1,0:T(8,128)(2,1)} %shard_map.73), calls=%async_computation | async-start | bytes 1376256 | tf_op jit(solution)/shard_map/all_to_all | solution.py:201
  13.9 18.0 %all-to-all-done.received_ref = bf16[8,336,128]{2,1,0:T(8,128)(2,1)S(1)} async-done(((bf16[8,336,128]{2,1,0:T(8,128)(2,1)}), bf16[8,336,128]{2,1,0:T(8,128)(2,1)S(1)}, u32[]{:S(2)}, u32[]{:S(2)}) %all-to-all-start) | async-done | bytes 688160 | tf_op jit(solution)/shard_map/all_to_all | solution.py:201
  31.9 0.0 copy-start
  31.9 0.1 reshape_squeeze.3
  32.0 0.1 dynamic-slice_reduce_fusion
  32.1 0.1 reshape.18
  32.2 2.3 %all_gather.3.tokens_ref = bf16[8,256,128]{2,1,0:T(8,128)(2,1)} all-gather(bf16[8,128,128]{2,1,0:T(8,128)(2,1)S(1)} %slice.14), channel_id=1, replica_groups=mesh['groups'=2,'blk'=8,'inner'=2] {'inner'}, dimensions={1}, use_global_device_ids=true | all-gather | bytes 786432 | tf_op jit(solution)/shard_map/all_gather | solution.py:202
  34.5 0.6 %maximum_convert_fusion.table_ref = s32[128]{0:T(128)} fusion(bf16[64]{0:T(256)(128)(2,1)S(1)} %reshape_squeeze.3, bf16[64]{0:T(256)(128)(2,1)S(1)} %reshape.18), kind=kLoop, calls=%fused_computation.2 | loop fusion | flops 512 | bytes 768 | tf_op jit(solution)/shard_map/convert_element_type | solution.py:209
  35.2 0.0 copy-done
  35.2 11.1 %shard_map.74 = f32[8,64]{1,0:T(8,128)} custom-call(s32[128]{0:T(128)} %maximum_convert_fusion.table_ref, bf16[8,336,128]{2,1,0:T(8,128)(2,1)} %copy-done, bf16[8,256,128]{2,1,0:T(8,128)(2,1)} %all_gather.3.tokens_ref), custom_call_target="tpu_custom_call" | custom-call | flops 1541406720 | bytes 1214464 | tf_op jit(solution)/shard_map/pallas_call | solution.py:170
  (3 shorter events, 0.1 us)
Async XLA Ops:
  6.6 25.3 %all-to-all-start = ((bf16[8,336,128]{2,1,0:T(8,128)(2,1)}), bf16[8,336,128]{2,1,0:T(8,128)(2,1)S(1)}, u32[]{:S(2)}, u32[]{:S(2)}) async-start(bf16[8,336,128]{2,1,0:T(8,128)(2,1)} %shard_map.73), calls=%async_computation | async-start | bytes 1376256 | tf_op jit(solution)/shard_map/all_to_all | solution.py:201
  31.9 3.3 %copy-start = (bf16[8,336,128]{2,1,0:T(8,128)(2,1)}, bf16[8,336,128]{2,1,0:T(8,128)(2,1)S(1)}, u32[]{:S(2)}) copy-start(bf16[8,336,128]{2,1,0:T(8,128)(2,1)S(1)} %all-to-all-done.received_ref) | copy-start | bytes 2064388

commit v8 on v5

--- a/solution.py
+++ b/solution.py
@@ -12,12 +12,23 @@
 
 
 def send_kernel(page_total, capacity, query_rows, block_at, query_counts_ref, owner_ref, page_ref, rows_ref, weight_ref,
-                bias_ref, queries_ref, message_ref):
-    owners = message_ref.shape[0]
-    rows = rows_ref.shape[0]
+                bias_ref, queries_ref, message_ref, local_ref):
+    step = pl.program_id(0)
+    row_block = rows_ref.shape[0]
     proj = jnp.dot(rows_ref[...], weight_ref[...], preferred_element_type=jnp.float32) + bias_ref[...]
     scale = lax.rsqrt(jnp.sum(proj * proj, axis=1, keepdims=True) + 1e-06)
-    local = (proj * scale).astype(jnp.bfloat16)
+    local_ref[pl.ds(pl.multiple_of(step * row_block, row_block), row_block), :] = (proj * scale).astype(jnp.bfloat16)
+
+    @pl.when(step == pl.num_programs(0) - 1)
+    def _():
+        send_layout(page_total, capacity, query_rows, block_at, query_counts_ref, owner_ref, page_ref, queries_ref,
+                    message_ref, local_ref[...])
+
+
+def send_layout(page_total, capacity, query_rows, block_at, query_counts_ref, owner_ref, page_ref, queries_ref,
+                message_ref, local):
+    owners = message_ref.shape[0]
+    rows = local.shape[0]
     combo = owner_ref[...].reshape(1, rows) * page_total + page_ref[...].reshape(1, rows)
     combos = -(-owners * page_total // 128) * 128
     combo_id = lax.broadcasted_iota(jnp.int32, (combos, rows), 0)
@@ -68,12 +79,24 @@
     per_block, token_slots, width = query_tokens.shape
     query_rows = per_block // halves * token_slots
     block_at = -(-(query_rows + capacity) // 16) * 16
-    vmem = pl.BlockSpec(memory_space=pltpu.VMEM)
+    row_block = 128 if rows % 128 == 0 else rows
+    message_rows = block_at + 16
+    whole = lambda *shape: pl.BlockSpec(shape, lambda i: (0,) * len(shape))
     return pl.pallas_call(
         functools.partial(send_kernel, PAGES_DEV, capacity, query_rows, block_at),
-        out_shape=jax.ShapeDtypeStruct((owners, block_at + 16, width), jnp.bfloat16),
-        in_specs=[pl.BlockSpec(memory_space=pltpu.SMEM)] + [vmem] * 6,
-        out_specs=vmem,
+        out_shape=jax.ShapeDtypeStruct((owners, message_rows, width), jnp.bfloat16),
+        grid=(rows // row_block,),
+        in_specs=[
+            pl.BlockSpec(memory_space=pltpu.SMEM),
+            whole(rows),
+            whole(rows),
+            pl.BlockSpec((row_block, features), lambda i: (i, 0)),
+            whole(features, width),
+            whole(1, width),
+            whole(per_block * token_slots, width),
+        ],
+        out_specs=whole(owners, message_rows, width),
+        scratch_shapes=[pltpu.VMEM((rows, width), jnp.bfloat16)],
         cost_estimate=pl.CostEstimate(
             flops=2 * rows * width * (features + owners * capacity),
             bytes_accessed=2 * (rows * features + features * width + owners * (block_at + 16) * width),

time: 43.7 us -> 45.4 us (1.039)
  Pallas kernels: 13.6 us -> 15 us
    pallas_call x1, Pallas kernels: 5.28 us -> 6.72 us  [send_message(): pl.pallas_call(functools.partial(send_kernel, PAGES_DEV, capacity, query_...]
where the time goes in v8:
time: 45.4 us; the launch traced here: 44.9 us
  waiting for transfers between devices  18 us (40%)
  Pallas kernels  15 us (33%)
  starting transfers between devices  7.31 us (16%)
  blocking collectives  2.31 us (5%)
  other arithmetic  1.9 us (4%)
    all_to_all x1, waiting for transfers between devices, shards(): lax.all_to_all(message, 'blk', split_axis=0, concat_axis=0, tiled=True)  18 us
    pallas_call x1, Pallas kernels, page_scores(): pl.pallas_call(functools.partial(score_kernel, page_total, token_slots, q...  8.31 us
    all_to_all x1, starting transfers between devices, shards(): lax.all_to_all(message, 'blk', split_axis=0, concat_axis=0, tiled=True)  7.31 us
    pallas_call x1, Pallas kernels, send_message(): pl.pallas_call(functools.partial(send_kernel, PAGES_DEV, capacity, query_...  6.72 us
    all_gather x1, blocking collectives, shards(): lax.all_gather(received[:, :query_rows], 'inner', axis=1, tiled=True)  2.31 us
    unnamed x1, other arithmetic  1.29 us
  transfers between devices with their start and end apart: 1, of which 1 were waited for; matrix products, arithmetic and copies ran while one was open for 0% of the time, Pallas kernels for 0%

profile of v8, /device:TPU:0, one launch (start us, length us, event | category | flops | bytes accessed | tf_op | source)
XLA Modules:
  0.0 44.9 jit_solution(1572947724892332080)
XLA Ops:
  0.0 1.3 %reduce.owner_ref = s32[768]{0:T(1024)} reduce(s32[768,1]{0,1:T(1,128)} %param.8, s32[]{:T(128)} %constant.3.clone.1), dimensions={1}, to_apply=%param.8.reduce_sub_computation | reduce | bytes 6148 | tf_op args[1]
  1.3 6.7 %shard_map.73 = bf16[8,336,128]{2,1,0:T(8,128)(2,1)} custom-call(s32[8]{0:T(128)} %query_counts_ref.1, s32[768]{0:T(1024)} %reduce.owner_ref, s32[768]{0:T(1024)} %page_ref.1, bf16[768,1536]{1,0:T(8,128)(2,1)} %rows_ref.1, bf16[1536,128]{1,0:T(8,128)(2,1)} %weight_ref.1, f32[1,128]{1,0:T(1,128)} %bitcast.3, bf16[256,128]{1,0:T(8,128)(2,1)} %bitcast.2), custom_call_target="tpu_custom_call" | custom-call | flops 603979776 | bytes 3440640 | tf_op jit(solution)/shard_map/pallas_call | solution.py:85
  8.0 7.3 %all-to-all-start = ((bf16[8,336,128]{2,1,0:T(8,128)(2,1)}), bf16[8,336,128]{2,1,0:T(8,128)(2,1)S(1)}, u32[]{:S(2)}, u32[]{:S(2)}) async-start(bf16[8,336,128]{2,1,0:T(8,128)(2,1)} %shard_map.73), calls=%async_computation | async-start | bytes 1376256 | tf_op jit(solution)/shard_map/all_to_all | solution.py:224
  15.3 18.0 %all-to-all-done.received_ref = bf16[8,336,128]{2,1,0:T(8,128)(2,1)S(1)} async-done(((bf16[8,336,128]{2,1,0:T(8,128)(2,1)}), bf16[8,336,128]{2,1,0:T(8,128)(2,1)S(1)}, u32[]{:S(2)}, u32[]{:S(2)}) %all-to-all-start) | async-done | bytes 688160 | tf_op jit(solution)/shard_map/all_to_all | solution.py:224
  33.3 0.0 copy-start
  33.3 0.1 reshape_squeeze.3
  33.4 0.1 dynamic-slice_reduce_fusion
  33.5 0.1 reshape.18
  33.7 2.3 %all_gather.3.tokens_ref = bf16[8,256,128]{2,1,0:T(8,128)(2,1)} all-gather(bf16[8,128,128]{2,1,0:T(8,128)(2,1)S(1)} %slice.14), channel_id=1, replica_groups=mesh['groups'=2,'blk'=8,'inner'=2] {'inner'}, dimensions={1}, use_global_device_ids=true | all-gather | bytes 786432 | tf_op jit(solution)/shard_map/all_gather | solution.py:225
  36.0 0.6 %maximum_convert_fusion.table_ref = s32[128]{0:T(128)} fusion(bf16[64]{0:T(256)(128)(2,1)S(1)} %reshape_squeeze.3, bf16[64]{0:T(256)(128)(2,1)S(1)} %reshape.18), kind=kLoop, calls=%fused_computation.2 | loop fusion | flops 512 | bytes 768 | tf_op jit(solution)/shard_map/convert_element_type | solution.py:232
  36.6 0.0 copy-done
  36.6 8.3 %shard_map.74 = f32[8,64]{1,0:T(8,128)} custom-call(s32[128]{0:T(128)} %maximum_convert_fusion.table_ref, bf16[8,336,128]{2,1,0:T(8,128)(2,1)} %copy-done, bf16[8,256,128]{2,1,0:T(8,128)(2,1)} %all_gather.3.tokens_ref), custom_call_target="tpu_custom_call" | custom-call | flops 1541406720 | bytes 1214464 | tf_op jit(solution)/shard_map/pallas_call | solution.py:193
  (3 shorter events, 0.1 us)
Async XLA Ops:
  8.0 25.3 %all-to-all-start = ((bf16[8,336,128]{2,1,0:T(8,128)(2,1)}), bf16[8,336,128]{2,1,0:T(8,128)(2,1)S(1)}, u32[]{:S(2)}, u32[]{:S(2)}) async-start(bf16[8,336,128]{2,1,0:T(8,128)(2,1)} %shard_map.73), calls=%async_computation | async-start | bytes 1376256 | tf_op jit(solution)/shard_map/all_to_all | solution.py:224
  33.3 3.3 %copy-start = (bf16[8,336,128]{2,1,0:T(8,128)(2,1)}, bf16[8,336,128]{2,1,0:T(8,128)(2,1)S(1)}, u32[]{:S(2)}) copy-start(bf16[8,336,128]{2,1,0:T(8,128)(2,1)S(1)} %all-to-all-done.received_ref) | copy-start | bytes 2064388

commit v9 on v5

--- a/solution.py
+++ b/solution.py
@@ -86,7 +86,7 @@
 
 
 def score_kernel(page_total, token_slots, query_rows, token_block, table_ref, received_ref, tokens_ref, out_ref,
-                 ordered_ref, sims_ref):
+                 ordered_ref, sims_ref, rows_ref):
     owners = received_ref.shape[0]
     ordered_rows, width = ordered_ref.shape
     capacity = (ordered_rows - 16 * page_total - 16) // owners
@@ -97,10 +97,9 @@
     for page in range(page_total):
         firsts.append(at)
         at = at + (totals[page] + 15) // 16 * 16
-    target = lax.broadcasted_iota(jnp.int32, (ordered_rows, capacity), 0)
     slot = lax.broadcasted_iota(jnp.int32, (1, capacity), 1)
-    ordered = jnp.zeros((ordered_rows, width), jnp.float32)
     before = [0] * page_total
+    positions = []
     for chunk in range(owners):
         position = jnp.full((1, capacity), -1, jnp.int32)
         low = 0
@@ -110,10 +109,11 @@
             position = jnp.where(inside, slot + (firsts[page] + before[page] - low), position)
             before[page] = before[page] + (high - low)
             low = high
-        place = (position == target).astype(jnp.bfloat16)
-        rows = received_ref[chunk, query_rows : query_rows + capacity, :]
-        ordered = ordered + jnp.dot(place, rows, preferred_element_type=jnp.float32)
-    ordered_ref[...] = ordered.astype(jnp.bfloat16)
+        positions.append(position)
+        rows_ref[chunk * capacity : (chunk + 1) * capacity, :] = received_ref[chunk, query_rows : query_rows + capacity, :]
+    position = jnp.concatenate(positions, axis=1)
+    place = (position == lax.broadcasted_iota(jnp.int32, (ordered_rows, owners * capacity), 0)).astype(jnp.bfloat16)
+    ordered_ref[...] = jnp.dot(place, rows_ref[...], preferred_element_type=jnp.float32).astype(jnp.bfloat16)
     sources = token_block // tokens_ref.shape[1]
     sub = lax.broadcasted_iota(jnp.int32, (8, token_block), 0)
     query_lane = lax.broadcasted_iota(jnp.int32, (1, total_queries), 1)
@@ -175,6 +175,7 @@
         scratch_shapes=[
             pltpu.VMEM((ordered_rows, width), jnp.bfloat16),
             pltpu.VMEM((ordered_rows, token_block), jnp.float32),
+            pltpu.VMEM((owners * capacity, width), jnp.bfloat16),
         ],
         cost_estimate=pl.CostEstimate(
             flops=2 * ordered_rows * width * (owners * capacity + token_total),

time: 43.7 us -> 43.8 us (level); the launches traced: 43.5 us -> 43.1 us
  no operation moved by 1% of the time
where the time goes in v9:
time: 43.8 us; the launch traced here: 43.1 us
  waiting for transfers between devices  18 us (41%)
  Pallas kernels  13.2 us (30%)
  starting transfers between devices  7.31 us (17%)
  blocking collectives  2.31 us (5%)
  other arithmetic  1.9 us (4%)
    all_to_all x1, waiting for transfers between devices, shards(): lax.all_to_all(message, 'blk', split_axis=0, concat_axis=0, tiled=True)  18 us
    pallas_call x1, Pallas kernels, page_scores(): pl.pallas_call(functools.partial(score_kernel, page_total, token_slots, q...  7.93 us
    all_to_all x1, starting transfers between devices, shards(): lax.all_to_all(message, 'blk', split_axis=0, concat_axis=0, tiled=True)  7.31 us
    pallas_call x1, Pallas kernels, send_message(): pl.pallas_call(functools.partial(send_kernel, PAGES_DEV, capacity, query_...  5.28 us
    all_gather x1, blocking collectives, shards(): lax.all_gather(received[:, :query_rows], 'inner', axis=1, tiled=True)  2.31 us
    unnamed x1, other arithmetic  1.29 us
  transfers between devices with their start and end apart: 1, of which 1 were waited for; matrix products, arithmetic and copies ran while one was open for 0% of the time, Pallas kernels for 0%

profile of v9, /device:TPU:0, one launch (start us, length us, event | category | flops | bytes accessed | tf_op | source)
XLA Modules:
  0.0 43.1 jit_solution(3309018392141304640)
XLA Ops:
  0.0 1.3 %reduce.owner_ref = s32[768]{0:T(1024)} reduce(s32[768,1]{0,1:T(1,128)} %param.8, s32[]{:T(128)} %constant.3.clone.1), dimensions={1}, to_apply=%param.8.reduce_sub_computation | reduce | bytes 6148 | tf_op args[1]
  1.3 5.3 %shard_map.73 = bf16[8,336,128]{2,1,0:T(8,128)(2,1)} custom-call(s32[8]{0:T(128)} %query_counts_ref.1, s32[768]{0:T(1024)} %reduce.owner_ref, s32[768]{0:T(1024)} %page_ref.1, bf16[768,1536]{1,0:T(8,128)(2,1)} %rows_ref.1, bf16[1536,128]{1,0:T(8,128)(2,1)} %weight_ref.1, f32[1,128]{1,0:T(1,128)} %bitcast.3, bf16[256,128]{1,0:T(8,128)(2,1)} %bitcast.2), custom_call_target="tpu_custom_call" | custom-call | flops 603979776 | bytes 3440640 | tf_op jit(solution)/shard_map/pallas_call | solution.py:72
  6.6 7.3 %all-to-all-start = ((bf16[8,336,128]{2,1,0:T(8,128)(2,1)}), bf16[8,336,128]{2,1,0:T(8,128)(2,1)S(1)}, u32[]{:S(2)}, u32[]{:S(2)}) async-start(bf16[8,336,128]{2,1,0:T(8,128)(2,1)} %shard_map.73), calls=%async_computation | async-start | bytes 1376256 | tf_op jit(solution)/shard_map/all_to_all | solution.py:202
  13.9 18.0 %all-to-all-done.received_ref = bf16[8,336,128]{2,1,0:T(8,128)(2,1)S(1)} async-done(((bf16[8,336,128]{2,1,0:T(8,128)(2,1)}), bf16[8,336,128]{2,1,0:T(8,128)(2,1)S(1)}, u32[]{:S(2)}, u32[]{:S(2)}) %all-to-all-start) | async-done | bytes 688160 | tf_op jit(solution)/shard_map/all_to_all | solution.py:202
  31.9 0.0 copy-start
  31.9 0.1 reshape_squeeze.3
  32.0 0.1 dynamic-slice_reduce_fusion
  32.1 0.1 reshape.18
  32.2 2.3 %all_gather.3.tokens_ref = bf16[8,256,128]{2,1,0:T(8,128)(2,1)} all-gather(bf16[8,128,128]{2,1,0:T(8,128)(2,1)S(1)} %slice.14), channel_id=1, replica_groups=mesh['groups'=2,'blk'=8,'inner'=2] {'inner'}, dimensions={1}, use_global_device_ids=true | all-gather | bytes 786432 | tf_op jit(solution)/shard_map/all_gather | solution.py:203
  34.5 0.6 %maximum_convert_fusion.table_ref = s32[128]{0:T(128)} fusion(bf16[64]{0:T(256)(128)(2,1)S(1)} %reshape_squeeze.3, bf16[64]{0:T(256)(128)(2,1)S(1)} %reshape.18), kind=kLoop, calls=%fused_computation.2 | loop fusion | flops 512 | bytes 768 | tf_op jit(solution)/shard_map/convert_element_type | solution.py:210
  35.2 0.0 copy-done
  35.2 7.9 %shard_map.74 = f32[8,64]{1,0:T(8,128)} custom-call(s32[128]{0:T(128)} %maximum_convert_fusion.table_ref, bf16[8,336,128]{2,1,0:T(8,128)(2,1)} %copy-done, bf16[8,256,128]{2,1,0:T(8,128)(2,1)} %all_gather.3.tokens_ref), custom_call_target="tpu_custom_call" | custom-call | flops 1541406720 | bytes 1214464 | tf_op jit(solution)/shard_map/pallas_call | solution.py:170
  (3 shorter events, 0.1 us)
Async XLA Ops:
  6.6 25.3 %all-to-all-start = ((bf16[8,336,128]{2,1,0:T(8,128)(2,1)}), bf16[8,336,128]{2,1,0:T(8,128)(2,1)S(1)}, u32[]{:S(2)}, u32[]{:S(2)}) async-start(bf16[8,336,128]{2,1,0:T(8,128)(2,1)} %shard_map.73), calls=%async_computation | async-start | bytes 1376256 | tf_op jit(solution)/shard_map/all_to_all | solution.py:202
  31.9 3.3 %copy-start = (bf16[8,336,128]{2,1,0:T(8,128)(2,1)}, bf16[8,336,128]{2,1,0:T(8,128)(2,1)S(1)}, u32[]{:S(2)}) copy-start(bf16[8,336,128]{2,1,0:T(8,128)(2,1)S(1)} %all-to-all-done.received_ref) | copy-start | bytes 2064388

commit v10 on v9

--- a/solution.py
+++ b/solution.py
@@ -80,7 +80,7 @@
             transcendentals=rows,
         ),
     )(
-        query_counts, owner_ids.reshape(rows), page_ids, patch_rows, proj_weight, proj_bias.reshape(1, width),
+        query_counts, owner_ids.reshape(1, rows), page_ids, patch_rows, proj_weight, proj_bias.reshape(1, width),
         query_tokens.reshape(per_block * token_slots, width),
     )
 

time: 43.8 us -> 42.7 us (0.975)
  other arithmetic: 1.9 us -> 0.62 us
    unnamed x1 -> x0, other arithmetic: 1.29 us -> none
where the time goes in v10:
time: 42.7 us; the launch traced here: 42 us
  waiting for transfers between devices  18 us (42%)
  Pallas kernels  13.4 us (31%)
  starting transfers between devices  7.31 us (17%)
  blocking collectives  2.31 us (5%)
  other arithmetic  0.62 us (1%)
    all_to_all x1, waiting for transfers between devices, shards(): lax.all_to_all(message, 'blk', split_axis=0, concat_axis=0, tiled=True)  18 us
    pallas_call x1, Pallas kernels, page_scores(): pl.pallas_call(functools.partial(score_kernel, page_total, token_slots, q...  8.15 us
    all_to_all x1, starting transfers between devices, shards(): lax.all_to_all(message, 'blk', split_axis=0, concat_axis=0, tiled=True)  7.31 us
    pallas_call x1, Pallas kernels, send_message(): pl.pallas_call(functools.partial(send_kernel, PAGES_DEV, capacity, query_...  5.28 us
    all_gather x1, blocking collectives, shards(): lax.all_gather(received[:, :query_rows], 'inner', axis=1, tiled=True)  2.31 us
  transfers between devices with their start and end apart: 1, of which 1 were waited for; matrix products, arithmetic and copies ran while one was open for 0% of the time, Pallas kernels for 0%

profile of v10, /device:TPU:0, one launch (start us, length us, event | category | flops | bytes accessed | tf_op | source)
XLA Modules:
  0.0 42.0 jit_solution(17884468274883777180)
XLA Ops:
  0.0 5.3 %shard_map.73 = bf16[8,336,128]{2,1,0:T(8,128)(2,1)} custom-call(s32[8]{0:T(128)} %query_counts_ref.1, s32[1,768]{1,0:T(1,128)} %bitcast.4, s32[768]{0:T(1024)} %page_ref.1, bf16[768,1536]{1,0:T(8,128)(2,1)} %rows_ref.1, bf16[1536,128]{1,0:T(8,128)(2,1)} %weight_ref.1, f32[1,128]{1,0:T(1,128)} %bitcast.5, bf16[256,128]{1,0:T(8,128)(2,1)} %bitcast.3), custom_call_target="tpu_custom_call" | custom-call | flops 603979776 | bytes 3440640 | tf_op jit(solution)/shard_map/pallas_call | solution.py:72
  5.3 7.3 %all-to-all-start = ((bf16[8,336,128]{2,1,0:T(8,128)(2,1)}), bf16[8,336,128]{2,1,0:T(8,128)(2,1)S(1)}, u32[]{:S(2)}, u32[]{:S(2)}) async-start(bf16[8,336,128]{2,1,0:T(8,128)(2,1)} %shard_map.73), calls=%async_computation | async-start | bytes 1376256 | tf_op jit(solution)/shard_map/all_to_all | solution.py:202
  12.6 18.0 %all-to-all-done.received_ref = bf16[8,336,128]{2,1,0:T(8,128)(2,1)S(1)} async-done(((bf16[8,336,128]{2,1,0:T(8,128)(2,1)}), bf16[8,336,128]{2,1,0:T(8,128)(2,1)S(1)}, u32[]{:S(2)}, u32[]{:S(2)}) %all-to-all-start) | async-done | bytes 688160 | tf_op jit(solution)/shard_map/all_to_all | solution.py:202
  30.6 0.0 copy-start
  30.6 0.1 reshape_squeeze.3
  30.7 0.1 dynamic-slice_reduce_fusion
  30.8 0.1 reshape.18
  30.9 2.3 %all_gather.3.tokens_ref = bf16[8,256,128]{2,1,0:T(8,128)(2,1)} all-gather(bf16[8,128,128]{2,1,0:T(8,128)(2,1)S(1)} %slice.14), channel_id=1, replica_groups=mesh['groups'=2,'blk'=8,'inner'=2] {'inner'}, dimensions={1}, use_global_device_ids=true | all-gather | bytes 786432 | tf_op jit(solution)/shard_map/all_gather | solution.py:203
  33.3 0.6 %maximum_convert_fusion.table_ref = s32[128]{0:T(128)} fusion(bf16[64]{0:T(256)(128)(2,1)S(1)} %reshape_squeeze.3, bf16[64]{0:T(256)(128)(2,1)S(1)} %reshape.18), kind=kLoop, calls=%fused_computation.2 | loop fusion | flops 512 | bytes 768 | tf_op jit(solution)/shard_map/convert_element_type | solution.py:210
  33.9 0.0 copy-done
  33.9 8.1 %shard_map.74 = f32[8,64]{1,0:T(8,128)} custom-call(s32[128]{0:T(128)} %maximum_convert_fusion.table_ref, bf16[8,336,128]{2,1,0:T(8,128)(2,1)} %copy-done, bf16[8,256,128]{2,1,0:T(8,128)(2,1)} %all_gather.3.tokens_ref), custom_call_target="tpu_custom_call" | custom-call | flops 1541406720 | bytes 1214464 | tf_op jit(solution)/shard_map/pallas_call | solution.py:170
  (3 shorter events, 0.1 us)
Async XLA Ops:
  5.3 25.3 %all-to-all-start = ((bf16[8,336,128]{2,1,0:T(8,128)(2,1)}), bf16[8,336,128]{2,1,0:T(8,128)(2,1)S(1)}, u32[]{:S(2)}, u32[]{:S(2)}) async-start(bf16[8,336,128]{2,1,0:T(8,128)(2,1)} %shard_map.73), calls=%async_computation | async-start | bytes 1376256 | tf_op jit(solution)/shard_map/all_to_all | solution.py:202
  30.6 3.3 %copy-start = (bf16[8,336,128]{2,1,0:T(8,128)(2,1)}, bf16[8,336,128]{2,1,0:T(8,128)(2,1)S(1)}, u32[]{:S(2)}) copy-start(bf16[8,336,128]{2,1,0:T(8,128)(2,1)S(1)} %all-to-all-done.received_ref) | copy-start | bytes 2064388

commit v11 on v10

--- a/solution.py
+++ b/solution.py
@@ -85,12 +85,30 @@
     )
 
 
-def score_kernel(page_total, token_slots, query_rows, token_block, table_ref, received_ref, tokens_ref, out_ref,
-                 ordered_ref, sims_ref, rows_ref):
+def score_kernel(page_total, token_slots, query_rows, token_block, block_at, received_ref, tokens_ref, out_ref,
+                 ordered_ref, sims_ref, rows_ref, counts_vmem, counts_smem, copy_sem):
     owners = received_ref.shape[0]
     ordered_rows, width = ordered_ref.shape
     capacity = (ordered_rows - 16 * page_total - 16) // owners
     total_queries = out_ref.shape[1]
+    per_block = total_queries // owners
+    count_rows = counts_vmem.shape[1] - 1
+    counts_vmem[...] = received_ref[:, block_at : block_at + count_rows + 1, :].astype(jnp.float32).astype(jnp.int32)
+    copy = pltpu.make_async_copy(counts_vmem, counts_smem, copy_sem)
+    copy.start()
+    copy.wait()
+    mine = lax.axis_index("blk") * page_total
+
+    class Table:
+        def __getitem__(self, index):
+            chunk, rest = divmod(index, page_total)
+            if chunk < owners:
+                lane = mine + rest
+                return counts_smem[chunk, lane // 128, lane % 128]
+            query = index - owners * page_total
+            return counts_smem[query // per_block, count_rows, query % per_block]
+
+    table_ref = Table()
     totals = [sum(table_ref[chunk * page_total + page] for chunk in range(owners)) for page in range(page_total)]
     firsts = []
     at = 0
@@ -160,7 +178,7 @@
     )
 
 
-def page_scores(received, tokens, table, total_queries, page_total, token_slots, query_rows, capacity):
+def page_scores(received, tokens, total_queries, page_total, token_slots, query_rows, capacity, block_at, count_rows):
     owners = received.shape[0]
     width = received.shape[2]
     ordered_rows = owners * capacity + 16 * page_total + 16
@@ -168,21 +186,24 @@
     token_block = min(token_total, 1024)
     vmem = pl.BlockSpec(memory_space=pltpu.VMEM)
     return pl.pallas_call(
-        functools.partial(score_kernel, page_total, token_slots, query_rows, token_block),
+        functools.partial(score_kernel, page_total, token_slots, query_rows, token_block, block_at),
         out_shape=jax.ShapeDtypeStruct((page_total, total_queries), jnp.float32),
-        in_specs=[pl.BlockSpec(memory_space=pltpu.SMEM), vmem, vmem],
+        in_specs=[vmem, vmem],
         out_specs=vmem,
         scratch_shapes=[
             pltpu.VMEM((ordered_rows, width), jnp.bfloat16),
             pltpu.VMEM((ordered_rows, token_block), jnp.float32),
             pltpu.VMEM((owners * capacity, width), jnp.bfloat16),
+            pltpu.VMEM((owners, count_rows + 1, width), jnp.int32),
+            pltpu.SMEM((owners, count_rows + 1, width), jnp.int32),
+            pltpu.SemaphoreType.DMA,
         ],
         cost_estimate=pl.CostEstimate(
             flops=2 * ordered_rows * width * (owners * capacity + token_total),
             bytes_accessed=2 * received.size + 2 * tokens.size + 4 * page_total * total_queries,
             transcendentals=0,
         ),
-    )(table, received, tokens)
+    )(received, tokens)
 
 
 def shards(patch_rows, owner_ids, page_ids, proj_weight, proj_bias, query_tokens, query_counts):
@@ -204,11 +225,9 @@
     block_at = -(-(query_rows + capacity) // 16) * 16
     combos = -(-owners * PAGES_DEV // 128) * 128
     count_rows = combos // 128
-    page_counts = received[:, block_at : block_at + count_rows].reshape(owners, combos)
-    page_counts = lax.dynamic_slice_in_dim(page_counts, lax.axis_index("blk") * PAGES_DEV, PAGES_DEV, axis=1)
-    counts = received[:, block_at + count_rows, :per_block]
-    table = jnp.concatenate([page_counts.reshape(owners * PAGES_DEV), counts.reshape(total_queries)]).astype(jnp.int32)
-    return page_scores(received, halves_in, table, total_queries, PAGES_DEV, token_slots, query_rows, capacity)
+    return page_scores(
+        received, halves_in, total_queries, PAGES_DEV, token_slots, query_rows, capacity, block_at, count_rows
+    )
 
 
 def solution(mesh):

time: 42.7 us -> 42.6 us (level)
  blocking collectives: 2.31 us -> 27.9 us
  waiting for transfers between devices: 18 us -> 0 us
  starting transfers between devices: 7.31 us -> 0 us
  other arithmetic: 0.62 us -> 0 us
  Pallas kernels: 13.4 us -> 14 us
    all_to_all x0 -> x1, blocking collectives: none -> 25.5 us  [shards(): lax.all_to_all(message, 'blk', split_axis=0, concat_axis=0, tiled=True)]
    all_to_all x1 -> x0, waiting for transfers between devices: 18 us -> none  [shards(): lax.all_to_all(message, 'blk', split_axis=0, concat_axis=0, tiled=True)]
    all_to_all x1 -> x0, starting transfers between devices: 7.31 us -> none  [shards(): lax.all_to_all(message, 'blk', split_axis=0, concat_axis=0, tiled=True)]
    convert_element_type x1 -> x0, other arithmetic: 0.62 us -> none  [shards(): jnp.concatenate([page_counts.reshape(owners * PAGES_DEV), counts.reshape(...]
    pallas_call x1, Pallas kernels: 8.15 us -> 8.73 us  [page_scores(): pl.pallas_call(functools.partial(score_kernel, page_total, token_slots, q...]
  transfers between devices with their start and end apart: 1 -> 0, of which waited for: 1 -> 0; matrix products, arithmetic and copies ran while one was open for 0% -> 0% of each run, Pallas kernels for 0% -> 0%
where the time goes in v11:
time: 42.6 us; the launch traced here: 41.9 us
  blocking collectives  27.9 us (65%)
  Pallas kernels  14 us (33%)
    all_to_all x1, blocking collectives, shards(): lax.all_to_all(message, 'blk', split_axis=0, concat_axis=0, tiled=True)  25.5 us
    pallas_call x1, Pallas kernels, page_scores(): pl.pallas_call(functools.partial(score_kernel, page_total, token_slots, q...  8.73 us
    pallas_call x1, Pallas kernels, send_message(): pl.pallas_call(functools.partial(send_kernel, PAGES_DEV, capacity, query_...  5.28 us
    all_gather x1, blocking collectives, shards(): lax.all_gather(received[:, :query_rows], 'inner', axis=1, tiled=True)  2.31 us

profile of v11, /device:TPU:0, one launch (start us, length us, event | category | flops | bytes accessed | tf_op | source)
XLA Modules:
  0.0 41.9 jit_solution(37517278985391903)
XLA Ops:
  0.0 5.3 %shard_map.73 = bf16[8,336,128]{2,1,0:T(8,128)(2,1)} custom-call(s32[8]{0:T(128)} %query_counts_ref.1, s32[1,768]{1,0:T(1,128)} %bitcast.4, s32[768]{0:T(1024)} %page_ref.1, bf16[768,1536]{1,0:T(8,128)(2,1)} %rows_ref.1, bf16[1536,128]{1,0:T(8,128)(2,1)} %weight_ref.1, f32[1,128]{1,0:T(1,128)} %bitcast.5, bf16[256,128]{1,0:T(8,128)(2,1)} %bitcast.3), custom_call_target="tpu_custom_call" | custom-call | flops 603979776 | bytes 3440640 | tf_op jit(solution)/shard_map/pallas_call | solution.py:72
  5.3 25.5 %all_to_all.5.received_ref = bf16[8,336,128]{2,1,0:T(8,128)(2,1)S(1)} all-to-all(bf16[8,336,128]{2,1,0:T(8,128)(2,1)} %shard_map.73), channel_id=1, replica_groups=mesh['groups'=2,'blk'=8,'inner'=2] {'blk'}, dimensions={0} | all-to-all | bytes 1376256 | tf_op jit(solution)/shard_map/all_to_all | solution.py:223
  30.8 0.0 copy-start
  30.9 2.3 %all_gather.3.tokens_ref = bf16[8,256,128]{2,1,0:T(8,128)(2,1)} all-gather(bf16[8,128,128]{2,1,0:T(8,128)(2,1)S(1)} %slice.4), channel_id=1, replica_groups=mesh['groups'=2,'blk'=8,'inner'=2] {'inner'}, dimensions={1}, use_global_device_ids=true | all-gather | bytes 786432 | tf_op jit(solution)/shard_map/all_gather | solution.py:224
  33.2 0.0 copy-done
  33.2 8.7 %shard_map.74 = f32[8,64]{1,0:T(8,128)} custom-call(bf16[8,336,128]{2,1,0:T(8,128)(2,1)} %copy-done, bf16[8,256,128]{2,1,0:T(8,128)(2,1)} %all_gather.3.tokens_ref), custom_call_target="tpu_custom_call" | custom-call | flops 1541406720 | bytes 1214464 | tf_op jit(solution)/shard_map/pallas_call | solution.py:188
  (1 shorter events, 0.0 us)
Async XLA Ops:
  30.8 2.3 %copy-start = (bf16[8,336,128]{2,1,0:T(8,128)(2,1)}, bf16[8,336,128]{2,1,0:T(8,128)(2,1)S(1)}, u32[]{:S(2)}) copy-start(bf16[8,336,128]{2,1,0:T(8,128)(2,1)S(1)} %all_to_all.5.received_ref) | copy-start | bytes 2064388

commit v12 on v6

--- a/solution.py
+++ b/solution.py
@@ -80,7 +80,7 @@
             transcendentals=rows,
         ),
     )(
-        query_counts, owner_ids.reshape(rows), page_ids, patch_rows, proj_weight, proj_bias.reshape(1, width),
+        query_counts, owner_ids.reshape(1, rows), page_ids, patch_rows, proj_weight, proj_bias.reshape(1, width),
         query_tokens.reshape(per_block * token_slots, width),
     )
 
@@ -147,16 +147,21 @@
     return lax.fori_loop(0, blocks, block_scores, jnp.zeros((page_total, total_queries), jnp.float32))
 
 
-def first_kernel(page_total, token_slots, per_block, query_rows, table_ref, received_ref, out_ref, ordered_ref,
-                 sims_ref):
+def score_kernel(page_total, token_slots, query_rows, table_ref, received_ref, partner_ref, out_ref, ordered_ref,
+                 sims_ref, rows_ref):
     owners = received_ref.shape[0]
     ordered_rows, width = ordered_ref.shape
     capacity = (ordered_rows - 16 * page_total - 16) // owners
-    totals, firsts = page_runs(table_ref, owners, page_total)
-    target = lax.broadcasted_iota(jnp.int32, (ordered_rows, capacity), 0)
+    total_queries = out_ref.shape[1]
+    totals = [sum(table_ref[chunk * page_total + page] for chunk in range(owners)) for page in range(page_total)]
+    firsts = []
+    at = 0
+    for page in range(page_total):
+        firsts.append(at)
+        at = at + (totals[page] + 15) // 16 * 16
     slot = lax.broadcasted_iota(jnp.int32, (1, capacity), 1)
-    ordered = jnp.zeros((ordered_rows, width), jnp.float32)
     before = [0] * page_total
+    positions = []
     for chunk in range(owners):
         position = jnp.full((1, capacity), -1, jnp.int32)
         low = 0
@@ -166,61 +171,43 @@
             position = jnp.where(inside, slot + (firsts[page] + before[page] - low), position)
             before[page] = before[page] + (high - low)
             low = high
-        place = (position == target).astype(jnp.bfloat16)
-        rows = received_ref[chunk, query_rows : query_rows + capacity, :]
-        ordered = ordered + jnp.dot(place, rows, preferred_element_type=jnp.float32)
-    ordered_ref[...] = ordered.astype(jnp.bfloat16)
+        positions.append(position)
+        rows_ref[chunk * capacity : (chunk + 1) * capacity, :] = received_ref[chunk, query_rows : query_rows + capacity, :]
+    position = jnp.concatenate(positions, axis=1)
+    place = (position == lax.broadcasted_iota(jnp.int32, (ordered_rows, owners * capacity), 0)).astype(jnp.bfloat16)
+    ordered_ref[...] = jnp.dot(place, rows_ref[...], preferred_element_type=jnp.float32).astype(jnp.bfloat16)
+    inner = lax.axis_index("inner")
     out_ref[...] = half_scores(
-        table_ref, ordered_ref, sims_ref, received_ref.at[:, 0:query_rows, :], lax.axis_index("inner"), owners,
-        page_total, token_slots, per_block, out_ref.shape[1],
-    )
-
-
-def second_kernel(page_total, token_slots, per_block, table_ref, ordered_ref, partner_ref, partial_ref, out_ref,
-                  sims_ref):
-    owners = partner_ref.shape[0]
-    out_ref[...] = partial_ref[...] + half_scores(
-        table_ref, ordered_ref, sims_ref, partner_ref, 1 - lax.axis_index("inner"), owners, page_total, token_slots,
-        per_block, out_ref.shape[1],
-    )
-
-
-def page_scores(received, table, total_queries, page_total, token_slots, per_block, query_rows, capacity):
+        table_ref, ordered_ref, sims_ref, received_ref.at[:, 0:query_rows, :], inner, owners, page_total, token_slots,
+        total_queries // owners, total_queries,
+    ) + half_scores(
+        table_ref, ordered_ref, sims_ref, partner_ref, 1 - inner, owners, page_total, token_slots,
+        total_queries // owners, total_queries,
+    )
+
+
+def page_scores(received, tokens, table, total_queries, page_total, token_slots, query_rows, capacity):
     owners = received.shape[0]
     width = received.shape[2]
     ordered_rows = owners * capacity + 16 * page_total + 16
     token_block = min(owners * query_rows, 1024)
     vmem = pl.BlockSpec(memory_space=pltpu.VMEM)
-    smem = pl.BlockSpec(memory_space=pltpu.SMEM)
-    partner = lax.ppermute(received[:, :query_rows], "inner", [(0, 1), (1, 0)])
-    half_flops = 2 * ordered_rows * width * owners * query_rows
-    partial, ordered = pl.pallas_call(
-        functools.partial(first_kernel, page_total, token_slots, per_block, query_rows),
-        out_shape=(
-            jax.ShapeDtypeStruct((page_total, total_queries), jnp.float32),
-            jax.ShapeDtypeStruct((ordered_rows, width), jnp.bfloat16),
-        ),
-        in_specs=[smem, vmem],
-        out_specs=(vmem, vmem),
-        scratch_shapes=[pltpu.VMEM((ordered_rows, token_block), jnp.float32)],
+    return pl.pallas_call(
+        functools.partial(score_kernel, page_total, token_slots, query_rows),
+        out_shape=jax.ShapeDtypeStruct((page_total, total_queries), jnp.float32),
+        in_specs=[pl.BlockSpec(memory_space=pltpu.SMEM), vmem, vmem],
+        out_specs=vmem,
+        scratch_shapes=[
+            pltpu.VMEM((ordered_rows, width), jnp.bfloat16),
+            pltpu.VMEM((ordered_rows, token_block), jnp.float32),
+            pltpu.VMEM((owners * capacity, width), jnp.bfloat16),
+        ],
         cost_estimate=pl.CostEstimate(
-            flops=2 * ordered_rows * width * owners * capacity + half_flops,
-            bytes_accessed=2 * received.size + 2 * ordered_rows * width + 4 * page_total * total_queries,
+            flops=2 * ordered_rows * width * owners * (capacity + 2 * query_rows),
+            bytes_accessed=2 * received.size + 2 * tokens.size + 4 * page_total * total_queries,
             transcendentals=0,
         ),
-    )(table, received)
-    return pl.pallas_call(
-        functools.partial(second_kernel, page_total, token_slots, per_block),
-        out_shape=jax.ShapeDtypeStruct((page_total, total_queries), jnp.float32),
-        in_specs=[smem, vmem, vmem, vmem],
-        out_specs=vmem,
-        scratch_shapes=[pltpu.VMEM((ordered_rows, token_block), jnp.float32)],
-        cost_estimate=pl.CostEstimate(
-            flops=half_flops,
-            bytes_accessed=2 * ordered_rows * width + 2 * partner.size + 8 * page_total * total_queries,
-            transcendentals=0,
-        ),
-    )(table, ordered, partner, partial)
+    )(table, received, tokens)
 
 
 def shards(patch_rows, owner_ids, page_ids, proj_weight, proj_bias, query_tokens, query_counts):
@@ -238,6 +225,7 @@
         patch_rows, owner_ids, page_ids, proj_weight, proj_bias, query_tokens, query_counts, owners, capacity, halves
     )
     received = lax.all_to_all(message, "blk", split_axis=0, concat_axis=0, tiled=True)
+    partner = lax.ppermute(received[:, :query_rows], "inner", [(0, 1), (1, 0)])
     block_at = -(-(query_rows + capacity) // 16) * 16
     combos = -(-owners * PAGES_DEV // 128) * 128
     count_rows = combos // 128
@@ -245,7 +233,7 @@
     page_counts = lax.dynamic_slice_in_dim(page_counts, lax.axis_index("blk") * PAGES_DEV, PAGES_DEV, axis=1)
     counts = received[:, block_at + count_rows, :per_block]
     table = jnp.concatenate([page_counts.reshape(owners * PAGES_DEV), counts.reshape(total_queries)]).astype(jnp.int32)
-    return page_scores(received, table, total_queries, PAGES_DEV, token_slots, per_block, query_rows, capacity)
+    return page_scores(received, partner, table, total_queries, PAGES_DEV, token_slots, query_rows, capacity)
 
 
 def solution(mesh):

time: 45.5 us -> 43.9 us (0.965)
  blocking collectives: 0 us -> 25.5 us
  waiting for transfers between devices: 18 us -> 0.55 us
  starting transfers between devices: 7.38 us -> 0.07 us
  Pallas kernels: 16.9 us -> 15.6 us
  other arithmetic: 1.95 us -> 0.66 us
    all_to_all x0 -> x1, blocking collectives: none -> 25.5 us  [shards(): lax.all_to_all(message, 'blk', split_axis=0, concat_axis=0, tiled=True)]
    all_to_all x1 -> x0, waiting for transfers between devices: 18 us -> none  [shards(): lax.all_to_all(message, 'blk', split_axis=0, concat_axis=0, tiled=True)]
    all_to_all x1 -> x0, starting transfers between devices: 7.31 us -> none  [shards(): lax.all_to_all(message, 'blk', split_axis=0, concat_axis=0, tiled=True)]
    unnamed x1 -> x0, other arithmetic: 1.29 us -> none
    pallas_call x2 -> x1, Pallas kernels: 11.6 us -> 10.3 us  [page_scores(): pl.pallas_call(functools.partial(score_kernel, page_total, token_slots, q...]
    ppermute x1, waiting for transfers between devices: 0.01 us -> 0.55 us  [shards(): partner = lax.ppermute(received[:, :query_rows], 'inner', [(0, 1), (1, 0)])]
  transfers between devices with their start and end apart: 2 -> 1, of which waited for: 1 -> 1; matrix products, arithmetic and copies ran while one was open for 2% -> 2% of each run, Pallas kernels for 17% -> 0%
where the time goes in v12:
time: 43.9 us; the launch traced here: 43.5 us
  blocking collectives  25.5 us (58%)
  Pallas kernels  15.6 us (36%)
  local copies, waits for them, and re-layouts  1.03 us (2%)
  other arithmetic  0.66 us (2%)
  waiting for transfers between devices  0.55 us (1%)
    all_to_all x1, blocking collectives, shards(): lax.all_to_all(message, 'blk', split_axis=0, concat_axis=0, tiled=True)  25.5 us
    pallas_call x1, Pallas kernels, page_scores(): pl.pallas_call(functools.partial(score_kernel, page_total, token_slots, q...  10.3 us
    pallas_call x1, Pallas kernels, send_message(): pl.pallas_call(functools.partial(send_kernel, PAGES_DEV, capacity, query_...  5.28 us
  transfers between devices with their start and end apart: 1, of which 1 were waited for; matrix products, arithmetic and copies ran while one was open for 2% of the time, Pallas kernels for 0%

profile of v12, /device:TPU:0, one launch (start us, length us, event | category | flops | bytes accessed | tf_op | source)
XLA Modules:
  0.0 43.5 jit_solution(9055861022769480745)
XLA Ops:
  0.0 5.3 %shard_map.73 = bf16[8,336,128]{2,1,0:T(8,128)(2,1)} custom-call(s32[8]{0:T(128)} %query_counts_ref.1, s32[1,768]{1,0:T(1,128)} %bitcast.4, s32[768]{0:T(1024)} %page_ref.1, bf16[768,1536]{1,0:T(8,128)(2,1)} %rows_ref.1, bf16[1536,128]{1,0:T(8,128)(2,1)} %weight_ref.1, f32[1,128]{1,0:T(1,128)} %bitcast.5, bf16[256,128]{1,0:T(8,128)(2,1)} %bitcast.3), custom_call_target="tpu_custom_call" | custom-call | flops 603979776 | bytes 3440640 | tf_op jit(solution)/shard_map/pallas_call | solution.py:72
  5.3 25.5 %all_to_all.5.received_ref = bf16[8,336,128]{2,1,0:T(8,128)(2,1)S(1)} all-to-all(bf16[8,336,128]{2,1,0:T(8,128)(2,1)} %shard_map.73), channel_id=1, replica_groups=mesh['groups'=2,'blk'=8,'inner'=2] {'blk'}, dimensions={0} | all-to-all | bytes 1376256 | tf_op jit(solution)/shard_map/all_to_all | solution.py:227
  30.8 0.0 copy-start
  30.9 0.1 collective-permute-start
  31.0 0.1 reshape_squeeze.3
  31.1 0.1 dynamic-slice_reduce_fusion
  31.2 0.1 reshape.18
  31.2 0.7 %maximum_convert_fusion.table_ref = s32[128]{0:T(128)} fusion(bf16[64]{0:T(256)(128)(2,1)S(1)} %reshape_squeeze.3, bf16[64]{0:T(256)(128)(2,1)S(1)} %reshape.18), kind=kLoop, calls=%fused_computation.2 | loop fusion | flops 512 | bytes 768 | tf_op jit(solution)/shard_map/convert_element_type | solution.py:235
  31.9 0.5 %collective-permute-done.partner_ref = bf16[8,128,128]{2,1,0:T(8,128)(2,1)S(1)} collective-permute-done((bf16[8,128,128]{2,1,0:T(8,128)(2,1)S(1)}, bf16[8,128,128]{2,1,0:T(8,128)(2,1)S(1)}, u32[]{:S(2)}, u32[]{:S(2)}) %collective-permute-start) | collective-permute-done | bytes 262176 | tf_op jit(solution)/shard_map/ppermute | solution.py:228
  32.5 0.0 copy-done
  32.5 0.0 copy-start.1
  32.5 0.7 %copy-done.1 = bf16[8,128,128]{2,1,0:T(8,128)(2,1)} copy-done((bf16[8,128,128]{2,1,0:T(8,128)(2,1)}, bf16[8,128,128]{2,1,0:T(8,128)(2,1)S(1)}, u32[]{:S(2)}) %copy-start.1) | copy-done | bytes 262168
  33.2 10.3 %shard_map.74 = f32[8,64]{1,0:T(8,128)} custom-call(s32[128]{0:T(128)} %maximum_convert_fusion.table_ref, bf16[8,336,128]{2,1,0:T(8,128)(2,1)} %copy-done, bf16[8,128,128]{2,1,0:T(8,128)(2,1)} %copy-done.1), custom_call_target="tpu_custom_call" | custom-call | flops 1541406720 | bytes 952320 | tf_op jit(solution)/shard_map/pallas_call | solution.py:195
  (3 shorter events, 0.1 us)
Async XLA Ops:
  30.8 1.6 %copy-start = (bf16[8,336,128]{2,1,0:T(8,128)(2,1)}, bf16[8,336,128]{2,1,0:T(8,128)(2,1)S(1)}, u32[]{:S(2)}) copy-start(bf16[8,336,128]{2,1,0:T(8,128)(2,1)S(1)} %all_to_all.5.received_ref) | copy-start | bytes 2064388
  30.9 1.6 %collective-permute-start = (bf16[8,128,128]{2,1,0:T(8,128)(2,1)S(1)}, bf16[8,128,128]{2,1,0:T(8,128)(2,1)S(1)}, u32[]{:S(2)}, u32[]{:S(2)}) collective-permute-start(bf16[8,128,128]{2,1,0:T(8,128)(2,1)S(1)} %slice.14), channel_id=1, source_target_pairs={{0,1},{1,0},{2,3},{3,2},{4,5},{5,4},{6,7},{7,6},{8,9},{9,8},{10,11... | collective-permute-start | bytes 786440 | tf_op jit(solution)/shard_map/ppermute | solution.py:228
  32.5 0.7 %copy-start.1 = (bf16[8,128,128]{2,1,0:T(8,128)(2,1)}, bf16[8,128,128]{2,1,0:T(8,128)(2,1)S(1)}, u32[]{:S(2)}) copy-start(bf16[8,128,128]{2,1,0:T(8,128)(2,1)S(1)} %collective-permute-done.partner_ref) | copy-start | bytes 786436

commit v13 on v10

--- a/solution.py
+++ b/solution.py
@@ -85,8 +85,8 @@
     )
 
 
-def score_kernel(page_total, token_slots, query_rows, token_block, table_ref, received_ref, tokens_ref, out_ref,
-                 ordered_ref, sims_ref, rows_ref):
+def score_kernel(page_total, token_slots, query_rows, token_block, table_ref, received_ref, partner_ref, out_ref,
+                 ordered_ref, sims_ref, rows_ref, tokens_ref):
     owners = received_ref.shape[0]
     ordered_rows, width = ordered_ref.shape
     capacity = (ordered_rows - 16 * page_total - 16) // owners
@@ -114,6 +114,11 @@
     position = jnp.concatenate(positions, axis=1)
     place = (position == lax.broadcasted_iota(jnp.int32, (ordered_rows, owners * capacity), 0)).astype(jnp.bfloat16)
     ordered_ref[...] = jnp.dot(place, rows_ref[...], preferred_element_type=jnp.float32).astype(jnp.bfloat16)
+    inner = lax.axis_index("inner")
+    tokens_ref[:, pl.ds(pl.multiple_of(inner * query_rows, query_rows), query_rows), :] = (
+        received_ref[:, 0:query_rows, :]
+    )
+    tokens_ref[:, pl.ds(pl.multiple_of((1 - inner) * query_rows, query_rows), query_rows), :] = partner_ref[...]
     sources = token_block // tokens_ref.shape[1]
     sub = lax.broadcasted_iota(jnp.int32, (8, token_block), 0)
     query_lane = lax.broadcasted_iota(jnp.int32, (1, total_queries), 1)
@@ -164,7 +169,7 @@
     owners = received.shape[0]
     width = received.shape[2]
     ordered_rows = owners * capacity + 16 * page_total + 16
-    token_total = tokens.shape[0] * tokens.shape[1]
+    token_total = 2 * tokens.shape[0] * tokens.shape[1]
     token_block = min(token_total, 1024)
     vmem = pl.BlockSpec(memory_space=pltpu.VMEM)
     return pl.pallas_call(
@@ -176,6 +181,7 @@
             pltpu.VMEM((ordered_rows, width), jnp.bfloat16),
             pltpu.VMEM((ordered_rows, token_block), jnp.float32),
             pltpu.VMEM((owners * capacity, width), jnp.bfloat16),
+            pltpu.VMEM((owners, 2 * query_rows, width), jnp.bfloat16),
         ],
         cost_estimate=pl.CostEstimate(
             flops=2 * ordered_rows * width * (owners * capacity + token_total),
@@ -200,7 +206,7 @@
         patch_rows, owner_ids, page_ids, proj_weight, proj_bias, query_tokens, query_counts, owners, capacity, halves
     )
     received = lax.all_to_all(message, "blk", split_axis=0, concat_axis=0, tiled=True)
-    halves_in = lax.all_gather(received[:, :query_rows], "inner", axis=1, tiled=True)
+    partner = lax.ppermute(received[:, :query_rows], "inner", [(0, 1), (1, 0)])
     block_at = -(-(query_rows + capacity) // 16) * 16
     combos = -(-owners * PAGES_DEV // 128) * 128
     count_rows = combos // 128
@@ -208,7 +214,7 @@
     page_counts = lax.dynamic_slice_in_dim(page_counts, lax.axis_index("blk") * PAGES_DEV, PAGES_DEV, axis=1)
     counts = received[:, block_at + count_rows, :per_block]
     table = jnp.concatenate([page_counts.reshape(owners * PAGES_DEV), counts.reshape(total_queries)]).astype(jnp.int32)
-    return page_scores(received, halves_in, table, total_queries, PAGES_DEV, token_slots, query_rows, capacity)
+    return page_scores(received, partner, table, total_queries, PAGES_DEV, token_slots, query_rows, capacity)
 
 
 def solution(mesh):

time: 42.7 us -> 41.4 us (0.970); the launches traced: 42 us -> 41.3 us
  blocking collectives: 2.31 us -> 25.5 us
  waiting for transfers between devices: 18 us -> 0.55 us
  starting transfers between devices: 7.31 us -> 0.07 us
  local copies, waits for them, and re-layouts: 0.33 us -> 1.03 us
    all_to_all x0 -> x1, blocking collectives: none -> 25.5 us  [shards(): lax.all_to_all(message, 'blk', split_axis=0, concat_axis=0, tiled=True)]
    all_to_all x1 -> x0, waiting for transfers between devices: 18 us -> none  [shards(): lax.all_to_all(message, 'blk', split_axis=0, concat_axis=0, tiled=True)]
    all_to_all x1 -> x0, starting transfers between devices: 7.31 us -> none  [shards(): lax.all_to_all(message, 'blk', split_axis=0, concat_axis=0, tiled=True)]
    all_gather x1 -> x0, blocking collectives: 2.31 us -> none  [shards(): lax.all_gather(received[:, :query_rows], 'inner', axis=1, tiled=True)]
    unnamed x2 -> x4, local copies, waits for them, and re-layouts: 0.01 us -> 0.71 us
    ppermute x0 -> x1, waiting for transfers between devices: none -> 0.55 us  [shards(): partner = lax.ppermute(received[:, :query_rows], 'inner', [(0, 1), (1, 0)])]
  transfers between devices with their start and end apart: 1 -> 1, of which waited for: 1 -> 1; matrix products, arithmetic and copies ran while one was open for 0% -> 2% of each run, Pallas kernels for 0% -> 0%
where the time goes in v13:
time: 41.4 us; the launch traced here: 41.3 us
  blocking collectives  25.5 us (62%)
  Pallas kernels  13.5 us (33%)
  local copies, waits for them, and re-layouts  1.03 us (2%)
  other arithmetic  0.66 us (2%)
  waiting for transfers between devices  0.55 us (1%)
    all_to_all x1, blocking collectives, shards(): lax.all_to_all(message, 'blk', split_axis=0, concat_axis=0, tiled=True)  25.5 us
    pallas_call x1, Pallas kernels, page_scores(): pl.pallas_call(functools.partial(score_kernel, page_total, token_slots, q...  8.18 us
    pallas_call x1, Pallas kernels, send_message(): pl.pallas_call(functools.partial(send_kernel, PAGES_DEV, capacity, query_...  5.28 us
  transfers between devices with their start and end apart: 1, of which 1 were waited for; matrix products, arithmetic and copies ran while one was open for 2% of the time, Pallas kernels for 0%

profile of v13, /device:TPU:0, one launch (start us, length us, event | category | flops | bytes accessed | tf_op | source)
XLA Modules:
  0.0 41.3 jit_solution(9716577539808434752)
XLA Ops:
  0.0 5.3 %shard_map.73 = bf16[8,336,128]{2,1,0:T(8,128)(2,1)} custom-call(s32[8]{0:T(128)} %query_counts_ref.1, s32[1,768]{1,0:T(1,128)} %bitcast.4, s32[768]{0:T(1024)} %page_ref.1, bf16[768,1536]{1,0:T(8,128)(2,1)} %rows_ref.1, bf16[1536,128]{1,0:T(8,128)(2,1)} %weight_ref.1, f32[1,128]{1,0:T(1,128)} %bitcast.5, bf16[256,128]{1,0:T(8,128)(2,1)} %bitcast.3), custom_call_target="tpu_custom_call" | custom-call | flops 603979776 | bytes 3440640 | tf_op jit(solution)/shard_map/pallas_call | solution.py:72
  5.3 25.5 %all_to_all.5.received_ref = bf16[8,336,128]{2,1,0:T(8,128)(2,1)S(1)} all-to-all(bf16[8,336,128]{2,1,0:T(8,128)(2,1)} %shard_map.73), channel_id=1, replica_groups=mesh['groups'=2,'blk'=8,'inner'=2] {'blk'}, dimensions={0} | all-to-all | bytes 1376256 | tf_op jit(solution)/shard_map/all_to_all | solution.py:208
  30.8 0.0 copy-start
  30.9 0.1 collective-permute-start
  31.0 0.1 reshape_squeeze.3
  31.1 0.1 dynamic-slice_reduce_fusion
  31.2 0.1 reshape.18
  31.2 0.7 %maximum_convert_fusion.table_ref = s32[128]{0:T(128)} fusion(bf16[64]{0:T(256)(128)(2,1)S(1)} %reshape_squeeze.3, bf16[64]{0:T(256)(128)(2,1)S(1)} %reshape.18), kind=kLoop, calls=%fused_computation.2 | loop fusion | flops 512 | bytes 768 | tf_op jit(solution)/shard_map/convert_element_type | solution.py:216
  31.9 0.5 %collective-permute-done.partner_ref = bf16[8,128,128]{2,1,0:T(8,128)(2,1)S(1)} collective-permute-done((bf16[8,128,128]{2,1,0:T(8,128)(2,1)S(1)}, bf16[8,128,128]{2,1,0:T(8,128)(2,1)S(1)}, u32[]{:S(2)}, u32[]{:S(2)}) %collective-permute-start) | collective-permute-done | bytes 262176 | tf_op jit(solution)/shard_map/ppermute | solution.py:209
  32.5 0.0 copy-done
  32.5 0.0 copy-start.1
  32.5 0.7 %copy-done.1 = bf16[8,128,128]{2,1,0:T(8,128)(2,1)} copy-done((bf16[8,128,128]{2,1,0:T(8,128)(2,1)}, bf16[8,128,128]{2,1,0:T(8,128)(2,1)S(1)}, u32[]{:S(2)}) %copy-start.1) | copy-done | bytes 262168
  33.2 8.2 %shard_map.74 = f32[8,64]{1,0:T(8,128)} custom-call(s32[128]{0:T(128)} %maximum_convert_fusion.table_ref, bf16[8,336,128]{2,1,0:T(8,128)(2,1)} %copy-done, bf16[8,128,128]{2,1,0:T(8,128)(2,1)} %copy-done.1), custom_call_target="tpu_custom_call" | custom-call | flops 1541406720 | bytes 952320 | tf_op jit(solution)/shard_map/pallas_call | solution.py:175
  (3 shorter events, 0.1 us)
Async XLA Ops:
  30.8 1.6 %copy-start = (bf16[8,336,128]{2,1,0:T(8,128)(2,1)}, bf16[8,336,128]{2,1,0:T(8,128)(2,1)S(1)}, u32[]{:S(2)}) copy-start(bf16[8,336,128]{2,1,0:T(8,128)(2,1)S(1)} %all_to_all.5.received_ref) | copy-start | bytes 2064388
  30.9 1.6 %collective-permute-start = (bf16[8,128,128]{2,1,0:T(8,128)(2,1)S(1)}, bf16[8,128,128]{2,1,0:T(8,128)(2,1)S(1)}, u32[]{:S(2)}, u32[]{:S(2)}) collective-permute-start(bf16[8,128,128]{2,1,0:T(8,128)(2,1)S(1)} %slice.14), channel_id=1, source_target_pairs={{0,1},{1,0},{2,3},{3,2},{4,5},{5,4},{6,7},{7,6},{8,9},{9,8},{10,11... | collective-permute-start | bytes 786440 | tf_op jit(solution)/shard_map/ppermute | solution.py:209
  32.5 0.7 %copy-start.1 = (bf16[8,128,128]{2,1,0:T(8,128)(2,1)}, bf16[8,128,128]{2,1,0:T(8,128)(2,1)S(1)}, u32[]{:S(2)}) copy-start(bf16[8,128,128]{2,1,0:T(8,128)(2,1)S(1)} %collective-permute-done.partner_ref) | copy-start | bytes 786436

commit v14 on v13

--- a/solution.py
+++ b/solution.py
@@ -22,11 +22,17 @@
     combos = -(-owners * page_total // 128) * 128
     combo_id = lax.broadcasted_iota(jnp.int32, (combos, rows), 0)
     onehot = (combo == combo_id).astype(jnp.bfloat16)
+    lane = 128 if rows % 128 == 0 else rows
     earlier = (
-        lax.broadcasted_iota(jnp.int32, (rows, rows), 0) < lax.broadcasted_iota(jnp.int32, (rows, rows), 1)
+        lax.broadcasted_iota(jnp.int32, (lane, lane), 0) < lax.broadcasted_iota(jnp.int32, (lane, lane), 1)
     ).astype(jnp.bfloat16)
-    seen = jnp.dot(onehot, earlier, preferred_element_type=jnp.float32)
-    count = jnp.sum(onehot.astype(jnp.float32), axis=1, keepdims=True)
+    parts = []
+    count = jnp.zeros((combos, 1), jnp.float32)
+    for start in range(0, rows, lane):
+        part = onehot[:, start : start + lane]
+        parts.append(jnp.dot(part, earlier, preferred_element_type=jnp.float32) + count)
+        count = count + jnp.sum(part.astype(jnp.float32), axis=1, keepdims=True)
+    seen = jnp.concatenate(parts, axis=1)
     row_id = lax.broadcasted_iota(jnp.int32, (combos, combos), 0)
     col_id = lax.broadcasted_iota(jnp.int32, (combos, combos), 1)
     same_owner_lower = (row_id // page_total == col_id // page_total) & (col_id % page_total < row_id % page_total)

time: 41.4 us -> 41.6 us (level)
  no operation moved by 1% of the time
where the time goes in v14:
time: 41.6 us; the launch traced here: 41.5 us
  blocking collectives  25.5 us (61%)
  Pallas kernels  13.6 us (33%)
  local copies, waits for them, and re-layouts  1.03 us (2%)
  other arithmetic  0.66 us (2%)
  waiting for transfers between devices  0.55 us (1%)
    all_to_all x1, blocking collectives, shards(): lax.all_to_all(message, 'blk', split_axis=0, concat_axis=0, tiled=True)  25.5 us
    pallas_call x1, Pallas kernels, page_scores(): pl.pallas_call(functools.partial(score_kernel, page_total, token_slots, q...  8.21 us
    pallas_call x1, Pallas kernels, send_message(): pl.pallas_call(functools.partial(send_kernel, PAGES_DEV, capacity, query_...  5.38 us
  transfers between devices with their start and end apart: 1, of which 1 were waited for; matrix products, arithmetic and copies ran while one was open for 2% of the time, Pallas kernels for 0%

profile of v14, /device:TPU:0, one launch (start us, length us, event | category | flops | bytes accessed | tf_op | source)
XLA Modules:
  0.0 41.5 jit_solution(11791555006943708065)
XLA Ops:
  0.0 5.4 %shard_map.73 = bf16[8,336,128]{2,1,0:T(8,128)(2,1)} custom-call(s32[8]{0:T(128)} %query_counts_ref.1, s32[1,768]{1,0:T(1,128)} %bitcast.4, s32[768]{0:T(1024)} %page_ref.1, bf16[768,1536]{1,0:T(8,128)(2,1)} %rows_ref.1, bf16[1536,128]{1,0:T(8,128)(2,1)} %weight_ref.1, f32[1,128]{1,0:T(1,128)} %bitcast.5, bf16[256,128]{1,0:T(8,128)(2,1)} %bitcast.3), custom_call_target="tpu_custom_call" | custom-call | flops 603979776 | bytes 3440640 | tf_op jit(solution)/shard_map/pallas_call | solution.py:78
  5.4 25.5 %all_to_all.5.received_ref = bf16[8,336,128]{2,1,0:T(8,128)(2,1)S(1)} all-to-all(bf16[8,336,128]{2,1,0:T(8,128)(2,1)} %shard_map.73), channel_id=1, replica_groups=mesh['groups'=2,'blk'=8,'inner'=2] {'blk'}, dimensions={0} | all-to-all | bytes 1376256 | tf_op jit(solution)/shard_map/all_to_all | solution.py:214
  30.9 0.0 copy-start
  30.9 0.1 collective-permute-start
  31.1 0.1 reshape_squeeze.3
  31.2 0.1 dynamic-slice_reduce_fusion
  31.3 0.1 reshape.18
  31.3 0.7 %maximum_convert_fusion.table_ref = s32[128]{0:T(128)} fusion(bf16[64]{0:T(256)(128)(2,1)S(1)} %reshape_squeeze.3, bf16[64]{0:T(256)(128)(2,1)S(1)} %reshape.18), kind=kLoop, calls=%fused_computation.2 | loop fusion | flops 512 | bytes 768 | tf_op jit(solution)/shard_map/convert_element_type | solution.py:222
  32.0 0.5 %collective-permute-done.partner_ref = bf16[8,128,128]{2,1,0:T(8,128)(2,1)S(1)} collective-permute-done((bf16[8,128,128]{2,1,0:T(8,128)(2,1)S(1)}, bf16[8,128,128]{2,1,0:T(8,128)(2,1)S(1)}, u32[]{:S(2)}, u32[]{:S(2)}) %collective-permute-start) | collective-permute-done | bytes 262176 | tf_op jit(solution)/shard_map/ppermute | solution.py:215
  32.5 0.0 copy-done
  32.6 0.0 copy-start.1
  32.6 0.7 %copy-done.1 = bf16[8,128,128]{2,1,0:T(8,128)(2,1)} copy-done((bf16[8,128,128]{2,1,0:T(8,128)(2,1)}, bf16[8,128,128]{2,1,0:T(8,128)(2,1)S(1)}, u32[]{:S(2)}) %copy-start.1) | copy-done | bytes 262168
  33.3 8.2 %shard_map.74 = f32[8,64]{1,0:T(8,128)} custom-call(s32[128]{0:T(128)} %maximum_convert_fusion.table_ref, bf16[8,336,128]{2,1,0:T(8,128)(2,1)} %copy-done, bf16[8,128,128]{2,1,0:T(8,128)(2,1)} %copy-done.1), custom_call_target="tpu_custom_call" | custom-call | flops 1541406720 | bytes 952320 | tf_op jit(solution)/shard_map/pallas_call | solution.py:181
  (3 shorter events, 0.1 us)
Async XLA Ops:
  30.9 1.6 %copy-start = (bf16[8,336,128]{2,1,0:T(8,128)(2,1)}, bf16[8,336,128]{2,1,0:T(8,128)(2,1)S(1)}, u32[]{:S(2)}) copy-start(bf16[8,336,128]{2,1,0:T(8,128)(2,1)S(1)} %all_to_all.5.received_ref) | copy-start | bytes 2064388
  30.9 1.6 %collective-permute-start = (bf16[8,128,128]{2,1,0:T(8,128)(2,1)S(1)}, bf16[8,128,128]{2,1,0:T(8,128)(2,1)S(1)}, u32[]{:S(2)}, u32[]{:S(2)}) collective-permute-start(bf16[8,128,128]{2,1,0:T(8,128)(2,1)S(1)} %slice.14), channel_id=1, source_target_pairs={{0,1},{1,0},{2,3},{3,2},{4,5},{5,4},{6,7},{7,6},{8,9},{9,8},{10,11... | collective-permute-start | bytes 786440 | tf_op jit(solution)/shard_map/ppermute | solution.py:215
  32.6 0.7 %copy-start.1 = (bf16[8,128,128]{2,1,0:T(8,128)(2,1)}, bf16[8,128,128]{2,1,0:T(8,128)(2,1)S(1)}, u32[]{:S(2)}) copy-start(bf16[8,128,128]{2,1,0:T(8,128)(2,1)S(1)} %collective-permute-done.partner_ref) | copy-start | bytes 786436

commit v15 on v14

--- a/solution.py
+++ b/solution.py
@@ -11,13 +11,12 @@
 PAGES_DEV = 8
 
 
-def send_kernel(page_total, capacity, query_rows, block_at, query_counts_ref, owner_ref, page_ref, rows_ref, weight_ref,
-                bias_ref, queries_ref, message_ref):
+def send_kernel(page_total, capacity, query_rows, block_at, query_counts_ref, owner_ref, page_ref, rows_hbm, weight_ref,
+                bias_ref, queries_ref, message_ref, rows_ref, copy_sem):
     owners = message_ref.shape[0]
     rows = rows_ref.shape[0]
-    proj = jnp.dot(rows_ref[...], weight_ref[...], preferred_element_type=jnp.float32) + bias_ref[...]
-    scale = lax.rsqrt(jnp.sum(proj * proj, axis=1, keepdims=True) + 1e-06)
-    local = (proj * scale).astype(jnp.bfloat16)
+    copy = pltpu.make_async_copy(rows_hbm, rows_ref, copy_sem)
+    copy.start()
     combo = owner_ref[...].reshape(1, rows) * page_total + page_ref[...].reshape(1, rows)
     combos = -(-owners * page_total // 128) * 128
     combo_id = lax.broadcasted_iota(jnp.int32, (combos, rows), 0)
@@ -57,6 +56,10 @@
         + [query_count_row, jnp.zeros((block_rows - len(count_rows) - 1, 128), jnp.float32)],
         axis=0,
     ).astype(jnp.bfloat16)
+    copy.wait()
+    proj = jnp.dot(rows_ref[...], weight_ref[...], preferred_element_type=jnp.float32) + bias_ref[...]
+    scale = lax.rsqrt(jnp.sum(proj * proj, axis=1, keepdims=True) + 1e-06)
+    local = (proj * scale).astype(jnp.bfloat16)
     own_half = queries_ref[pl.ds(pl.multiple_of(lax.axis_index("inner") * query_rows, query_rows), query_rows), :]
     slot_id = lax.broadcasted_iota(jnp.int32, (capacity, rows), 0)
     for owner in range(owners):
@@ -78,8 +81,9 @@
     return pl.pallas_call(
         functools.partial(send_kernel, PAGES_DEV, capacity, query_rows, block_at),
         out_shape=jax.ShapeDtypeStruct((owners, block_at + 16, width), jnp.bfloat16),
-        in_specs=[pl.BlockSpec(memory_space=pltpu.SMEM)] + [vmem] * 6,
+        in_specs=[pl.BlockSpec(memory_space=pltpu.SMEM), vmem, vmem, pl.BlockSpec(memory_space=pl.ANY)] + [vmem] * 3,
         out_specs=vmem,
+        scratch_shapes=[pltpu.VMEM((rows, features), jnp.bfloat16), pltpu.SemaphoreType.DMA],
         cost_estimate=pl.CostEstimate(
             flops=2 * rows * width * (features + owners * capacity),
             bytes_accessed=2 * (rows * features + features * width + owners * (block_at + 16) * width),

time: 41.6 us -> 42.5 us (1.022)
  Pallas kernels: 13.6 us -> 14.2 us
    pallas_call x1, Pallas kernels: 5.38 us -> 6.24 us  [send_message(): pl.pallas_call(functools.partial(send_kernel, PAGES_DEV, capacity, query_...]
where the time goes in v15:
time: 42.5 us; the launch traced here: 42.1 us
  blocking collectives  25.6 us (60%)
  Pallas kernels  14.2 us (33%)
  local copies, waits for them, and re-layouts  1.03 us (2%)
  other arithmetic  0.66 us (2%)
  waiting for transfers between devices  0.55 us (1%)
    all_to_all x1, blocking collectives, shards(): lax.all_to_all(message, 'blk', split_axis=0, concat_axis=0, tiled=True)  25.6 us
    pallas_call x1, Pallas kernels, page_scores(): pl.pallas_call(functools.partial(score_kernel, page_total, token_slots, q...  7.97 us
    pallas_call x1, Pallas kernels, send_message(): pl.pallas_call(functools.partial(send_kernel, PAGES_DEV, capacity, query_...  6.24 us
  transfers between devices with their start and end apart: 1, of which 1 were waited for; matrix products, arithmetic and copies ran while one was open for 2% of the time, Pallas kernels for 0%

profile of v15, /device:TPU:0, one launch (start us, length us, event | category | flops | bytes accessed | tf_op | source)
XLA Modules:
  0.0 42.1 jit_solution(16235554068937958093)
XLA Ops:
  0.0 6.2 %shard_map.73 = bf16[8,336,128]{2,1,0:T(8,128)(2,1)} custom-call(s32[8]{0:T(128)} %query_counts_ref.1, s32[1,768]{1,0:T(1,128)} %bitcast.4, s32[768]{0:T(1024)} %page_ref.1, bf16[768,1536]{1,0:T(8,128)(2,1)} %rows_hbm.1, bf16[1536,128]{1,0:T(8,128)(2,1)} %weight_ref.1, f32[1,128]{1,0:T(1,128)} %bitcast.5, bf16[256,128]{1,0:T(8,128)(2,1)} %bitcast.3), custom_call_target="tpu_custom_call" | custom-call | flops 603979776 | bytes 3440640 | tf_op jit(solution)/shard_map/pallas_call | solution.py:81
  6.2 25.6 %all_to_all.5.received_ref = bf16[8,336,128]{2,1,0:T(8,128)(2,1)S(1)} all-to-all(bf16[8,336,128]{2,1,0:T(8,128)(2,1)} %shard_map.73), channel_id=1, replica_groups=mesh['groups'=2,'blk'=8,'inner'=2] {'blk'}, dimensions={0} | all-to-all | bytes 1376256 | tf_op jit(solution)/shard_map/all_to_all | solution.py:218
  31.8 0.0 copy-start
  31.8 0.1 collective-permute-start
  31.9 0.1 reshape_squeeze.3
  32.0 0.1 dynamic-slice_reduce_fusion
  32.1 0.1 reshape.18
  32.2 0.7 %maximum_convert_fusion.table_ref = s32[128]{0:T(128)} fusion(bf16[64]{0:T(256)(128)(2,1)S(1)} %reshape_squeeze.3, bf16[64]{0:T(256)(128)(2,1)S(1)} %reshape.18), kind=kLoop, calls=%fused_computation.2 | loop fusion | flops 512 | bytes 768 | tf_op jit(solution)/shard_map/convert_element_type | solution.py:226
  32.9 0.5 %collective-permute-done.partner_ref = bf16[8,128,128]{2,1,0:T(8,128)(2,1)S(1)} collective-permute-done((bf16[8,128,128]{2,1,0:T(8,128)(2,1)S(1)}, bf16[8,128,128]{2,1,0:T(8,128)(2,1)S(1)}, u32[]{:S(2)}, u32[]{:S(2)}) %collective-permute-start) | collective-permute-done | bytes 262176 | tf_op jit(solution)/shard_map/ppermute | solution.py:219
  33.4 0.0 copy-done
  33.4 0.0 copy-start.1
  33.4 0.7 %copy-done.1 = bf16[8,128,128]{2,1,0:T(8,128)(2,1)} copy-done((bf16[8,128,128]{2,1,0:T(8,128)(2,1)}, bf16[8,128,128]{2,1,0:T(8,128)(2,1)S(1)}, u32[]{:S(2)}) %copy-start.1) | copy-done | bytes 262168
  34.1 8.0 %shard_map.74 = f32[8,64]{1,0:T(8,128)} custom-call(s32[128]{0:T(128)} %maximum_convert_fusion.table_ref, bf16[8,336,128]{2,1,0:T(8,128)(2,1)} %copy-done, bf16[8,128,128]{2,1,0:T(8,128)(2,1)} %copy-done.1), custom_call_target="tpu_custom_call" | custom-call | flops 1541406720 | bytes 952320 | tf_op jit(solution)/shard_map/pallas_call | solution.py:185
  (3 shorter events, 0.1 us)
Async XLA Ops:
  31.8 1.6 %copy-start = (bf16[8,336,128]{2,1,0:T(8,128)(2,1)}, bf16[8,336,128]{2,1,0:T(8,128)(2,1)S(1)}, u32[]{:S(2)}) copy-start(bf16[8,336,128]{2,1,0:T(8,128)(2,1)S(1)} %all_to_all.5.received_ref) | copy-start | bytes 2064388
  31.8 1.6 %collective-permute-start = (bf16[8,128,128]{2,1,0:T(8,128)(2,1)S(1)}, bf16[8,128,128]{2,1,0:T(8,128)(2,1)S(1)}, u32[]{:S(2)}, u32[]{:S(2)}) collective-permute-start(bf16[8,128,128]{2,1,0:T(8,128)(2,1)S(1)} %slice.14), channel_id=1, source_target_pairs={{0,1},{1,0},{2,3},{3,2},{4,5},{5,4},{6,7},{7,6},{8,9},{9,8},{10,11... | collective-permute-start | bytes 786440 | tf_op jit(solution)/shard_map/ppermute | solution.py:219
  33.4 0.7 %copy-start.1 = (bf16[8,128,128]{2,1,0:T(8,128)(2,1)}, bf16[8,128,128]{2,1,0:T(8,128)(2,1)S(1)}, u32[]{:S(2)}) copy-start(bf16[8,128,128]{2,1,0:T(8,128)(2,1)S(1)} %collective-permute-done.partner_ref) | copy-start | bytes 786436

commit v16 on v14

--- a/solution.py
+++ b/solution.py
@@ -58,9 +58,10 @@
         axis=0,
     ).astype(jnp.bfloat16)
     own_half = queries_ref[pl.ds(pl.multiple_of(lax.axis_index("inner") * query_rows, query_rows), query_rows), :]
-    slot_id = lax.broadcasted_iota(jnp.int32, (capacity, rows), 0)
+    slot_id = lax.broadcasted_iota(jnp.int32, (capacity, rows), 0).astype(jnp.bfloat16)
     for owner in range(owners):
-        placed = (slot == slot_id + owner * capacity).astype(jnp.bfloat16)
+        offset = (slot - owner * capacity).astype(jnp.bfloat16)
+        placed = (offset == slot_id).astype(jnp.bfloat16)
         message_ref[owner, 0:query_rows, :] = own_half
         message_ref[owner, query_rows : query_rows + capacity, :] = jnp.dot(
             placed, local, preferred_element_type=jnp.float32

time: 41.6 us -> 42.6 us (1.024)
  Pallas kernels: 13.6 us -> 14.4 us
    pallas_call x1, Pallas kernels: 8.21 us -> 8.81 us  [page_scores(): pl.pallas_call(functools.partial(score_kernel, page_total, token_slots, q...]
where the time goes in v16:
time: 42.6 us; the launch traced here: 42.3 us
  blocking collectives  25.5 us (60%)
  Pallas kernels  14.4 us (34%)
  local copies, waits for them, and re-layouts  1.03 us (2%)
  other arithmetic  0.66 us (2%)
  waiting for transfers between devices  0.55 us (1%)
    all_to_all x1, blocking collectives, shards(): lax.all_to_all(message, 'blk', split_axis=0, concat_axis=0, tiled=True)  25.5 us
    pallas_call x1, Pallas kernels, page_scores(): pl.pallas_call(functools.partial(score_kernel, page_total, token_slots, q...  8.81 us
    pallas_call x1, Pallas kernels, send_message(): pl.pallas_call(functools.partial(send_kernel, PAGES_DEV, capacity, query_...  5.62 us
  transfers between devices with their start and end apart: 1, of which 1 were waited for; matrix products, arithmetic and copies ran while one was open for 2% of the time, Pallas kernels for 0%

profile of v16, /device:TPU:0, one launch (start us, length us, event | category | flops | bytes accessed | tf_op | source)
XLA Modules:
  0.0 42.3 jit_solution(7234330519251122759)
XLA Ops:
  0.0 5.6 %shard_map.73 = bf16[8,336,128]{2,1,0:T(8,128)(2,1)} custom-call(s32[8]{0:T(128)} %query_counts_ref.1, s32[1,768]{1,0:T(1,128)} %bitcast.4, s32[768]{0:T(1024)} %page_ref.1, bf16[768,1536]{1,0:T(8,128)(2,1)} %rows_ref.1, bf16[1536,128]{1,0:T(8,128)(2,1)} %weight_ref.1, f32[1,128]{1,0:T(1,128)} %bitcast.5, bf16[256,128]{1,0:T(8,128)(2,1)} %bitcast.3), custom_call_target="tpu_custom_call" | custom-call | flops 603979776 | bytes 3440640 | tf_op jit(solution)/shard_map/pallas_call | solution.py:79
  5.6 25.5 %all_to_all.5.received_ref = bf16[8,336,128]{2,1,0:T(8,128)(2,1)S(1)} all-to-all(bf16[8,336,128]{2,1,0:T(8,128)(2,1)} %shard_map.73), channel_id=1, replica_groups=mesh['groups'=2,'blk'=8,'inner'=2] {'blk'}, dimensions={0} | all-to-all | bytes 1376256 | tf_op jit(solution)/shard_map/all_to_all | solution.py:215
  31.2 0.0 copy-start
  31.2 0.1 collective-permute-start
  31.3 0.1 reshape_squeeze.3
  31.4 0.1 dynamic-slice_reduce_fusion
  31.5 0.1 reshape.18
  31.6 0.7 %maximum_convert_fusion.table_ref = s32[128]{0:T(128)} fusion(bf16[64]{0:T(256)(128)(2,1)S(1)} %reshape_squeeze.3, bf16[64]{0:T(256)(128)(2,1)S(1)} %reshape.18), kind=kLoop, calls=%fused_computation.2 | loop fusion | flops 512 | bytes 768 | tf_op jit(solution)/shard_map/convert_element_type | solution.py:223
  32.2 0.5 %collective-permute-done.partner_ref = bf16[8,128,128]{2,1,0:T(8,128)(2,1)S(1)} collective-permute-done((bf16[8,128,128]{2,1,0:T(8,128)(2,1)S(1)}, bf16[8,128,128]{2,1,0:T(8,128)(2,1)S(1)}, u32[]{:S(2)}, u32[]{:S(2)}) %collective-permute-start) | collective-permute-done | bytes 262176 | tf_op jit(solution)/shard_map/ppermute | solution.py:216
  32.8 0.0 copy-done
  32.8 0.0 copy-start.1
  32.8 0.7 %copy-done.1 = bf16[8,128,128]{2,1,0:T(8,128)(2,1)} copy-done((bf16[8,128,128]{2,1,0:T(8,128)(2,1)}, bf16[8,128,128]{2,1,0:T(8,128)(2,1)S(1)}, u32[]{:S(2)}) %copy-start.1) | copy-done | bytes 262168
  33.5 8.8 %shard_map.74 = f32[8,64]{1,0:T(8,128)} custom-call(s32[128]{0:T(128)} %maximum_convert_fusion.table_ref, bf16[8,336,128]{2,1,0:T(8,128)(2,1)} %copy-done, bf16[8,128,128]{2,1,0:T(8,128)(2,1)} %copy-done.1), custom_call_target="tpu_custom_call" | custom-call | flops 1541406720 | bytes 952320 | tf_op jit(solution)/shard_map/pallas_call | solution.py:182
  (3 shorter events, 0.1 us)
Async XLA Ops:
  31.2 1.6 %copy-start = (bf16[8,336,128]{2,1,0:T(8,128)(2,1)}, bf16[8,336,128]{2,1,0:T(8,128)(2,1)S(1)}, u32[]{:S(2)}) copy-start(bf16[8,336,128]{2,1,0:T(8,128)(2,1)S(1)} %all_to_all.5.received_ref) | copy-start | bytes 2064388
  31.2 1.6 %collective-permute-start = (bf16[8,128,128]{2,1,0:T(8,128)(2,1)S(1)}, bf16[8,128,128]{2,1,0:T(8,128)(2,1)S(1)}, u32[]{:S(2)}, u32[]{:S(2)}) collective-permute-start(bf16[8,128,128]{2,1,0:T(8,128)(2,1)S(1)} %slice.14), channel_id=1, source_target_pairs={{0,1},{1,0},{2,3},{3,2},{4,5},{5,4},{6,7},{7,6},{8,9},{9,8},{10,11... | collective-permute-start | bytes 786440 | tf_op jit(solution)/shard_map/ppermute | solution.py:216
  32.8 0.7 %copy-start.1 = (bf16[8,128,128]{2,1,0:T(8,128)(2,1)}, bf16[8,128,128]{2,1,0:T(8,128)(2,1)S(1)}, u32[]{:S(2)}) copy-start(bf16[8,128,128]{2,1,0:T(8,128)(2,1)S(1)} %collective-permute-done.partner_ref) | copy-start | bytes 786436

commit v17 on v14

--- a/solution.py
+++ b/solution.py
@@ -133,6 +133,8 @@
         live_count = jnp.where(query_lane == query, table_ref[owners * page_total + query], live_count)
     token_id = lax.broadcasted_iota(jnp.int32, (token_block, total_queries), 0)
     query_id = lax.broadcasted_iota(jnp.int32, (token_block, total_queries), 1)
+    query_gap = query_id - token_id // token_slots
+    slot_live = (token_id % token_slots) < live_count
 
     def block_scores(block, total):
         tokens = tokens_ref[pl.ds(block * sources, sources)].reshape(token_block, width)
@@ -159,8 +161,7 @@
             high = jnp.maximum(high, jnp.where(sub + 8 < rest, sims_ref[pl.ds(start + 8, 8), :], jnp.float32(-2.0)))
             best_rows.append(jnp.max(jnp.maximum(low, high), axis=0, keepdims=True))
         best = jnp.concatenate(best_rows, axis=0)
-        token = token_id + block * token_block
-        live = ((token // token_slots) == query_id) & ((token % token_slots) < live_count)
+        live = (query_gap == block * (token_block // token_slots)) & slot_live
         return total + jnp.dot(
             best, live.astype(jnp.float32), precision=lax.Precision.HIGHEST, preferred_element_type=jnp.float32
         )

time: 41.6 us -> 40.8 us (0.981)
  Pallas kernels: 13.6 us -> 12.6 us
    pallas_call x1, Pallas kernels: 8.21 us -> 7.18 us  [page_scores(): pl.pallas_call(functools.partial(score_kernel, page_total, token_slots, q...]
where the time goes in v17:
time: 40.8 us; the launch traced here: 40.4 us
  blocking collectives  25.5 us (63%)
  Pallas kernels  12.6 us (31%)
  local copies, waits for them, and re-layouts  1.03 us (3%)
  other arithmetic  0.66 us (2%)
  waiting for transfers between devices  0.55 us (1%)
    all_to_all x1, blocking collectives, shards(): lax.all_to_all(message, 'blk', split_axis=0, concat_axis=0, tiled=True)  25.5 us
    pallas_call x1, Pallas kernels, page_scores(): pl.pallas_call(functools.partial(score_kernel, page_total, token_slots, q...  7.18 us
    pallas_call x1, Pallas kernels, send_message(): pl.pallas_call(functools.partial(send_kernel, PAGES_DEV, capacity, query_...  5.38 us
  transfers between devices with their start and end apart: 1, of which 1 were waited for; matrix products, arithmetic and copies ran while one was open for 2% of the time, Pallas kernels for 0%

profile of v17, /device:TPU:0, one launch (start us, length us, event | category | flops | bytes accessed | tf_op | source)
XLA Modules:
  0.0 40.4 jit_solution(17036820726753025102)
XLA Ops:
  0.0 5.4 %shard_map.73 = bf16[8,336,128]{2,1,0:T(8,128)(2,1)} custom-call(s32[8]{0:T(128)} %query_counts_ref.1, s32[1,768]{1,0:T(1,128)} %bitcast.4, s32[768]{0:T(1024)} %page_ref.1, bf16[768,1536]{1,0:T(8,128)(2,1)} %rows_ref.1, bf16[1536,128]{1,0:T(8,128)(2,1)} %weight_ref.1, f32[1,128]{1,0:T(1,128)} %bitcast.5, bf16[256,128]{1,0:T(8,128)(2,1)} %bitcast.3), custom_call_target="tpu_custom_call" | custom-call | flops 603979776 | bytes 3440640 | tf_op jit(solution)/shard_map/pallas_call | solution.py:78
  5.4 25.5 %all_to_all.5.received_ref = bf16[8,336,128]{2,1,0:T(8,128)(2,1)S(1)} all-to-all(bf16[8,336,128]{2,1,0:T(8,128)(2,1)} %shard_map.73), channel_id=1, replica_groups=mesh['groups'=2,'blk'=8,'inner'=2] {'blk'}, dimensions={0} | all-to-all | bytes 1376256 | tf_op jit(solution)/shard_map/all_to_all | solution.py:215
  30.9 0.0 copy-start
  30.9 0.1 collective-permute-start
  31.1 0.1 reshape_squeeze.3
  31.2 0.1 dynamic-slice_reduce_fusion
  31.3 0.1 reshape.18
  31.3 0.7 %maximum_convert_fusion.table_ref = s32[128]{0:T(128)} fusion(bf16[64]{0:T(256)(128)(2,1)S(1)} %reshape_squeeze.3, bf16[64]{0:T(256)(128)(2,1)S(1)} %reshape.18), kind=kLoop, calls=%fused_computation.2 | loop fusion | flops 512 | bytes 768 | tf_op jit(solution)/shard_map/convert_element_type | solution.py:223
  32.0 0.5 %collective-permute-done.partner_ref = bf16[8,128,128]{2,1,0:T(8,128)(2,1)S(1)} collective-permute-done((bf16[8,128,128]{2,1,0:T(8,128)(2,1)S(1)}, bf16[8,128,128]{2,1,0:T(8,128)(2,1)S(1)}, u32[]{:S(2)}, u32[]{:S(2)}) %collective-permute-start) | collective-permute-done | bytes 262176 | tf_op jit(solution)/shard_map/ppermute | solution.py:216
  32.5 0.0 copy-done
  32.6 0.0 copy-start.1
  32.6 0.7 %copy-done.1 = bf16[8,128,128]{2,1,0:T(8,128)(2,1)} copy-done((bf16[8,128,128]{2,1,0:T(8,128)(2,1)}, bf16[8,128,128]{2,1,0:T(8,128)(2,1)S(1)}, u32[]{:S(2)}) %copy-start.1) | copy-done | bytes 262168
  33.3 7.2 %shard_map.74 = f32[8,64]{1,0:T(8,128)} custom-call(s32[128]{0:T(128)} %maximum_convert_fusion.table_ref, bf16[8,336,128]{2,1,0:T(8,128)(2,1)} %copy-done, bf16[8,128,128]{2,1,0:T(8,128)(2,1)} %copy-done.1), custom_call_target="tpu_custom_call" | custom-call | flops 1541406720 | bytes 952320 | tf_op jit(solution)/shard_map/pallas_call | solution.py:182
  (3 shorter events, 0.1 us)
Async XLA Ops:
  30.9 1.6 %copy-start = (bf16[8,336,128]{2,1,0:T(8,128)(2,1)}, bf16[8,336,128]{2,1,0:T(8,128)(2,1)S(1)}, u32[]{:S(2)}) copy-start(bf16[8,336,128]{2,1,0:T(8,128)(2,1)S(1)} %all_to_all.5.received_ref) | copy-start | bytes 2064388
  30.9 1.6 %collective-permute-start = (bf16[8,128,128]{2,1,0:T(8,128)(2,1)S(1)}, bf16[8,128,128]{2,1,0:T(8,128)(2,1)S(1)}, u32[]{:S(2)}, u32[]{:S(2)}) collective-permute-start(bf16[8,128,128]{2,1,0:T(8,128)(2,1)S(1)} %slice.14), channel_id=1, source_target_pairs={{0,1},{1,0},{2,3},{3,2},{4,5},{5,4},{6,7},{7,6},{8,9},{9,8},{10,11... | collective-permute-start | bytes 786440 | tf_op jit(solution)/shard_map/ppermute | solution.py:216
  32.6 0.7 %copy-start.1 = (bf16[8,128,128]{2,1,0:T(8,128)(2,1)}, bf16[8,128,128]{2,1,0:T(8,128)(2,1)S(1)}, u32[]{:S(2)}) copy-start(bf16[8,128,128]{2,1,0:T(8,128)(2,1)S(1)} %collective-permute-done.partner_ref) | copy-start | bytes 786436

commit v18 on v17

--- a/solution.py
+++ b/solution.py
@@ -168,7 +168,7 @@
 
     blocks = tokens_ref.shape[0] * tokens_ref.shape[1] // token_block
     out_ref[...] = lax.fori_loop(
-        0, blocks, block_scores, jnp.zeros((page_total, total_queries), jnp.float32)
+        0, blocks, block_scores, jnp.zeros((page_total, total_queries), jnp.float32), unroll=blocks <= 4
     )
 
 

time: 40.8 us -> 44 us (1.078)
  Pallas kernels: 12.6 us -> 15.9 us
    pallas_call x1, Pallas kernels: 7.18 us -> 10.5 us  [page_scores(): pl.pallas_call(functools.partial(score_kernel, page_total, token_slots, q...]
where the time goes in v18:
time: 44 us; the launch traced here: 43.8 us
  blocking collectives  25.5 us (58%)
  Pallas kernels  15.9 us (36%)
  local copies, waits for them, and re-layouts  1.03 us (2%)
  other arithmetic  0.66 us (2%)
  waiting for transfers between devices  0.55 us (1%)
    all_to_all x1, blocking collectives, shards(): lax.all_to_all(message, 'blk', split_axis=0, concat_axis=0, tiled=True)  25.5 us
    pallas_call x1, Pallas kernels, page_scores(): pl.pallas_call(functools.partial(score_kernel, page_total, token_slots, q...  10.5 us
    pallas_call x1, Pallas kernels, send_message(): pl.pallas_call(functools.partial(send_kernel, PAGES_DEV, capacity, query_...  5.38 us
  transfers between devices with their start and end apart: 1, of which 1 were waited for; matrix products, arithmetic and copies ran while one was open for 2% of the time, Pallas kernels for 0%

profile of v18, /device:TPU:0, one launch (start us, length us, event | category | flops | bytes accessed | tf_op | source)
XLA Modules:
  0.0 43.8 jit_solution(14056302044015746464)
XLA Ops:
  0.0 5.4 %shard_map.73 = bf16[8,336,128]{2,1,0:T(8,128)(2,1)} custom-call(s32[8]{0:T(128)} %query_counts_ref.1, s32[1,768]{1,0:T(1,128)} %bitcast.4, s32[768]{0:T(1024)} %page_ref.1, bf16[768,1536]{1,0:T(8,128)(2,1)} %rows_ref.1, bf16[1536,128]{1,0:T(8,128)(2,1)} %weight_ref.1, f32[1,128]{1,0:T(1,128)} %bitcast.5, bf16[256,128]{1,0:T(8,128)(2,1)} %bitcast.3), custom_call_target="tpu_custom_call" | custom-call | flops 603979776 | bytes 3440640 | tf_op jit(solution)/shard_map/pallas_call | solution.py:78
  5.4 25.5 %all_to_all.5.received_ref = bf16[8,336,128]{2,1,0:T(8,128)(2,1)S(1)} all-to-all(bf16[8,336,128]{2,1,0:T(8,128)(2,1)} %shard_map.73), channel_id=1, replica_groups=mesh['groups'=2,'blk'=8,'inner'=2] {'blk'}, dimensions={0} | all-to-all | bytes 1376256 | tf_op jit(solution)/shard_map/all_to_all | solution.py:215
  30.9 0.0 copy-start
  30.9 0.1 collective-permute-start
  31.1 0.1 reshape_squeeze.3
  31.2 0.1 dynamic-slice_reduce_fusion
  31.3 0.1 reshape.18
  31.3 0.7 %maximum_convert_fusion.table_ref = s32[128]{0:T(128)} fusion(bf16[64]{0:T(256)(128)(2,1)S(1)} %reshape_squeeze.3, bf16[64]{0:T(256)(128)(2,1)S(1)} %reshape.18), kind=kLoop, calls=%fused_computation.2 | loop fusion | flops 512 | bytes 768 | tf_op jit(solution)/shard_map/convert_element_type | solution.py:223
  32.0 0.5 %collective-permute-done.partner_ref = bf16[8,128,128]{2,1,0:T(8,128)(2,1)S(1)} collective-permute-done((bf16[8,128,128]{2,1,0:T(8,128)(2,1)S(1)}, bf16[8,128,128]{2,1,0:T(8,128)(2,1)S(1)}, u32[]{:S(2)}, u32[]{:S(2)}) %collective-permute-start) | collective-permute-done | bytes 262176 | tf_op jit(solution)/shard_map/ppermute | solution.py:216
  32.5 0.0 copy-done
  32.6 0.0 copy-start.1
  32.6 0.7 %copy-done.1 = bf16[8,128,128]{2,1,0:T(8,128)(2,1)} copy-done((bf16[8,128,128]{2,1,0:T(8,128)(2,1)}, bf16[8,128,128]{2,1,0:T(8,128)(2,1)S(1)}, u32[]{:S(2)}) %copy-start.1) | copy-done | bytes 262168
  33.3 10.5 %shard_map.74 = f32[8,64]{1,0:T(8,128)} custom-call(s32[128]{0:T(128)} %maximum_convert_fusion.table_ref, bf16[8,336,128]{2,1,0:T(8,128)(2,1)} %copy-done, bf16[8,128,128]{2,1,0:T(8,128)(2,1)} %copy-done.1), custom_call_target="tpu_custom_call" | custom-call | flops 1541406720 | bytes 952320 | tf_op jit(solution)/shard_map/pallas_call | solution.py:182
  (3 shorter events, 0.1 us)
Async XLA Ops:
  30.9 1.6 %copy-start = (bf16[8,336,128]{2,1,0:T(8,128)(2,1)}, bf16[8,336,128]{2,1,0:T(8,128)(2,1)S(1)}, u32[]{:S(2)}) copy-start(bf16[8,336,128]{2,1,0:T(8,128)(2,1)S(1)} %all_to_all.5.received_ref) | copy-start | bytes 2064388
  30.9 1.6 %collective-permute-start = (bf16[8,128,128]{2,1,0:T(8,128)(2,1)S(1)}, bf16[8,128,128]{2,1,0:T(8,128)(2,1)S(1)}, u32[]{:S(2)}, u32[]{:S(2)}) collective-permute-start(bf16[8,128,128]{2,1,0:T(8,128)(2,1)S(1)} %slice.14), channel_id=1, source_target_pairs={{0,1},{1,0},{2,3},{3,2},{4,5},{5,4},{6,7},{7,6},{8,9},{9,8},{10,11... | collective-permute-start | bytes 786440 | tf_op jit(solution)/shard_map/ppermute | solution.py:216
  32.6 0.7 %copy-start.1 = (bf16[8,128,128]{2,1,0:T(8,128)(2,1)}, bf16[8,128,128]{2,1,0:T(8,128)(2,1)S(1)}, u32[]{:S(2)}) copy-start(bf16[8,128,128]{2,1,0:T(8,128)(2,1)S(1)} %collective-permute-done.partner_ref) | copy-start | bytes 786436

commit v19 on v17

--- a/solution.py
+++ b/solution.py
@@ -163,7 +163,7 @@
         best = jnp.concatenate(best_rows, axis=0)
         live = (query_gap == block * (token_block // token_slots)) & slot_live
         return total + jnp.dot(
-            best, live.astype(jnp.float32), precision=lax.Precision.HIGHEST, preferred_element_type=jnp.float32
+            best, live.astype(jnp.float32), precision=lax.Precision.HIGH, preferred_element_type=jnp.float32
         )
 
     blocks = tokens_ref.shape[0] * tokens_ref.shape[1] // token_block

time: 40.8 us -> 41.2 us (level); the launches traced: 40.4 us -> 41.5 us
  Pallas kernels: 12.6 us -> 13.7 us
    pallas_call x1, Pallas kernels: 7.18 us -> 8.28 us  [page_scores(): pl.pallas_call(functools.partial(score_kernel, page_total, token_slots, q...]
where the time goes in v19:
time: 41.2 us; the launch traced here: 41.5 us
  blocking collectives  25.5 us (62%)
  Pallas kernels  13.7 us (33%)
  local copies, waits for them, and re-layouts  1.03 us (2%)
  other arithmetic  0.66 us (2%)
  waiting for transfers between devices  0.55 us (1%)
    all_to_all x1, blocking collectives, shards(): lax.all_to_all(message, 'blk', split_axis=0, concat_axis=0, tiled=True)  25.5 us
    pallas_call x1, Pallas kernels, page_scores(): pl.pallas_call(functools.partial(score_kernel, page_total, token_slots, q...  8.28 us
    pallas_call x1, Pallas kernels, send_message(): pl.pallas_call(functools.partial(send_kernel, PAGES_DEV, capacity, query_...  5.38 us
  transfers between devices with their start and end apart: 1, of which 1 were waited for; matrix products, arithmetic and copies ran while one was open for 2% of the time, Pallas kernels for 0%

profile of v19, /device:TPU:0, one launch (start us, length us, event | category | flops | bytes accessed | tf_op | source)
XLA Modules:
  0.0 41.5 jit_solution(445053072020562851)
XLA Ops:
  0.0 5.4 %shard_map.73 = bf16[8,336,128]{2,1,0:T(8,128)(2,1)} custom-call(s32[8]{0:T(128)} %query_counts_ref.1, s32[1,768]{1,0:T(1,128)} %bitcast.4, s32[768]{0:T(1024)} %page_ref.1, bf16[768,1536]{1,0:T(8,128)(2,1)} %rows_ref.1, bf16[1536,128]{1,0:T(8,128)(2,1)} %weight_ref.1, f32[1,128]{1,0:T(1,128)} %bitcast.5, bf16[256,128]{1,0:T(8,128)(2,1)} %bitcast.3), custom_call_target="tpu_custom_call" | custom-call | flops 603979776 | bytes 3440640 | tf_op jit(solution)/shard_map/pallas_call | solution.py:78
  5.4 25.5 %all_to_all.5.received_ref = bf16[8,336,128]{2,1,0:T(8,128)(2,1)S(1)} all-to-all(bf16[8,336,128]{2,1,0:T(8,128)(2,1)} %shard_map.73), channel_id=1, replica_groups=mesh['groups'=2,'blk'=8,'inner'=2] {'blk'}, dimensions={0} | all-to-all | bytes 1376256 | tf_op jit(solution)/shard_map/all_to_all | solution.py:215
  30.9 0.0 copy-start
  30.9 0.1 collective-permute-start
  31.1 0.1 reshape_squeeze.3
  31.2 0.1 dynamic-slice_reduce_fusion
  31.3 0.1 reshape.18
  31.3 0.7 %maximum_convert_fusion.table_ref = s32[128]{0:T(128)} fusion(bf16[64]{0:T(256)(128)(2,1)S(1)} %reshape_squeeze.3, bf16[64]{0:T(256)(128)(2,1)S(1)} %reshape.18), kind=kLoop, calls=%fused_computation.2 | loop fusion | flops 512 | bytes 768 | tf_op jit(solution)/shard_map/convert_element_type | solution.py:223
  32.0 0.5 %collective-permute-done.partner_ref = bf16[8,128,128]{2,1,0:T(8,128)(2,1)S(1)} collective-permute-done((bf16[8,128,128]{2,1,0:T(8,128)(2,1)S(1)}, bf16[8,128,128]{2,1,0:T(8,128)(2,1)S(1)}, u32[]{:S(2)}, u32[]{:S(2)}) %collective-permute-start) | collective-permute-done | bytes 262176 | tf_op jit(solution)/shard_map/ppermute | solution.py:216
  32.5 0.0 copy-done
  32.6 0.0 copy-start.1
  32.6 0.7 %copy-done.1 = bf16[8,128,128]{2,1,0:T(8,128)(2,1)} copy-done((bf16[8,128,128]{2,1,0:T(8,128)(2,1)}, bf16[8,128,128]{2,1,0:T(8,128)(2,1)S(1)}, u32[]{:S(2)}) %copy-start.1) | copy-done | bytes 262168
  33.3 8.3 %shard_map.74 = f32[8,64]{1,0:T(8,128)} custom-call(s32[128]{0:T(128)} %maximum_convert_fusion.table_ref, bf16[8,336,128]{2,1,0:T(8,128)(2,1)} %copy-done, bf16[8,128,128]{2,1,0:T(8,128)(2,1)} %copy-done.1), custom_call_target="tpu_custom_call" | custom-call | flops 1541406720 | bytes 952320 | tf_op jit(solution)/shard_map/pallas_call | solution.py:182
  (3 shorter events, 0.1 us)
Async XLA Ops:
  30.9 1.6 %copy-start = (bf16[8,336,128]{2,1,0:T(8,128)(2,1)}, bf16[8,336,128]{2,1,0:T(8,128)(2,1)S(1)}, u32[]{:S(2)}) copy-start(bf16[8,336,128]{2,1,0:T(8,128)(2,1)S(1)} %all_to_all.5.received_ref) | copy-start | bytes 2064388
  30.9 1.6 %collective-permute-start = (bf16[8,128,128]{2,1,0:T(8,128)(2,1)S(1)}, bf16[8,128,128]{2,1,0:T(8,128)(2,1)S(1)}, u32[]{:S(2)}, u32[]{:S(2)}) collective-permute-start(bf16[8,128,128]{2,1,0:T(8,128)(2,1)S(1)} %slice.14), channel_id=1, source_target_pairs={{0,1},{1,0},{2,3},{3,2},{4,5},{5,4},{6,7},{7,6},{8,9},{9,8},{10,11... | collective-permute-start | bytes 786440 | tf_op jit(solution)/shard_map/ppermute | solution.py:216
  32.6 0.7 %copy-start.1 = (bf16[8,128,128]{2,1,0:T(8,128)(2,1)}, bf16[8,128,128]{2,1,0:T(8,128)(2,1)S(1)}, u32[]{:S(2)}) copy-start(bf16[8,128,128]{2,1,0:T(8,128)(2,1)S(1)} %collective-permute-done.partner_ref) | copy-start | bytes 786436
